TPU v7x, 256 devices: a whole 4x4x8 slice. The times are simulated.
256 devices in a mesh: req: 16 (over z, core), head: 16 (over x, y).
Axes of the slice: x: 4, y: 4, z: 8, core: 2. Of those that a mesh axis runs over, the one named last changes fastest.
Arguments:
- tree_heads: bfloat16 [4096, 16384], P(('req', 'head')), may hold values from -6 to 6
- tree_gates: bfloat16 [4096, 16384], P(('req', 'head')), may hold values from -6 to 6
- tree_steps: bfloat16 [4096, 256], P(('req', 'head')), may hold values from -6 to 6
- tree_groups: bfloat16 [4096, 4096], P(('req', 'head')), may hold values from -6 to 6
- new_tree: int32 [128, 32, 32], P('req'), may hold values from 0 to 1, as said below
- kernel_heads: bfloat16 [4, 16384], P(None, 'head'), may hold values from -3 to 3
- shift_heads: float32 [16384], P('head'), may hold values from -3 to 3
- kernel_groups: bfloat16 [4, 4096], replicated, may hold values from -3 to 3
- shift_groups: float32 [4096], replicated, may hold values from -3 to 3
- log_rates: float32 [256], P('head'), may hold values from 0 to 2.77
- step_bias: float32 [256], P('head'), may hold values from -6 to -2
- skip_gain: float32 [256], P('head'), may hold values from 0.5 to 1.5
- norm_gain: float32 [16384], P('head'), may hold values from 0.5 to 1.5
- old_state: bfloat16 [128, 256, 64, 256], P('req', 'head'), may hold values from -0.59765625 to 0.59765625
- old_heads: bfloat16 [128, 32, 16384], P('req', None, 'head'), may hold values from -3 to 3
- old_keys: bfloat16 [128, 32, 2048], P('req'), may hold values from -3 to 3
- old_steps: float32 [128, 32, 256], P('req', None, 'head'), may hold values from 0.002 to 0.2
- prior_heads: bfloat16 [128, 32, 16384], P('req', None, 'head'), may hold values from -6 to 6
- prior_groups: bfloat16 [128, 32, 4096], P('req', 'head'), may hold values from -6 to 6
- old_tree: int32 [128, 32, 32], P('req'), may hold values from 0 to 1, as said below
- accepted: int32 [128], P('req'), may hold values from 2 to 31, as said below
- new_owner: int32 [128], replicated, may hold values from 0 to 127, as said below
Outputs:
- mixed: bfloat16 [4096, 16384], P('req', 'head')
Inputs may be any that keep to these rules, and one draw needn't show every extreme that they name: `old_tree`: entry (t, j) is 1 when node j is node t or one of its ancestors, else 0; node 0 is the root, every parent has a lower number than its child, node 1 is the child of node 0 and node 2 the child of node 1, and every node numbered 2 or more has depth two or more. `new_tree`: ancestor masks of the same kind as old_tree. The accepted node has depth two or more in old_tree. A permutation of the slots. Slot i lives on device i // 8 of req before and on device new_owner[i] // 8 after; no old device hands more than 2 requests to one new device, and in every draw some pairs of devices carry exactly 2.
All inputs are finite; a program needn't handle non-finite values.
Results may differ from a plain program's by a relative error of at most 0.0052.
Values may be sent and summed in bfloat16 or wider, within the bound.
No kernel may reach another device: no remote copies, remote signals or barrier semaphores. Data moves between devices by JAX's collectives and lax.ppermute only.
A program may use at most 128 MiB of HBM per device.

v0:
```python
import jax
import jax.numpy as jnp
from jax import lax
from jax.sharding import PartitionSpec as P

HEADS = 256
HEAD_DIM = 64
STATE = 256
GROUPS = 8
NODES = 32
MOST = 2


EPSILON = 1e-05


def tree_conv(tree_rows, tail_rows, ancestry, weight, offset_bias):
    node_depth = jnp.sum(ancestry, axis=-1) - 1
    places = jnp.arange(3, dtype=jnp.int32)
    summed = weight[3].astype(jnp.float32) * tree_rows.astype(jnp.float32) + offset_bias
    for upward in range(1, 4):
        picked = (
            (ancestry == 1) & (node_depth[:, None, :] == node_depth[:, :, None] - upward)
        ).astype(jnp.bfloat16)
        older_rows = (places[None, None, :] == node_depth[:, :, None] - upward + 3).astype(
            jnp.bfloat16
        )
        shifted = jnp.einsum("btj,bjc->btc", picked, tree_rows, preferred_element_type=jnp.float32)
        shifted = shifted + jnp.einsum(
            "bti,bic->btc", older_rows, tail_rows, preferred_element_type=jnp.float32
        )
        summed = summed + weight[3 - upward].astype(jnp.float32) * shifted
    return jax.nn.silu(summed).astype(jnp.bfloat16)


def place_slots(payload, positions, count):
    wanted = jnp.arange(count, dtype=jnp.int32)
    owners = jnp.arange(positions.shape[0], dtype=jnp.int32)
    hits = positions[None, :] == wanted[:, None]
    chosen = jnp.sum(jnp.where(hits, owners[None, :], 0), axis=1)
    filled = jnp.any(hits, axis=1).reshape((count,) + (1,) * (payload.ndim - 1))
    taken = jnp.take(payload, chosen, axis=0)
    return jnp.where(filled, taken, jnp.zeros_like(taken))


def shards(
    tree_heads,
    tree_gates,
    tree_steps,
    tree_groups,
    new_tree,
    kernel_heads,
    shift_heads,
    kernel_groups,
    shift_groups,
    log_rates,
    step_bias,
    skip_gain,
    norm_gain,
    old_state,
    old_heads,
    old_keys,
    old_steps,
    prior_heads,
    prior_groups,
    old_tree,
    accepted,
    new_owner,
):
    req_count = lax.axis_size("req")
    req_index = lax.axis_index("req")
    head_index = lax.axis_index("head")
    reqs_dev = new_tree.shape[0]
    local_heads = log_rates.shape[0]
    local_nodes = prior_groups.shape[1]
    per_group = HEADS // GROUPS
    span_heads = min(local_heads, per_group)
    span_groups = local_heads // span_heads
    first_group = head_index * local_heads // per_group
    slot_count = req_count * MOST
    key_width = GROUPS * STATE
    highest = lax.Precision.HIGHEST
    owner_table = new_owner.reshape(req_count, reqs_dev)
    target_dev = owner_table // reqs_dev
    local_ids = jnp.arange(reqs_dev, dtype=jnp.int32)
    before = local_ids[None, :, None] > local_ids[None, None, :]
    same_dest = target_dev[:, :, None] == target_dev[:, None, :]
    arrival = jnp.sum((same_dest & before).astype(jnp.int32), axis=-1)
    send_table = target_dev * MOST + arrival
    send_pos = lax.dynamic_index_in_dim(send_table, req_index, 0, keepdims=False)
    wanted_slot = req_index * reqs_dev + local_ids
    all_ids = jnp.arange(new_owner.shape[0], dtype=jnp.int32)
    match = new_owner[None, :] == wanted_slot[:, None]
    anchor = jnp.sum(jnp.where(match, all_ids[None, :], 0), axis=1)
    recv_pos = anchor // reqs_dev * MOST + jnp.take(arrival.reshape(-1), anchor)
    decay_rates = -jnp.exp(log_rates)
    node_ids = jnp.arange(NODES, dtype=jnp.int32)
    chosen_hot = node_ids[None, :] == accepted[:, None]
    chosen_row = jnp.sum(jnp.where(chosen_hot[:, :, None], old_tree, 0), axis=1)
    old_depth = jnp.sum(old_tree, axis=-1) - 1
    chosen_depth = jnp.sum(jnp.where(chosen_hot, old_depth, 0), axis=1)
    places = jnp.arange(3, dtype=jnp.int32)
    lineage = chosen_row == 1
    tail_pick = (
        lineage[:, None, :]
        & (old_depth[:, None, :] == chosen_depth[:, None, None] - 2 + places[None, :, None])
    ).astype(jnp.bfloat16)
    tail_heads = jnp.einsum(
        "bij,bjc->bic", tail_pick, prior_heads, preferred_element_type=jnp.float32
    ).astype(jnp.bfloat16)
    pick_local = lax.dynamic_slice_in_dim(tail_pick, head_index * local_nodes, local_nodes, 2)
    tail_part = jnp.einsum(
        "bij,bjc->bic", pick_local, prior_groups, preferred_element_type=jnp.float32
    )
    tail_groups = lax.psum(tail_part.astype(jnp.bfloat16), "head")
    old_sums = jnp.einsum(
        "btj,bjh->bth", old_tree.astype(jnp.float32), old_steps * decay_rates, precision=highest
    )
    chosen_sum = jnp.sum(jnp.where(chosen_hot[:, :, None], old_sums, 0.0), axis=1)
    kept_weight = (
        jnp.where(
            lineage[:, :, None],
            jnp.exp(jnp.where(lineage[:, :, None], chosen_sum[:, None, :] - old_sums, 0.0)),
            0.0,
        )
        * old_steps
    )
    weighted = (
        (
            kept_weight[..., None]
            * old_heads.reshape(reqs_dev, NODES, local_heads, HEAD_DIM).astype(jnp.float32)
        )
        .astype(jnp.bfloat16)
        .reshape(reqs_dev, NODES, span_groups, span_heads, HEAD_DIM)
    )
    key_slice = lax.dynamic_slice_in_dim(
        old_keys, first_group * STATE, span_groups * STATE, 2
    ).reshape(reqs_dev, NODES, span_groups, STATE)
    update = jnp.einsum(
        "bjgqp,bjgn->bgqpn", weighted, key_slice, preferred_element_type=jnp.float32
    )
    carry_state = (
        jnp.exp(chosen_sum).reshape(reqs_dev, span_groups, span_heads, 1, 1)
        * old_state.reshape(reqs_dev, span_groups, span_heads, HEAD_DIM, STATE).astype(jnp.float32)
        + update
    ).astype(jnp.bfloat16)
    head_rows, gate_rows, step_rows = (
        lax.all_to_all(tree_heads, "head", split_axis=1, concat_axis=0, tiled=True),
        lax.all_to_all(tree_gates, "head", split_axis=1, concat_axis=0, tiled=True),
        lax.all_to_all(tree_steps, "head", split_axis=1, concat_axis=0, tiled=True),
    )
    group_rows = lax.all_gather(tree_groups, "head", axis=0, tiled=True)
    head_rows = head_rows.reshape(reqs_dev, NODES, -1)
    gate_rows = gate_rows.reshape(reqs_dev, NODES, span_groups, span_heads, HEAD_DIM)
    step_rows = step_rows.reshape(reqs_dev, NODES, local_heads)
    group_rows = group_rows.reshape(reqs_dev, NODES, -1)
    moved = (
        lax.all_to_all(
            place_slots(carry_state, send_pos, slot_count),
            "req",
            split_axis=0,
            concat_axis=0,
            tiled=True,
        ),
        lax.all_to_all(
            place_slots(tail_heads, send_pos, slot_count),
            "req",
            split_axis=0,
            concat_axis=0,
            tiled=True,
        ),
        lax.all_to_all(
            place_slots(tail_groups, send_pos, slot_count),
            "req",
            split_axis=0,
            concat_axis=0,
            tiled=True,
        ),
    )
    held_state = jnp.take(moved[0], recv_pos, axis=0)
    conv_heads = tree_conv(
        head_rows, jnp.take(moved[1], recv_pos, axis=0), new_tree, kernel_heads, shift_heads
    )
    conv_groups = tree_conv(
        group_rows, jnp.take(moved[2], recv_pos, axis=0), new_tree, kernel_groups, shift_groups
    )
    own_keys = lax.dynamic_slice_in_dim(conv_groups, first_group * STATE, span_groups * STATE, 2)
    own_queries = lax.dynamic_slice_in_dim(
        conv_groups, key_width + first_group * STATE, span_groups * STATE, 2
    )
    conv_heads, own_keys, own_queries = (conv_heads, own_keys, own_queries)
    query_four = own_queries.reshape(reqs_dev, NODES, span_groups, STATE)
    carried = jnp.einsum(
        "btgn,bgqpn->btgqp", query_four, held_state, preferred_element_type=jnp.float32
    )
    key_four = own_keys.reshape(reqs_dev, NODES, span_groups, STATE)
    step_sizes = jax.nn.softplus(step_rows.astype(jnp.float32) + step_bias)
    decay_sum = jnp.einsum(
        "btj,bjh->bth", new_tree.astype(jnp.float32), step_sizes * decay_rates, precision=highest
    )
    intersection = jnp.einsum(
        "btgn,bjgn->btjg", query_four, key_four, preferred_element_type=jnp.float32
    )
    lineage_new = (new_tree == 1)[:, :, :, None]
    decay_gap = decay_sum[:, :, None, :] - decay_sum[:, None, :, :]
    decays = jnp.where(lineage_new, jnp.exp(jnp.where(lineage_new, decay_gap, 0.0)), 0.0)
    mixing = (
        decays.reshape(reqs_dev, NODES, NODES, span_groups, span_heads)
        * intersection[..., None]
        * step_sizes.reshape(reqs_dev, 1, NODES, span_groups, span_heads)
    ).astype(jnp.bfloat16)
    values = conv_heads.reshape(reqs_dev, NODES, span_groups, span_heads, HEAD_DIM)
    inner_part = jnp.einsum(
        "btjgq,bjgqp->btgqp", mixing, values, preferred_element_type=jnp.float32
    )
    output = (
        inner_part
        + jnp.exp(decay_sum).reshape(reqs_dev, NODES, span_groups, span_heads, 1) * carried
        + skip_gain.reshape(1, 1, span_groups, span_heads, 1) * values.astype(jnp.float32)
    )
    gated_out = output * jax.nn.silu(gate_rows.astype(jnp.float32))
    group_power = jnp.sum(gated_out * gated_out, axis=(3, 4))
    zero_index = jnp.zeros((), jnp.int32)
    power_full = lax.dynamic_update_slice(
        jnp.zeros((reqs_dev, NODES, GROUPS), jnp.float32),
        group_power,
        (zero_index, zero_index, first_group),
    )
    power_total = lax.psum(power_full, "head")
    power_own = lax.dynamic_slice_in_dim(power_total, first_group, span_groups, 2)
    scale_factor = lax.rsqrt(power_own / (per_group * HEAD_DIM) + EPSILON)
    normed = (
        gated_out
        * scale_factor[..., None, None]
        * norm_gain.reshape(1, 1, span_groups, span_heads, HEAD_DIM)
    )
    return normed.reshape(reqs_dev * NODES, local_heads * HEAD_DIM).astype(jnp.bfloat16)


def solution(mesh):
    placed = (
        P(("req", "head"), None),
        P(("req", "head"), None),
        P(("req", "head"), None),
        P(("req", "head"), None),
        P("req", None, None),
        P(None, "head"),
        P("head"),
        P(),
        P(),
        P("head"),
        P("head"),
        P("head"),
        P("head"),
        P("req", "head", None, None),
        P("req", None, "head"),
        P("req", None, None),
        P("req", None, "head"),
        P("req", None, "head"),
        P("req", "head", None),
        P("req", None, None),
        P("req"),
        P(),
    )
    return jax.shard_map(
        shards, mesh=mesh, in_specs=placed, out_specs=P("req", "head"), check_vma=False
    )
```

profile of v0, /device:TPU:32, one launch (start us, length us, event | category | flops | bytes accessed | tf_op | source)
XLA Modules:
  0.0 639.1 jit_solution(553130558290788781)
XLA Ops:
  8.2 7.0 %all-to-all-start.2 = ((bf16[16,2,128]{2,1,0:T(2,128)(2,1)}), bf16[16,2,128]{2,1,0:T(2,128)(2,1)S(1)}, u32[]{:S(2)}, u32[]{:S(2)}) async-start(bf16[16,2,128]{2,1,0:T(2,128)(2,1)} %reshape.611), calls=%async_computation.2 | async-start | bytes 16384 | tf_op jit(solution)/shard_map/all_to_all | solution.py:150
  18.2 2.0 convolution_convert_fusion
  31.5 8.6 %all-to-all-start.1 = ((bf16[32,3,1024]{2,1,0:T(4,128)(2,1)}), bf16[32,3,1024]{2,1,0:T(4,128)(2,1)}, u32[]{:S(2)}, u32[]{:S(2)}) async-start(bf16[32,3,1024]{2,1,0:T(4,128)(2,1)} %select_select_fusion.1), calls=%async_computation.1 | async-start | bytes 524288 | tf_op jit(solution)/shard_map/all_to_all | solution.py:165
  42.3 7.5 %all-to-all-done.1 = bf16[32,3,1024]{2,1,0:T(4,128)(2,1)} async-done(((bf16[32,3,1024]{2,1,0:T(4,128)(2,1)}), bf16[32,3,1024]{2,1,0:T(4,128)(2,1)}, u32[]{:S(2)}, u32[]{:S(2)}) %all-to-all-start.1) | async-done | bytes 196640 | tf_op jit(solution)/shard_map/all_to_all | solution.py:165
  49.7 7.3 %all-to-all-start = ((bf16[16,16,1024]{2,0,1:T(8,128)(2,1)}), bf16[16,16,1024]{2,0,1:T(8,128)(2,1)}, u32[]{:S(2)}, u32[]{:S(2)}) async-start(bf16[16,16,1024]{2,0,1:T(8,128)(2,1)} %bitcast.122), calls=%async_computation | async-start | bytes 1048576 | tf_op jit(solution)/shard_map/all_to_all | solution.py:148
  57.0 5.6 add_convert_fusion
  62.7 9.3 %gather_fusion.5 = bf16[32,16,64,256]{3,2,1,0:T(8,128)(2,1)} fusion(bf16[8,16,64,256]{3,2,1,0:T(8,128)(2,1)} %add_convert_fusion, s32[1024]{0:T(1024)S(1)} %pad_clamp_fusion.1), kind=kCustom, calls=%fused_computation.5 | custom fusion | bytes 33554560 | tf_op jit(solution)/shard_map/jit(_take)/gather | solution.py:42
  72.0 47.7 %all-reduce.2.cloned.1.call-done = bf16[8,3,4096]{2,1,0:T(4,128)(2,1)} async-done(((bf16[8,3,4096]{2,1,0:T(4,128)(2,1)}), bf16[8,3,4096]{2,1,0:T(4,128)(2,1)}) %all-reduce.2.cloned.1.call-update) | async-done | bytes 196624 | tf_op jit(solution)/shard_map/psum | solution.py:115
  119.7 2.4 gather_fusion.3
  122.1 5.0 all-to-all-start.5
  128.9 8.4 %all-to-all-done.5 = bf16[16,16,1024]{2,0,1:T(8,128)(2,1)S(1)} async-done(((bf16[16,16,1024]{2,0,1:T(8,128)(2,1)}), bf16[16,16,1024]{2,0,1:T(8,128)(2,1)S(1)}, u32[]{:S(2)}, u32[]{:S(2)}) %all-to-all-start.5) | async-done | bytes 524320 | tf_op jit(solution)/shard_map/all_to_all | solution.py:149
  137.3 7.5 %all-to-all-start.3 = ((bf16[32,3,4096]{2,1,0:T(4,128)(2,1)}), bf16[32,3,4096]{2,1,0:T(4,128)(2,1)S(1)}, u32[]{:S(2)}, u32[]{:S(2)}) async-start(bf16[32,3,4096]{2,1,0:T(4,128)(2,1)} %select_select_fusion), calls=%async_computation.3 | async-start | bytes 2097152 | tf_op jit(solution)/shard_map/all_to_all | solution.py:172
  144.8 14.3 %fusion.1 = bf16[32,1,16,64,256]{4,3,2,1,0:T(8,128)(2,1)} fusion(bf16[32,16,64,256]{3,2,1,0:T(8,128)(2,1)} %gather_fusion.5, pred[32]{0:T(512)(128)(4,1)S(1)} %compare_and_fusion.10, pred[32]{0:T(512)(128)(4,1)S(1)} %copy-done.19), kind=kLoop, calls=%fused_computation.9 | loop fusion | flops 16777216 | bytes 33554496 | tf_op jit(solution)/shard_map/jit(_where)/select_n | solution.py:43
  159.1 10.3 %all-to-all-done.3 = bf16[32,3,4096]{2,1,0:T(4,128)(2,1)S(1)} async-done(((bf16[32,3,4096]{2,1,0:T(4,128)(2,1)}), bf16[32,3,4096]{2,1,0:T(4,128)(2,1)S(1)}, u32[]{:S(2)}, u32[]{:S(2)}) %all-to-all-start.3) | async-done | bytes 786464 | tf_op jit(solution)/shard_map/all_to_all | solution.py:172
  170.3 6.8 %all-to-all-start.4 = ((bf16[32,1,16,64,256]{4,3,2,1,0:T(8,128)(2,1)}), bf16[32,1,16,64,256]{4,3,2,1,0:T(8,128)(2,1)}, u32[]{:S(2)}, u32[]{:S(2)}) async-start(bf16[32,1,16,64,256]{4,3,2,1,0:T(8,128)(2,1)} %fusion.1), calls=%async_computation.4 | async-start | bytes 33554432 | tf_op jit(solution)/shard_map/all_to_all | solution.py:158
  194.0 2.1 gather_fusion.4
  196.1 31.9 %all-gather.2.cloned.1.call-done = bf16[256,4096]{1,0:T(8,128)(2,1)} async-done(((bf16[16,4096]{1,0:T(8,128)(2,1)}), bf16[256,4096]{1,0:T(8,128)(2,1)}) %all-gather.2.cloned.1.call-update) | async-done | bytes 2097168 | tf_op jit(solution)/shard_map/all_gather | solution.py:152
  228.0 2.5 fusion.42
  238.0 301.8 %all-to-all-done.4 = bf16[32,1,16,64,256]{4,3,2,1,0:T(8,128)(2,1)} async-done(((bf16[32,1,16,64,256]{4,3,2,1,0:T(8,128)(2,1)}), bf16[32,1,16,64,256]{4,3,2,1,0:T(8,128)(2,1)}, u32[]{:S(2)}, u32[]{:S(2)}) %all-to-all-start.4) | async-done | bytes 16777248 | tf_op jit(solution)/shard_map/all_to_all | solution.py:158
  539.8 8.6 %gather_fusion.6 = bf16[8,16,64,256]{3,2,1,0:T(8,128)(2,1)} fusion(bf16[32,16,64,256]{3,2,1,0:T(8,128)(2,1)} %bitcast.31, s32[1024]{0:T(1024)} %copy-done.17), kind=kCustom, calls=%fused_computation.6 | custom fusion | bytes 8388640 | tf_op jit(solution)/shard_map/jit(_take)/gather | solution.py:180
  548.4 4.7 fusion.8
  553.2 4.7 multiply_reduce_fusion
  557.8 70.6 %psum.15 = f32[8,32,8]{1,0,2:T(8,128)S(1)} all-reduce(f32[8,32,8]{1,0,2:T(8,128)S(1)} %bitcast_dynamic-update-slice_fusion), channel_id=1, replica_groups=mesh['req'=16,'head'=16] {'head'}, use_global_device_ids=true, to_apply=%region_11.12 | all-reduce | flops 2048 | bytes 16384 | tf_op jit(solution)/shard_map/psum | solution.py:229
  628.4 1.9 multiply_convert_fusion.1
  (134 shorter events, 46.5 us)
Async XLA Ops:
  6.5 50.5 %copy-start = (bf16[8,32,2048]{2,1,0:T(8,128)(2,1)S(1)}, bf16[8,32,2048]{2,1,0:T(8,128)(2,1)}, u32[]{:S(2)}) copy-start(bf16[8,32,2048]{2,1,0:T(8,128)(2,1)} %param.37) | copy-start | bytes 3145732
  8.2 23.3 %all-to-all-start.2 = ((bf16[16,2,128]{2,1,0:T(2,128)(2,1)}), bf16[16,2,128]{2,1,0:T(2,128)(2,1)S(1)}, u32[]{:S(2)}, u32[]{:S(2)}) async-start(bf16[16,2,128]{2,1,0:T(2,128)(2,1)} %reshape.611), calls=%async_computation.2 | async-start | bytes 16384 | tf_op jit(solution)/shard_map/all_to_all | solution.py:150
  15.2 104.5 %all-reduce.2.cloned.1.call-start = ((), (), s32[]{:S(2)}) async-start(), calls=%async_computation.7 | async-start | bytes 524288 | tf_op jit(solution)/shard_map/psum | solution.py:115
  18.2 22.1 %copy-start.9 = (f32[8,32,16]{1,2,0:T(8,128)S(1)}, f32[8,32,16]{1,2,0:T(8,128)}, u32[]{:S(2)}) copy-start(f32[8,32,16]{1,2,0:T(8,128)} %param.38) | copy-start | bytes 49156
  20.2 20.9 %copy-start.8 = (s32[8,32,32]{2,1,0:T(8,128)S(1)}, s32[8,32,32]{2,1,0:T(8,128)}, u32[]{:S(2)}) copy-start(s32[8,32,32]{2,1,0:T(8,128)} %param.41) | copy-start | bytes 98308
  21.6 18.5 %copy-start.18 = (pred[32]{0:T(512)(128)(4,1)}, pred[32]{0:T(512)(128)(4,1)S(1)}, u32[]{:S(2)}) copy-start(pred[32]{0:T(512)(128)(4,1)S(1)} %fusion.68) | copy-start | bytes 100
  31.5 18.3 %all-to-all-start.1 = ((bf16[32,3,1024]{2,1,0:T(4,128)(2,1)}), bf16[32,3,1024]{2,1,0:T(4,128)(2,1)}, u32[]{:S(2)}, u32[]{:S(2)}) async-start(bf16[32,3,1024]{2,1,0:T(4,128)(2,1)} %select_select_fusion.1), calls=%async_computation.1 | async-start | bytes 524288 | tf_op jit(solution)/shard_map/all_to_all | solution.py:165
  49.7 72.4 %all-to-all-start = ((bf16[16,16,1024]{2,0,1:T(8,128)(2,1)}), bf16[16,16,1024]{2,0,1:T(8,128)(2,1)}, u32[]{:S(2)}, u32[]{:S(2)}) async-start(bf16[16,16,1024]{2,0,1:T(8,128)(2,1)} %bitcast.122), calls=%async_computation | async-start | bytes 1048576 | tf_op jit(solution)/shard_map/all_to_all | solution.py:148
  62.7 64.5 %copy-start.19 = (pred[32]{0:T(512)(128)(4,1)S(1)}, pred[32]{0:T(512)(128)(4,1)}, u32[]{:S(2)}) copy-start(pred[32]{0:T(512)(128)(4,1)} %copy-done.18) | copy-start | bytes 100
  122.1 15.1 %all-to-all-start.5 = ((bf16[16,16,1024]{2,0,1:T(8,128)(2,1)}), bf16[16,16,1024]{2,0,1:T(8,128)(2,1)S(1)}, u32[]{:S(2)}, u32[]{:S(2)}) async-start(bf16[16,16,1024]{2,0,1:T(8,128)(2,1)} %bitcast.116), calls=%async_computation.5 | async-start | bytes 1048576 | tf_op jit(solution)/shard_map/all_to_all | solution.py:149
  137.3 21.8 %copy-start.3 = (bf16[16,16,1024]{2,0,1:T(8,128)(2,1)}, bf16[16,16,1024]{2,0,1:T(8,128)(2,1)S(1)}, u32[]{:S(2)}) copy-start(bf16[16,16,1024]{2,0,1:T(8,128)(2,1)S(1)} %all-to-all-done.5) | copy-start | bytes 1572868
  137.3 32.1 %all-to-all-start.3 = ((bf16[32,3,4096]{2,1,0:T(4,128)(2,1)}), bf16[32,3,4096]{2,1,0:T(4,128)(2,1)S(1)}, u32[]{:S(2)}, u32[]{:S(2)}) async-start(bf16[32,3,4096]{2,1,0:T(4,128)(2,1)} %select_select_fusion), calls=%async_computation.3 | async-start | bytes 2097152 | tf_op jit(solution)/shard_map/all_to_all | solution.py:172
  159.0 19.1 %copy-start.22 = (s32[128]{0:T(128)S(1)}, s32[128]{0:T(128)}, u32[]{:S(2)}) copy-start(s32[128]{0:T(128)} %param.43) | copy-start | bytes 1540
  159.0 20.0 %copy-start.6 = (s32[8,32,32]{2,1,0:T(8,128)S(1)}, s32[8,32,32]{2,1,0:T(8,128)}, u32[]{:S(2)}) copy-start(s32[8,32,32]{2,1,0:T(8,128)} %param.26) | copy-start | bytes 98308
  159.0 20.2 %copy-start.21 = (f32[1024]{0:T(1024)S(1)}, f32[1024]{0:T(1024)}, u32[]{:S(2)}) copy-start(f32[1024]{0:T(1024)} %param.34) | copy-start | bytes 12292
  159.0 20.3 %copy-start.12 = (bf16[4,1024]{1,0:T(4,128)(2,1)S(1)}, bf16[4,1024]{1,0:T(4,128)(2,1)}, u32[]{:S(2)}) copy-start(bf16[4,1024]{1,0:T(4,128)(2,1)} %param.27) | copy-start | bytes 24580
  159.1 20.3 %copy-start.10 = (bf16[4,4096]{1,0:T(4,128)(2,1)S(1)}, bf16[4,4096]{1,0:T(4,128)(2,1)}, u32[]{:S(2)}) copy-start(bf16[4,4096]{1,0:T(4,128)(2,1)} %param.29) | copy-start | bytes 98308
  170.3 369.5 %all-to-all-start.4 = ((bf16[32,1,16,64,256]{4,3,2,1,0:T(8,128)(2,1)}), bf16[32,1,16,64,256]{4,3,2,1,0:T(8,128)(2,1)}, u32[]{:S(2)}, u32[]{:S(2)}) async-start(bf16[32,1,16,64,256]{4,3,2,1,0:T(8,128)(2,1)} %fusion.1), calls=%async_computation.4 | async-start | bytes 33554432 | tf_op jit(solution)/shard_map/all_to_all | solution.py:158
  177.2 50.9 %all-gather.2.cloned.1.call-start = ((), (), s32[]{:S(2)}) async-start(), calls=%async_computation.6 | async-start | bytes 2228224 | tf_op jit(solution)/shard_map/all_gather | solution.py:152
  179.0 8.0 %copy-start.15 = (pred[8]{0:T(512)(128)(4,1)}, pred[8]{0:T(512)(128)(4,1)S(1)}, u32[]{:S(2)}) copy-start(pred[8]{0:T(512)(128)(4,1)S(1)} %compare_and_fusion.11) | copy-start | bytes 28
  179.3 7.6 %copy-start.17 = (s32[1024]{0:T(1024)}, s32[1024]{0:T(1024)S(1)}, u32[]{:S(2)}) copy-start(s32[1024]{0:T(1024)S(1)} %pad_clamp_fusion) | copy-start | bytes 12292
  548.4 4.7 copy-start.7
  548.4 4.7 copy-start.24
  553.2 79.1 %copy-start.1 = (bf16[8,32,2048]{2,1,0:T(8,128)(2,1)S(1)}, bf16[8,32,2048]{2,1,0:T(8,128)(2,1)}, u32[]{:S(2)}) copy-start(bf16[8,32,2048]{2,1,0:T(8,128)(2,1)} %param.37) | copy-start | bytes 3145732
  (9 other events, 18.4 us)
Sparse Core Ops, SparseCore 0:
  20.4 99.3 all-reduce.1
  180.4 47.5 all-gather.1
where the time goes:
time: 641 us; the launch traced here: 639 us
  waiting for transfers between devices  408 us (64%)
  blocking collectives  70.6 us (11%)
  local copies, waits for them, and re-layouts  42.5 us (7%)
  starting transfers between devices  42.5 us (7%)
  matrix products  34.7 us (5%)
  other arithmetic  26.6 us (4%)
  between operations  14.1 us (2%)
    all_to_all x1, waiting for transfers between devices, shards(): lax.all_to_all(place_slots(carry_state, send_pos, slot_count), 'req', spl...  302 us
    psum x1, blocking collectives, shards(): power_total = lax.psum(power_full, 'head')  70.6 us
    psum x1, waiting for transfers between devices, shards(): tail_groups = lax.psum(tail_part.astype(jnp.bfloat16), 'head')  47.7 us
    all_gather x1, waiting for transfers between devices, shards(): group_rows = lax.all_gather(tree_groups, 'head', axis=0, tiled=True)  31.9 us
    select_n x3, other arithmetic, place_slots(): return jnp.where(filled, taken, jnp.zeros_like(taken))  16.9 us
  transfers between devices with their start and end apart: 8, of which 6 were waited for; matrix products, arithmetic and copies ran while one was open for 12% of the time, Pallas kernels for 0%

commit v1 on v0

--- a/solution.py
+++ b/solution.py
@@ -41,6 +41,17 @@
     filled = jnp.any(hits, axis=1).reshape((count,) + (1,) * (payload.ndim - 1))
     taken = jnp.take(payload, chosen, axis=0)
     return jnp.where(filled, taken, jnp.zeros_like(taken))
+
+
+def own_columns(rows, span_groups, dest_count, per_dest):
+    lead = rows.shape[:-1]
+    split = rows.reshape(lead + (2, GROUPS, STATE))
+    moved = jnp.moveaxis(split, -2, 0)
+    picks = (jnp.arange(dest_count, dtype=jnp.int32) // per_dest)[:, None] * span_groups + jnp.arange(
+        span_groups, dtype=jnp.int32
+    )[None, :]
+    taken = jnp.take(moved, picks.reshape(-1), axis=0).reshape((dest_count, span_groups) + lead + (2, STATE))
+    return jnp.moveaxis(taken, 1, -2).reshape((dest_count,) + lead + (2 * span_groups * STATE,))
 
 
 def shards(
@@ -68,6 +79,7 @@
     new_owner,
 ):
     req_count = lax.axis_size("req")
+    head_count = lax.axis_size("head")
     req_index = lax.axis_index("req")
     head_index = lax.axis_index("head")
     reqs_dev = new_tree.shape[0]
@@ -76,9 +88,10 @@
     per_group = HEADS // GROUPS
     span_heads = min(local_heads, per_group)
     span_groups = local_heads // span_heads
+    per_dest = per_group // span_heads
     first_group = head_index * local_heads // per_group
     slot_count = req_count * MOST
-    key_width = GROUPS * STATE
+    own_width = span_groups * STATE
     highest = lax.Precision.HIGHEST
     owner_table = new_owner.reshape(req_count, reqs_dev)
     target_dev = owner_table // reqs_dev
@@ -93,6 +106,17 @@
     match = new_owner[None, :] == wanted_slot[:, None]
     anchor = jnp.sum(jnp.where(match, all_ids[None, :], 0), axis=1)
     recv_pos = anchor // reqs_dev * MOST + jnp.take(arrival.reshape(-1), anchor)
+
+    def to_new(payload):
+        placed = place_slots(payload, send_pos, slot_count)
+        moved = lax.all_to_all(placed, "req", split_axis=0, concat_axis=0, tiled=True)
+        return jnp.take(moved, recv_pos, axis=0)
+
+    def to_old(payload):
+        placed = place_slots(payload, recv_pos, slot_count)
+        moved = lax.all_to_all(placed, "req", split_axis=0, concat_axis=0, tiled=True)
+        return jnp.take(moved, send_pos, axis=0)
+
     decay_rates = -jnp.exp(log_rates)
     node_ids = jnp.arange(NODES, dtype=jnp.int32)
     chosen_hot = node_ids[None, :] == accepted[:, None]
@@ -108,11 +132,19 @@
     tail_heads = jnp.einsum(
         "bij,bjc->bic", tail_pick, prior_heads, preferred_element_type=jnp.float32
     ).astype(jnp.bfloat16)
-    pick_local = lax.dynamic_slice_in_dim(tail_pick, head_index * local_nodes, local_nodes, 2)
-    tail_part = jnp.einsum(
-        "bij,bjc->bic", pick_local, prior_groups, preferred_element_type=jnp.float32
-    )
-    tail_groups = lax.psum(tail_part.astype(jnp.bfloat16), "head")
+    prior_own = lax.all_to_all(
+        own_columns(prior_groups, span_groups, head_count, per_dest),
+        "head",
+        split_axis=0,
+        concat_axis=0,
+        tiled=True,
+    )
+    prior_own = jnp.moveaxis(
+        prior_own.reshape(head_count, reqs_dev, local_nodes, 2 * own_width), 0, 1
+    ).reshape(reqs_dev, NODES, 2 * own_width)
+    tail_groups = jnp.einsum(
+        "bij,bjc->bic", tail_pick, prior_own, preferred_element_type=jnp.float32
+    ).astype(jnp.bfloat16)
     old_sums = jnp.einsum(
         "btj,bjh->bth", old_tree.astype(jnp.float32), old_steps * decay_rates, precision=highest
     )
@@ -149,50 +181,35 @@
         lax.all_to_all(tree_gates, "head", split_axis=1, concat_axis=0, tiled=True),
         lax.all_to_all(tree_steps, "head", split_axis=1, concat_axis=0, tiled=True),
     )
-    group_rows = lax.all_gather(tree_groups, "head", axis=0, tiled=True)
+    group_rows = lax.all_to_all(
+        own_columns(tree_groups, span_groups, head_count, per_dest),
+        "head",
+        split_axis=0,
+        concat_axis=0,
+        tiled=True,
+    )
     head_rows = head_rows.reshape(reqs_dev, NODES, -1)
     gate_rows = gate_rows.reshape(reqs_dev, NODES, span_groups, span_heads, HEAD_DIM)
     step_rows = step_rows.reshape(reqs_dev, NODES, local_heads)
     group_rows = group_rows.reshape(reqs_dev, NODES, -1)
-    moved = (
-        lax.all_to_all(
-            place_slots(carry_state, send_pos, slot_count),
-            "req",
-            split_axis=0,
-            concat_axis=0,
-            tiled=True,
-        ),
-        lax.all_to_all(
-            place_slots(tail_heads, send_pos, slot_count),
-            "req",
-            split_axis=0,
-            concat_axis=0,
-            tiled=True,
-        ),
-        lax.all_to_all(
-            place_slots(tail_groups, send_pos, slot_count),
-            "req",
-            split_axis=0,
-            concat_axis=0,
-            tiled=True,
-        ),
-    )
-    held_state = jnp.take(moved[0], recv_pos, axis=0)
+    head_width = tail_heads.shape[-1]
+    tails_new = to_new(jnp.concatenate([tail_heads, tail_groups], axis=-1))
     conv_heads = tree_conv(
-        head_rows, jnp.take(moved[1], recv_pos, axis=0), new_tree, kernel_heads, shift_heads
-    )
+        head_rows, tails_new[..., :head_width], new_tree, kernel_heads, shift_heads
+    )
+    kernel_own = own_columns(kernel_groups, span_groups, head_count, per_dest)[head_index]
+    shift_own = own_columns(shift_groups, span_groups, head_count, per_dest)[head_index]
     conv_groups = tree_conv(
-        group_rows, jnp.take(moved[2], recv_pos, axis=0), new_tree, kernel_groups, shift_groups
-    )
-    own_keys = lax.dynamic_slice_in_dim(conv_groups, first_group * STATE, span_groups * STATE, 2)
-    own_queries = lax.dynamic_slice_in_dim(
-        conv_groups, key_width + first_group * STATE, span_groups * STATE, 2
-    )
-    conv_heads, own_keys, own_queries = (conv_heads, own_keys, own_queries)
+        group_rows, tails_new[..., head_width:], new_tree, kernel_own, shift_own
+    )
+    own_keys = conv_groups[..., :own_width]
+    own_queries = conv_groups[..., own_width:]
     query_four = own_queries.reshape(reqs_dev, NODES, span_groups, STATE)
-    carried = jnp.einsum(
-        "btgn,bgqpn->btgqp", query_four, held_state, preferred_element_type=jnp.float32
-    )
+    query_old = to_old(query_four)
+    carried_old = jnp.einsum(
+        "btgn,bgqpn->btgqp", query_old, carry_state, preferred_element_type=jnp.float32
+    )
+    carried = to_new(carried_old)
     key_four = own_keys.reshape(reqs_dev, NODES, span_groups, STATE)
     step_sizes = jax.nn.softplus(step_rows.astype(jnp.float32) + step_bias)
     decay_sum = jnp.einsum(
@@ -220,14 +237,18 @@
     )
     gated_out = output * jax.nn.silu(gate_rows.astype(jnp.float32))
     group_power = jnp.sum(gated_out * gated_out, axis=(3, 4))
-    zero_index = jnp.zeros((), jnp.int32)
-    power_full = lax.dynamic_update_slice(
-        jnp.zeros((reqs_dev, NODES, GROUPS), jnp.float32),
-        group_power,
-        (zero_index, zero_index, first_group),
-    )
-    power_total = lax.psum(power_full, "head")
-    power_own = lax.dynamic_slice_in_dim(power_total, first_group, span_groups, 2)
+    if per_dest == 2:
+        partner = [(d, d ^ 1) for d in range(head_count)]
+        power_own = group_power + lax.ppermute(group_power, "head", partner)
+    else:
+        zero_index = jnp.zeros((), jnp.int32)
+        power_full = lax.dynamic_update_slice(
+            jnp.zeros((reqs_dev, NODES, GROUPS), jnp.float32),
+            group_power,
+            (zero_index, zero_index, first_group),
+        )
+        power_total = lax.psum(power_full, "head")
+        power_own = lax.dynamic_slice_in_dim(power_total, first_group, span_groups, 2)
     scale_factor = lax.rsqrt(power_own / (per_group * HEAD_DIM) + EPSILON)
     normed = (
         gated_out

time: 641 us -> 290 us (0.45)
  the two profiles are of different devices: /device:TPU:32 before, /device:TPU:1 now
where the time goes in v1:
time: 290 us; the launch traced here: 288 us
  waiting for transfers between devices  116 us (40%)
  local copies, waits for them, and re-layouts  62.6 us (22%)
  starting transfers between devices  50.3 us (17%)
  other arithmetic  33.1 us (11%)
  matrix products  24.4 us (8%)
    all_to_all x2, waiting for transfers between devices, to_new(): lax.all_to_all(placed, 'req', split_axis=0, concat_axis=0, tiled=True)  92.7 us
    unnamed x94, local copies, waits for them, and re-layouts  22.4 us
    all_to_all x2, starting transfers between devices, to_new(): lax.all_to_all(placed, 'req', split_axis=0, concat_axis=0, tiled=True)  15.8 us
    all_to_all x1, waiting for transfers between devices, to_old(): lax.all_to_all(placed, 'req', split_axis=0, concat_axis=0, tiled=True)  15.7 us
    all_to_all x1, other arithmetic, to_new(): lax.all_to_all(placed, 'req', split_axis=0, concat_axis=0, tiled=True)  13.7 us
    all_to_all x2, local copies, waits for them, and re-layouts, to_new(): lax.all_to_all(placed, 'req', split_axis=0, concat_axis=0, tiled=True)  8.77 us
    unnamed x1, other arithmetic  8.57 us
    all_to_all x1, starting transfers between devices, shards(): lax.all_to_all(own_columns(prior_groups, span_groups, head_count, per_des...  7.7 us
  transfers between devices with their start and end apart: 9, of which 6 were waited for; matrix products, arithmetic and copies ran while one was open for 25% of the time, Pallas kernels for 0%

profile of v1, /device:TPU:1, one launch (start us, length us, event | category | flops | bytes accessed | tf_op | source)
XLA Modules:
  0.0 287.8 jit_solution(3807208754857388213)
XLA Ops:
  2.6 7.7 %all-to-all-start.1 = ((bf16[16,8,2,512]{3,1,2,0:T(8,128)(2,1)}), bf16[16,8,2,512]{3,1,2,0:T(8,128)(2,1)S(1)}, u32[]{:S(2)}, u32[]{:S(2)}) async-start(bf16[16,8,2,512]{3,1,2,0:T(8,128)(2,1)} %broadcast_select_fusion.1), calls=%async_computation.1 | async-start | bytes 524288 | tf_op jit(solution)/shard_map/all_to_all | solution.py:135
  21.5 1.9 copy.195
  25.5 6.7 %all-to-all-start.4 = ((bf16[16,16,512]{2,1,0:T(8,128)(2,1)}), bf16[16,16,512]{2,1,0:T(8,128)(2,1)S(1)}, u32[]{:S(2)}, u32[]{:S(2)}) async-start(bf16[16,16,512]{2,1,0:T(8,128)(2,1)} %broadcast_select_fusion), calls=%async_computation.4 | async-start | bytes 524288 | tf_op jit(solution)/shard_map/all_to_all | solution.py:184
  34.5 5.0 %all-to-all-done.4 = bf16[16,16,512]{2,1,0:T(8,128)(2,1)S(1)} async-done(((bf16[16,16,512]{2,1,0:T(8,128)(2,1)}), bf16[16,16,512]{2,1,0:T(8,128)(2,1)S(1)}, u32[]{:S(2)}, u32[]{:S(2)}) %all-to-all-start.4) | async-done | bytes 262176 | tf_op jit(solution)/shard_map/all_to_all | solution.py:184
  39.5 11.2 %all-to-all-start.2 = ((bf16[32,3,1536]{2,1,0:T(4,128)(2,1)}), bf16[32,3,1536]{2,1,0:T(4,128)(2,1)S(1)}, u32[]{:S(2)}, u32[]{:S(2)}) async-start(bf16[32,3,1536]{2,1,0:T(4,128)(2,1)} %select_select_fusion), calls=%async_computation.2 | async-start | bytes 786432 | tf_op jit(solution)/shard_map/all_to_all | solution.py:112
  52.4 12.8 %all-to-all-done.2 = bf16[32,3,1536]{2,1,0:T(4,128)(2,1)S(1)} async-done(((bf16[32,3,1536]{2,1,0:T(4,128)(2,1)}), bf16[32,3,1536]{2,1,0:T(4,128)(2,1)S(1)}, u32[]{:S(2)}, u32[]{:S(2)}) %all-to-all-start.2) | async-done | bytes 294944 | tf_op jit(solution)/shard_map/all_to_all | solution.py:112
  65.2 3.5 %all-to-all-start.3 = ((bf16[16,2,128]{2,1,0:T(2,128)(2,1)}), bf16[16,2,128]{2,1,0:T(2,128)(2,1)S(1)}, u32[]{:S(2)}, u32[]{:S(2)}) async-start(bf16[16,2,128]{2,1,0:T(2,128)(2,1)} %reshape.812), calls=%async_computation.3 | async-start | bytes 16384 | tf_op jit(solution)/shard_map/all_to_all | solution.py:182
  73.2 1.9 all-to-all-done.3
  75.1 4.2 %all-to-all-start.5 = ((bf16[32,32,1,256]{3,1,2,0:T(8,128)(2,1)}), bf16[32,32,1,256]{3,1,2,0:T(8,128)(2,1)S(1)}, u32[]{:S(2)}, u32[]{:S(2)}) async-start(bf16[32,32,1,256]{3,1,2,0:T(8,128)(2,1)} %fusion.35), calls=%async_computation.5 | async-start | bytes 1048576 | tf_op jit(solution)/shard_map/all_to_all | solution.py:117
  80.8 15.7 %all-to-all-done.5 = bf16[32,32,1,256]{3,1,2,0:T(8,128)(2,1)S(1)} async-done(((bf16[32,32,1,256]{3,1,2,0:T(8,128)(2,1)}), bf16[32,32,1,256]{3,1,2,0:T(8,128)(2,1)S(1)}, u32[]{:S(2)}, u32[]{:S(2)}) %all-to-all-start.5) | async-done | bytes 524320 | tf_op jit(solution)/shard_map/all_to_all | solution.py:117
  96.5 4.2 %all-to-all-start = ((bf16[16,16,1024]{2,0,1:T(8,128)(2,1)}), bf16[16,16,1024]{2,0,1:T(8,128)(2,1)}, u32[]{:S(2)}, u32[]{:S(2)}) async-start(bf16[16,16,1024]{2,0,1:T(8,128)(2,1)} %bitcast.177), calls=%async_computation | async-start | bytes 1048576 | tf_op jit(solution)/shard_map/all_to_all | solution.py:180
  102.7 7.3 %fusion.10 = f32[8,32,16,64]{3,1,2,0:T(8,128)S(1)} fusion(bf16[8,16,64,256]{3,2,1,0:T(8,128)(2,1)} %param.35, f32[8,16]{1,0:T(8,128)} %exp.56, f32[8,32,16,64]{3,2,1,0:T(8,128)} %reshape.704, f32[8,32,16]{1,2,0:T(8,128)} %bitcast_multiply_fusion, bf16[8,32,256]{2,1,0:T(8,128)(2,1)S(1)} %gather_fusion.8, bf16[8,32,2048]{2,1,0:T(8,128)(2,1)S(1)} %copy-done, ...), kind=kOutput, calls=%fused_computation.29 | convolution fusion | flops 277413888 | bytes 6570508 | tf_op jit(solution)/shard_map/btgn,bgqpn->btgqp/dot_general | solution.py:209
  110.0 4.5 %gather_fusion.9 = f32[32,32,16,64]{3,1,2,0:T(8,128)} fusion(f32[8,32,16,64]{3,1,2,0:T(8,128)S(1)} %fusion.10, s32[1024]{0:T(1024)} %copy-done.24), kind=kCustom, calls=%fused_computation.9 | custom fusion | bytes 8388736 | tf_op jit(solution)/shard_map/jit(_take)/gather | solution.py:42
  114.5 6.5 %all-to-all-start.7 = ((bf16[16,16,1024]{2,0,1:T(8,128)(2,1)}), bf16[16,16,1024]{2,0,1:T(8,128)(2,1)S(1)}, u32[]{:S(2)}, u32[]{:S(2)}) async-start(bf16[16,16,1024]{2,0,1:T(8,128)(2,1)} %bitcast.176), calls=%async_computation.7 | async-start | bytes 1048576 | tf_op jit(solution)/shard_map/all_to_all | solution.py:181
  121.1 8.6 %fusion.107 = f32[32,1,16,32,64]{4,3,2,1,0:T(8,128)} fusion(f32[32,32,16,64]{3,1,2,0:T(8,128)} %gather_fusion.9, pred[32]{0:T(512)(128)(4,1)S(1)} %copy-done.27, pred[32]{0:T(512)(128)(4,1)S(1)} %copy-done.34), kind=kLoop, calls=%fused_computation.241 | loop fusion | flops 2097152 | bytes 8388672
  129.7 13.3 %reshape.810 = f32[16,1,65536]{2,1,0:T(1,128)} reshape(f32[32,1,16,32,64]{4,3,2,1,0:T(8,128)} %fusion.107) | data formatting | bytes 8388608
  143.0 4.6 %all-to-all-start.6 = ((f32[16,1,65536]{2,1,0:T(1,128)}), f32[16,1,65536]{2,1,0:T(1,128)}, u32[]{:S(2)}, u32[]{:S(2)}) async-start(f32[16,1,65536]{2,1,0:T(1,128)} %reshape.810), calls=%async_computation.6 | async-start | bytes 8388608 | tf_op jit(solution)/shard_map/all_to_all | solution.py:112
  160.4 79.9 %all-to-all-done.6 = f32[16,1,65536]{2,1,0:T(1,128)} async-done(((f32[16,1,65536]{2,1,0:T(1,128)}), f32[16,1,65536]{2,1,0:T(1,128)}, u32[]{:S(2)}, u32[]{:S(2)}) %all-to-all-start.6) | async-done | bytes 4194336 | tf_op jit(solution)/shard_map/all_to_all | solution.py:112
  240.8 13.7 %reduce.5 = f32[16,65536]{1,0:T(8,128)} reduce(f32[16,1,65536]{2,1,0:T(1,128)} %all-to-all-done.6, f32[]{:T(128)} %broadcast.910), dimensions={1}, to_apply=%all_to_all.56.reduce_sub_computation | reduce | bytes 8388612 | tf_op jit(solution)/shard_map/all_to_all | solution.py:112
  254.5 7.0 %reshape.811 = f32[32,1,16,32,64]{4,3,2,1,0:T(8,128)} reshape(f32[16,65536]{1,0:T(8,128)} %reduce.5) | data formatting | bytes 8388608
  261.5 8.2 %bitcast_bitcast_fusion = f32[32,32,16,64]{3,1,2,0:T(8,128)} fusion(f32[32,1,16,32,64]{4,3,2,1,0:T(8,128)} %reshape.811), kind=kLoop, calls=%fused_computation.240 | loop fusion | bytes 8388608 | tf_op jit(solution)/shard_map/all_to_all | solution.py:112
  269.7 5.6 %gather_fusion.10 = f32[8,32,16,64]{3,1,2,0:T(8,128)} fusion(f32[32,32,16,64]{3,1,2,0:T(8,128)} %bitcast_bitcast_fusion, s32[1024]{0:T(1024)} %copy-done.25), kind=kCustom, calls=%fused_computation.10 | custom fusion | bytes 2097184 | tf_op jit(solution)/shard_map/jit(_take)/gather | solution.py:113
  275.4 5.8 %multiply_reduce_fusion = (f32[8,32]{1,0:T(8,128)S(1)}, f32[8,32,1,16,64]{4,1,3,0,2:T(8,128)}) fusion(f32[8,32,1,16,64]{4,3,1,0,2:T(8,128)} %reshape.706, f32[8,32,1,16,64]{4,3,1,0,2:T(8,128)S(1)} %reshape.705, f32[16]{0:T(128)S(1)} %copy-done.42, f32[8,32,16,64]{3,1,2,0:T(8,128)} %gather_fusion.10, pred[8]{0:T(512)(128)(4,1)S(1)} %copy-done.36, ...), kind=kOutput, calls=%fused_computation.27 | convolution fusion | flops 20709120 | bytes 4809800 | tf_op jit(solution)/shard_map/btjgq,bjgqp->btgqp/dot_general | solution.py:230
  283.9 2.0 multiply_convert_fusion
  (204 shorter events, 44.8 us)
Async XLA Ops:
  0.0 102.7 %copy-start = (bf16[8,32,2048]{2,1,0:T(8,128)(2,1)S(1)}, bf16[8,32,2048]{2,1,0:T(8,128)(2,1)}, u32[]{:S(2)}) copy-start(bf16[8,32,2048]{2,1,0:T(8,128)(2,1)} %param.37) | copy-start | bytes 3145732
  0.0 13.1 %copy-start.39 = (s32[8]{0:T(128)S(1)}, s32[8]{0:T(128)}, u32[]{:S(2)}) copy-start(s32[8]{0:T(128)} %param.42) | copy-start | bytes 100
  0.0 13.2 %copy-start.9 = (s32[8,32,32]{2,1,0:T(8,128)S(1)}, s32[8,32,32]{2,1,0:T(8,128)}, u32[]{:S(2)}) copy-start(s32[8,32,32]{2,1,0:T(8,128)} %param.41) | copy-start | bytes 98308
  0.0 14.4 %copy-start.18 = (bf16[4,4096]{1,0:T(4,128)(2,1)S(1)}, bf16[4,4096]{1,0:T(4,128)(2,1)}, u32[]{:S(2)}) copy-start(bf16[4,4096]{1,0:T(4,128)(2,1)} %param.29) | copy-start | bytes 98308
  0.0 15.8 %copy-start.13 = (bf16[16,4096]{1,0:T(8,128)(2,1)S(1)}, bf16[16,4096]{1,0:T(8,128)(2,1)}, u32[]{:S(2)}) copy-start(bf16[16,4096]{1,0:T(8,128)(2,1)} %param.25) | copy-start | bytes 393220
  2.6 14.7 %copy-start.22 = (f32[4096]{0:T(1024)S(1)}, f32[4096]{0:T(1024)}, u32[]{:S(2)}) copy-start(f32[4096]{0:T(1024)} %param.30) | copy-start | bytes 49156
  2.6 22.9 %all-to-all-start.1 = ((bf16[16,8,2,512]{3,1,2,0:T(8,128)(2,1)}), bf16[16,8,2,512]{3,1,2,0:T(8,128)(2,1)S(1)}, u32[]{:S(2)}, u32[]{:S(2)}) async-start(bf16[16,8,2,512]{3,1,2,0:T(8,128)(2,1)} %broadcast_select_fusion.1), calls=%async_computation.1 | async-start | bytes 524288 | tf_op jit(solution)/shard_map/all_to_all | solution.py:135
  11.1 22.3 %copy-start.33 = (pred[32]{0:T(512)(128)(4,1)}, pred[32]{0:T(512)(128)(4,1)S(1)}, u32[]{:S(2)}) copy-start(pred[32]{0:T(512)(128)(4,1)S(1)} %fusion.89) | copy-start | bytes 100
  12.1 57.3 %copy-start.35 = (pred[8]{0:T(512)(128)(4,1)}, pred[8]{0:T(512)(128)(4,1)S(1)}, u32[]{:S(2)}) copy-start(pred[8]{0:T(512)(128)(4,1)S(1)} %get-tuple-element.9) | copy-start | bytes 28
  12.5 20.9 %copy-start.26 = (pred[32]{0:T(512)(128)(4,1)}, pred[32]{0:T(512)(128)(4,1)S(1)}, u32[]{:S(2)}) copy-start(pred[32]{0:T(512)(128)(4,1)S(1)} %get-tuple-element.34) | copy-start | bytes 100
  13.7 18.5 %copy-start.20 = (pred[8,32]{1,0:T(8,128)(4,1)}, pred[8,32]{1,0:T(8,128)(4,1)S(1)}, u32[]{:S(2)}) copy-start(pred[8,32]{1,0:T(8,128)(4,1)S(1)} %broadcast_compare_fusion.1) | copy-start | bytes 772
  13.8 18.8 %copy-start.24 = (s32[1024]{0:T(1024)}, s32[1024]{0:T(1024)S(1)}, u32[]{:S(2)}) copy-start(s32[1024]{0:T(1024)S(1)} %pad_clamp_fusion.3) | copy-start | bytes 12292
  13.8 54.9 %copy-start.25 = (s32[1024]{0:T(1024)}, s32[1024]{0:T(1024)S(1)}, u32[]{:S(2)}) copy-start(s32[1024]{0:T(1024)S(1)} %pad_clamp_fusion.2) | copy-start | bytes 12292
  15.9 34.9 %copy-start.16 = (s32[8,32]{1,0:T(8,128)}, s32[8,32]{1,0:T(8,128)S(1)}, u32[]{:S(2)}) copy-start(s32[8,32]{1,0:T(8,128)S(1)} %get-tuple-element.20) | copy-start | bytes 3076
  15.9 54.2 %copy-start.31 = (s32[8,32]{1,0:T(8,128)}, s32[8,32]{1,0:T(8,128)S(1)}, u32[]{:S(2)}) copy-start(s32[8,32]{1,0:T(8,128)S(1)} %get-tuple-element.19) | copy-start | bytes 3076
  25.5 14.0 %all-to-all-start.4 = ((bf16[16,16,512]{2,1,0:T(8,128)(2,1)}), bf16[16,16,512]{2,1,0:T(8,128)(2,1)S(1)}, u32[]{:S(2)}, u32[]{:S(2)}) async-start(bf16[16,16,512]{2,1,0:T(8,128)(2,1)} %broadcast_select_fusion), calls=%async_computation.4 | async-start | bytes 524288 | tf_op jit(solution)/shard_map/all_to_all | solution.py:184
  39.5 25.7 %all-to-all-start.2 = ((bf16[32,3,1536]{2,1,0:T(4,128)(2,1)}), bf16[32,3,1536]{2,1,0:T(4,128)(2,1)S(1)}, u32[]{:S(2)}, u32[]{:S(2)}) async-start(bf16[32,3,1536]{2,1,0:T(4,128)(2,1)} %select_select_fusion), calls=%async_computation.2 | async-start | bytes 786432 | tf_op jit(solution)/shard_map/all_to_all | solution.py:112
  65.2 9.9 %all-to-all-start.3 = ((bf16[16,2,128]{2,1,0:T(2,128)(2,1)}), bf16[16,2,128]{2,1,0:T(2,128)(2,1)S(1)}, u32[]{:S(2)}, u32[]{:S(2)}) async-start(bf16[16,2,128]{2,1,0:T(2,128)(2,1)} %reshape.812), calls=%async_computation.3 | async-start | bytes 16384 | tf_op jit(solution)/shard_map/all_to_all | solution.py:182
  72.2 28.6 %copy-start.21 = (pred[8,32]{1,0:T(8,128)(4,1)S(1)}, pred[8,32]{1,0:T(8,128)(4,1)}, u32[]{:S(2)}) copy-start(pred[8,32]{1,0:T(8,128)(4,1)} %copy-done.20) | copy-start | bytes 772
  75.1 21.5 %all-to-all-start.5 = ((bf16[32,32,1,256]{3,1,2,0:T(8,128)(2,1)}), bf16[32,32,1,256]{3,1,2,0:T(8,128)(2,1)S(1)}, u32[]{:S(2)}, u32[]{:S(2)}) async-start(bf16[32,32,1,256]{3,1,2,0:T(8,128)(2,1)} %fusion.35), calls=%async_computation.5 | async-start | bytes 1048576 | tf_op jit(solution)/shard_map/all_to_all | solution.py:117
  96.5 18.0 %all-to-all-start = ((bf16[16,16,1024]{2,0,1:T(8,128)(2,1)}), bf16[16,16,1024]{2,0,1:T(8,128)(2,1)}, u32[]{:S(2)}, u32[]{:S(2)}) async-start(bf16[16,16,1024]{2,0,1:T(8,128)(2,1)} %bitcast.177), calls=%async_computation | async-start | bytes 1048576 | tf_op jit(solution)/shard_map/all_to_all | solution.py:180
  114.5 28.4 %all-to-all-start.7 = ((bf16[16,16,1024]{2,0,1:T(8,128)(2,1)}), bf16[16,16,1024]{2,0,1:T(8,128)(2,1)S(1)}, u32[]{:S(2)}, u32[]{:S(2)}) async-start(bf16[16,16,1024]{2,0,1:T(8,128)(2,1)} %bitcast.176), calls=%async_computation.7 | async-start | bytes 1048576 | tf_op jit(solution)/shard_map/all_to_all | solution.py:181
  143.0 97.3 %all-to-all-start.6 = ((f32[16,1,65536]{2,1,0:T(1,128)}), f32[16,1,65536]{2,1,0:T(1,128)}, u32[]{:S(2)}, u32[]{:S(2)}) async-start(f32[16,1,65536]{2,1,0:T(1,128)} %reshape.810), calls=%async_computation.6 | async-start | bytes 8388608 | tf_op jit(solution)/shard_map/all_to_all | solution.py:112
  281.2 2.6 collective-permute-start
  (28 other events, 162.7 us)

commit v2 on v1

--- a/solution.py
+++ b/solution.py
@@ -132,19 +132,6 @@
     tail_heads = jnp.einsum(
         "bij,bjc->bic", tail_pick, prior_heads, preferred_element_type=jnp.float32
     ).astype(jnp.bfloat16)
-    prior_own = lax.all_to_all(
-        own_columns(prior_groups, span_groups, head_count, per_dest),
-        "head",
-        split_axis=0,
-        concat_axis=0,
-        tiled=True,
-    )
-    prior_own = jnp.moveaxis(
-        prior_own.reshape(head_count, reqs_dev, local_nodes, 2 * own_width), 0, 1
-    ).reshape(reqs_dev, NODES, 2 * own_width)
-    tail_groups = jnp.einsum(
-        "bij,bjc->bic", tail_pick, prior_own, preferred_element_type=jnp.float32
-    ).astype(jnp.bfloat16)
     old_sums = jnp.einsum(
         "btj,bjh->bth", old_tree.astype(jnp.float32), old_steps * decay_rates, precision=highest
     )
@@ -176,40 +163,69 @@
         * old_state.reshape(reqs_dev, span_groups, span_heads, HEAD_DIM, STATE).astype(jnp.float32)
         + update
     ).astype(jnp.bfloat16)
-    head_rows, gate_rows, step_rows = (
-        lax.all_to_all(tree_heads, "head", split_axis=1, concat_axis=0, tiled=True),
-        lax.all_to_all(tree_gates, "head", split_axis=1, concat_axis=0, tiled=True),
-        lax.all_to_all(tree_steps, "head", split_axis=1, concat_axis=0, tiled=True),
-    )
-    group_rows = lax.all_to_all(
-        own_columns(tree_groups, span_groups, head_count, per_dest),
-        "head",
-        split_axis=0,
-        concat_axis=0,
-        tiled=True,
-    )
-    head_rows = head_rows.reshape(reqs_dev, NODES, -1)
-    gate_rows = gate_rows.reshape(reqs_dev, NODES, span_groups, span_heads, HEAD_DIM)
-    step_rows = step_rows.reshape(reqs_dev, NODES, local_heads)
-    group_rows = group_rows.reshape(reqs_dev, NODES, -1)
-    head_width = tail_heads.shape[-1]
-    tails_new = to_new(jnp.concatenate([tail_heads, tail_groups], axis=-1))
+    tree_rows = tree_heads.shape[0]
+    head_width = local_heads * HEAD_DIM
+    split_heads = jnp.moveaxis(tree_heads.reshape(tree_rows, head_count, head_width), 1, 0)
+    split_gates = jnp.moveaxis(tree_gates.reshape(tree_rows, head_count, head_width), 1, 0)
+    split_steps = jnp.moveaxis(tree_steps.reshape(tree_rows, head_count, local_heads), 1, 0)
+    split_groups = own_columns(tree_groups, span_groups, head_count, per_dest)
+    split_prior = own_columns(prior_groups, span_groups, head_count, per_dest).reshape(
+        head_count, reqs_dev * local_nodes, 2 * own_width
+    )
+    widths = [head_width, head_width, local_heads, 2 * own_width, 2 * own_width]
+    bundle = jnp.concatenate(
+        [split_heads, split_gates, split_steps, split_groups, split_prior.astype(jnp.bfloat16)], axis=-1
+    )
+    bundle = lax.all_to_all(bundle, "head", split_axis=0, concat_axis=0, tiled=True)
+    cuts = [0]
+    for width in widths:
+        cuts.append(cuts[-1] + width)
+    pieces = [bundle[..., cuts[n] : cuts[n + 1]] for n in range(len(widths))]
+    head_rows = pieces[0].reshape(reqs_dev, NODES, head_width)
+    gate_rows = pieces[1].reshape(reqs_dev, NODES, span_groups, span_heads, HEAD_DIM)
+    step_rows = pieces[2].reshape(reqs_dev, NODES, local_heads)
+    group_rows = pieces[3].reshape(reqs_dev, NODES, 2 * own_width)
+    prior_own = jnp.moveaxis(
+        pieces[4].reshape(head_count, reqs_dev, local_nodes, 2 * own_width), 0, 1
+    ).reshape(reqs_dev, NODES, 2 * own_width)
+    tail_groups = jnp.einsum(
+        "bij,bjc->bic", tail_pick, prior_own, preferred_element_type=jnp.float32
+    ).astype(jnp.bfloat16)
+    new_part = jnp.concatenate([tail_heads, tail_groups], axis=-1).reshape(reqs_dev, -1)
+    old_part = jnp.concatenate(
+        [group_rows[..., own_width:], new_tree.astype(jnp.bfloat16)], axis=-1
+    ).reshape(reqs_dev, -1)
+    new_len = new_part.shape[-1]
+    exchange = jnp.concatenate(
+        [place_slots(new_part, send_pos, slot_count), place_slots(old_part, recv_pos, slot_count)],
+        axis=-1,
+    )
+    exchange = lax.all_to_all(exchange, "req", split_axis=0, concat_axis=0, tiled=True)
+    tails_new = jnp.take(exchange[:, :new_len], recv_pos, axis=0).reshape(reqs_dev, 3, -1)
+    rows_old = jnp.take(exchange[:, new_len:], send_pos, axis=0).reshape(reqs_dev, NODES, -1)
+    tree_old = rows_old[..., own_width:].astype(jnp.int32)
+    kernel_own = own_columns(kernel_groups, span_groups, head_count, per_dest)[head_index]
+    shift_own = own_columns(shift_groups, span_groups, head_count, per_dest)[head_index]
+    query_old = tree_conv(
+        rows_old[..., :own_width],
+        tail_groups[..., own_width:],
+        tree_old,
+        kernel_own[:, own_width:],
+        shift_own[own_width:],
+    ).reshape(reqs_dev, NODES, span_groups, STATE)
+    carried_old = jnp.einsum(
+        "btgn,bgqpn->btgqp", query_old, carry_state, preferred_element_type=jnp.float32
+    ).reshape(reqs_dev, NODES, head_width)
+    carried = to_new(carried_old).reshape(reqs_dev, NODES, span_groups, span_heads, HEAD_DIM)
     conv_heads = tree_conv(
         head_rows, tails_new[..., :head_width], new_tree, kernel_heads, shift_heads
     )
-    kernel_own = own_columns(kernel_groups, span_groups, head_count, per_dest)[head_index]
-    shift_own = own_columns(shift_groups, span_groups, head_count, per_dest)[head_index]
     conv_groups = tree_conv(
         group_rows, tails_new[..., head_width:], new_tree, kernel_own, shift_own
     )
     own_keys = conv_groups[..., :own_width]
     own_queries = conv_groups[..., own_width:]
     query_four = own_queries.reshape(reqs_dev, NODES, span_groups, STATE)
-    query_old = to_old(query_four)
-    carried_old = jnp.einsum(
-        "btgn,bgqpn->btgqp", query_old, carry_state, preferred_element_type=jnp.float32
-    )
-    carried = to_new(carried_old)
     key_four = own_keys.reshape(reqs_dev, NODES, span_groups, STATE)
     step_sizes = jax.nn.softplus(step_rows.astype(jnp.float32) + step_bias)
     decay_sum = jnp.einsum(

time: 290 us -> 247 us (0.85)
  starting transfers between devices: 50.3 us -> 25.5 us
  waiting for transfers between devices: 116 us -> 96.4 us
  matrix products: 24.4 us -> 33.4 us
  other arithmetic: 33.1 us -> 29.4 us
  local copies, waits for them, and re-layouts: 62.6 us -> 59.6 us
    unnamed x94 -> x125, local copies, waits for them, and re-layouts: 22.4 us -> 1.93 us
    all_to_all x2 -> x1, waiting for transfers between devices: 92.7 us -> 72.4 us  [to_new(): lax.all_to_all(placed, 'req', split_axis=0, concat_axis=0, tiled=True)]
    all_to_all x1 -> x0, other arithmetic: 13.7 us -> none  [to_new(): lax.all_to_all(placed, 'req', split_axis=0, concat_axis=0, tiled=True)]
    all_to_all x6 -> x2, starting transfers between devices: 32.9 us -> 20.4 us  [the longest x1 12.6 us: shards(): lax.all_to_all(exchange, 'req', split_axis=0, concat_axis=0, tiled=True)]
    all_to_all x2 -> x1, starting transfers between devices: 15.8 us -> 4.82 us  [to_new(): lax.all_to_all(placed, 'req', split_axis=0, concat_axis=0, tiled=True)]
    all_to_all x4 -> x1, local copies, waits for them, and re-layouts: 12.6 us -> 3.15 us  [shards(): lax.all_to_all(exchange, 'req', split_axis=0, concat_axis=0, tiled=True)]
    unnamed x1, other arithmetic: 8.57 us -> 0.04 us
    reshape x0 -> x7, local copies, waits for them, and re-layouts: none -> 7.21 us  [the longest x2 3.57 us: shards(): pieces[4].reshape(head_count, reqs_dev, local_nodes, 2 * own_width)]
  transfers between devices with their start and end apart: 9 -> 4, of which waited for: 6 -> 4; matrix products, arithmetic and copies ran while one was open for 25% -> 17% of each run, Pallas kernels for 0% -> 0%
where the time goes in v2:
time: 247 us; the launch traced here: 245 us
  waiting for transfers between devices  96.4 us (39%)
  local copies, waits for them, and re-layouts  59.6 us (24%)
  matrix products  33.4 us (14%)
  other arithmetic  29.4 us (12%)
  starting transfers between devices  25.5 us (10%)
    all_to_all x1, waiting for transfers between devices, to_new(): lax.all_to_all(placed, 'req', split_axis=0, concat_axis=0, tiled=True)  72.4 us
    all_to_all x1, waiting for transfers between devices, shards(): lax.all_to_all(exchange, 'req', split_axis=0, concat_axis=0, tiled=True)  16.3 us
    all_to_all x1, starting transfers between devices, shards(): lax.all_to_all(exchange, 'req', split_axis=0, concat_axis=0, tiled=True)  12.6 us
    gather x5, local copies, waits for them, and re-layouts, place_slots(): taken = jnp.take(payload, chosen, axis=0)  10.2 us
    select_n x3, other arithmetic, place_slots(): return jnp.where(filled, taken, jnp.zeros_like(taken))  8.41 us
    dot_general x1, matrix products, shards(): jnp.einsum('btgn,bgqpn->btgqp', query_old, carry_state, preferred_element...  8.02 us
    dot_general x9, matrix products, tree_conv(): jnp.einsum('btj,bjc->btc', picked, tree_rows, preferred_element_type=jnp....  7.99 us
    all_to_all x1, starting transfers between devices, shards(): lax.all_to_all(bundle, 'head', split_axis=0, concat_axis=0, tiled=True)  7.76 us
  transfers between devices with their start and end apart: 4, of which 4 were waited for; matrix products, arithmetic and copies ran while one was open for 17% of the time, Pallas kernels for 0%

profile of v2, /device:TPU:1, one launch (start us, length us, event | category | flops | bytes accessed | tf_op | source)
XLA Modules:
  0.0 245.4 jit_solution(15583107996244641149)
XLA Ops:
  4.4 2.1 concatenate.13
  6.5 7.8 %all-to-all-start = ((bf16[16,16,3088]{2,1,0:T(8,128)(2,1)}), bf16[16,16,3088]{2,1,0:T(8,128)(2,1)}, u32[]{:S(2)}, u32[]{:S(2)}) async-start(bf16[16,16,3088]{2,1,0:T(8,128)(2,1)} %concatenate.13), calls=%async_computation | async-start | bytes 3276800 | tf_op jit(solution)/shard_map/all_to_all | solution.py:179
  30.2 5.6 %all-to-all-done = bf16[16,16,3088]{2,1,0:T(8,128)(2,1)} async-done(((bf16[16,16,3088]{2,1,0:T(8,128)(2,1)}), bf16[16,16,3088]{2,1,0:T(8,128)(2,1)}, u32[]{:S(2)}, u32[]{:S(2)}) %all-to-all-start) | async-done | bytes 1581088 | tf_op jit(solution)/shard_map/all_to_all | solution.py:179
  35.7 2.0 fusion.126
  39.5 1.8 copy.190
  50.1 1.9 gather_fusion.4
  52.0 2.1 gather.72
  59.1 12.6 %all-to-all-start.1 = ((bf16[16,2,13824]{2,1,0:T(2,128)(2,1)}), bf16[16,2,13824]{2,1,0:T(2,128)(2,1)}, u32[]{:S(2)}, u32[]{:S(2)}) async-start(bf16[16,2,13824]{2,1,0:T(2,128)(2,1)} %pad_maximum_fusion), calls=%async_computation.1 | async-start | bytes 1769472 | tf_op jit(solution)/shard_map/all_to_all | solution.py:203
  80.2 16.3 %all-to-all-done.1 = bf16[16,2,13824]{2,1,0:T(2,128)(2,1)} async-done(((bf16[16,2,13824]{2,1,0:T(2,128)(2,1)}), bf16[16,2,13824]{2,1,0:T(2,128)(2,1)}, u32[]{:S(2)}, u32[]{:S(2)}) %all-to-all-start.1) | async-done | bytes 884768 | tf_op jit(solution)/shard_map/all_to_all | solution.py:203
  96.5 3.1 %all_to_all.14 = bf16[32,13824]{1,0:T(8,128)(2,1)} reshape(bf16[16,2,13824]{2,1,0:T(2,128)(2,1)} %all-to-all-done.1) | data formatting | bytes 1769472 | tf_op jit(solution)/shard_map/all_to_all | solution.py:203
  99.7 1.9 slice.159
  101.6 2.0 gather_fusion.8
  111.5 8.0 %fusion.8 = f32[8,32,1,16,64]{4,1,3,0,2:T(8,128)} fusion(bf16[8,32,256,1]{2,1,3,0:T(8,128)(2,1)} %fusion.38, bf16[8,16,64,256]{3,2,1,0:T(8,128)(2,1)} %param.35, f32[8,16]{1,0:T(8,128)S(1)} %copy-done.24, f32[8,32,16,64]{3,2,1,0:T(8,128)S(1)} %reshape.789, f32[8,32,16]{1,2,0:T(8,128)S(1)} %copy-done.10, bf16[8,32,2048]{2,1,0:T(8,128)(2,1)S(1)} %copy-done, ...), kind=kOutput, calls=%fused_computation.27 | convolution fusion | flops 277348352 | bytes 7671812 | tf_op jit(solution)/shard_map/btgn,bgqpn->btgqp/dot_general | solution.py:216
  119.6 2.8 %copy.134 = f32[8,32,1,16,64]{4,3,1,0,2:T(8,128)S(1)} copy(f32[8,32,1,16,64]{4,1,3,0,2:T(8,128)} %fusion.8) | data formatting | bytes 2097152 | tf_op jit(solution)/shard_map/btgn,bgqpn->btgqp/transpose | solution.py:216
  122.9 3.0 %gather_fusion.9 = f32[32,32,1024]{2,1,0:T(8,128)} fusion(f32[8,32,1024]{2,1,0:T(8,128)S(1)} %reshape.779, s32[1024]{0:T(1024)} %copy-done.28), kind=kCustom, calls=%fused_computation.9 | custom fusion | bytes 8388736 | tf_op jit(solution)/shard_map/jit(_take)/gather | solution.py:42
  125.9 5.3 %select_select_fusion = f32[32,32,1024]{2,1,0:T(8,128)} fusion(f32[32,32,1024]{2,1,0:T(8,128)} %gather_fusion.9, pred[32]{0:T(512)(128)(4,1)S(1)} %copy-done.51, pred[32]{0:T(512)(128)(4,1)S(1)} %copy-done.40), kind=kLoop, calls=%fused_computation.13 | loop fusion | flops 2097152 | bytes 8388672 | tf_op jit(solution)/shard_map/jit(_where)/select_n | solution.py:43
  131.2 4.8 %all-to-all-start.2 = ((f32[32,32,1024]{2,1,0:T(8,128)}), f32[32,32,1024]{2,1,0:T(8,128)}, u32[]{:S(2)}, u32[]{:S(2)}) async-start(f32[32,32,1024]{2,1,0:T(8,128)} %select_select_fusion), calls=%async_computation.2 | async-start | bytes 8388608 | tf_op jit(solution)/shard_map/all_to_all | solution.py:112
  140.0 1.9 reshape.795
  155.6 72.4 %all-to-all-done.2 = f32[32,32,1024]{2,1,0:T(8,128)} async-done(((f32[32,32,1024]{2,1,0:T(8,128)}), f32[32,32,1024]{2,1,0:T(8,128)}, u32[]{:S(2)}, u32[]{:S(2)}) %all-to-all-start.2) | async-done | bytes 4194336 | tf_op jit(solution)/shard_map/all_to_all | solution.py:112
  228.0 2.9 %gather_fusion.10 = f32[8,32,1024]{2,1,0:T(8,128)S(1)} fusion(f32[32,32,1024]{2,1,0:T(8,128)} %all-to-all-done.2, s32[1024]{0:T(1024)} %copy-done.29), kind=kCustom, calls=%fused_computation.10 | custom fusion | bytes 2097184 | tf_op jit(solution)/shard_map/jit(_take)/gather | solution.py:113
  231.0 1.9 gather.84
  232.9 6.0 %multiply_reduce_fusion = (f32[8,32]{1,0:T(8,128)S(1)}, f32[8,32,1,16,64]{4,1,3,0,2:T(8,128)}) fusion(f32[8,32,1,16,64]{4,3,1,0,2:T(8,128)} %reshape.795, f32[8,32,1,16,64]{4,3,1,0,2:T(8,128)S(1)} %reshape.794, f32[16]{0:T(128)S(1)} %copy-done.59, f32[8,32,1,16,64]{4,3,1,0,2:T(8,128)} %gather.84, pred[8]{0:T(512)(128)(4,1)S(1)} %copy-done.42, ...), kind=kOutput, calls=%fused_computation.25 | convolution fusion | flops 20709120 | bytes 4809800 | tf_op jit(solution)/shard_map/btjgq,bjgqp->btgqp/dot_general | solution.py:246
  239.3 2.1 collective-permute-done
  241.4 2.0 multiply_convert_fusion
  (258 shorter events, 71.8 us)
Async XLA Ops:
  0.0 111.5 %copy-start = (bf16[8,32,2048]{2,1,0:T(8,128)(2,1)S(1)}, bf16[8,32,2048]{2,1,0:T(8,128)(2,1)}, u32[]{:S(2)}) copy-start(bf16[8,32,2048]{2,1,0:T(8,128)(2,1)} %param.37) | copy-start | bytes 3145732
  6.5 11.4 %copy-start.53 = (s32[8]{0:T(128)S(1)}, s32[8]{0:T(128)}, u32[]{:S(2)}) copy-start(s32[8]{0:T(128)} %param.42) | copy-start | bytes 100
  6.5 11.5 %copy-start.3 = (s32[8,32,32]{2,1,0:T(8,128)S(1)}, s32[8,32,32]{2,1,0:T(8,128)}, u32[]{:S(2)}) copy-start(s32[8,32,32]{2,1,0:T(8,128)} %param.26) | copy-start | bytes 98308
  6.5 11.5 %copy-start.7 = (s32[8,32,32]{2,1,0:T(8,128)S(1)}, s32[8,32,32]{2,1,0:T(8,128)}, u32[]{:S(2)}) copy-start(s32[8,32,32]{2,1,0:T(8,128)} %param.41) | copy-start | bytes 98308
  6.5 13.3 %copy-start.20 = (bf16[4,4096]{1,0:T(4,128)(2,1)S(1)}, bf16[4,4096]{1,0:T(4,128)(2,1)}, u32[]{:S(2)}) copy-start(bf16[4,4096]{1,0:T(4,128)(2,1)} %param.29) | copy-start | bytes 98308
  6.5 14.1 %copy-start.26 = (f32[4096]{0:T(1024)S(1)}, f32[4096]{0:T(1024)}, u32[]{:S(2)}) copy-start(f32[4096]{0:T(1024)} %param.30) | copy-start | bytes 49156
  6.5 29.2 %all-to-all-start = ((bf16[16,16,3088]{2,1,0:T(8,128)(2,1)}), bf16[16,16,3088]{2,1,0:T(8,128)(2,1)}, u32[]{:S(2)}, u32[]{:S(2)}) async-start(bf16[16,16,3088]{2,1,0:T(8,128)(2,1)} %concatenate.13), calls=%async_computation | async-start | bytes 3276800 | tf_op jit(solution)/shard_map/all_to_all | solution.py:179
  14.9 12.0 %copy-start.43 = (s32[32]{0:T(128)}, s32[32]{0:T(128)S(1)}, u32[]{:S(2)}) copy-start(s32[32]{0:T(128)S(1)} %select_reduce_fusion.4) | copy-start | bytes 388
  15.0 11.9 %copy-start.39 = (pred[32]{0:T(512)(128)(4,1)}, pred[32]{0:T(512)(128)(4,1)S(1)}, u32[]{:S(2)}) copy-start(pred[32]{0:T(512)(128)(4,1)S(1)} %fusion.112) | copy-start | bytes 100
  18.0 10.9 %copy-start.32 = (pred[8,32]{1,0:T(8,128)(4,1)}, pred[8,32]{1,0:T(8,128)(4,1)S(1)}, u32[]{:S(2)}) copy-start(pred[8,32]{1,0:T(8,128)(4,1)S(1)} %iota_compare_fusion.16) | copy-start | bytes 772
  19.2 25.8 %copy-start.28 = (s32[1024]{0:T(1024)}, s32[1024]{0:T(1024)S(1)}, u32[]{:S(2)}) copy-start(s32[1024]{0:T(1024)S(1)} %pad_clamp_fusion.3) | copy-start | bytes 12292
  21.9 8.3 %copy-start.14 = (bf16[1,4,512]{2,0,1:T(2,128)(2,1)}, bf16[1,4,512]{2,0,1:T(2,128)(2,1)S(1)}, u32[]{:S(2)}) copy-start(bf16[1,4,512]{2,0,1:T(2,128)(2,1)S(1)} %broadcast_select_fusion.8) | copy-start | bytes 12292
  27.6 18.8 %copy-start.22 = (pred[8,32]{1,0:T(8,128)(4,1)}, pred[8,32]{1,0:T(8,128)(4,1)S(1)}, u32[]{:S(2)}) copy-start(pred[8,32]{1,0:T(8,128)(4,1)S(1)} %broadcast_compare_fusion.1) | copy-start | bytes 772
  55.5 16.2 %copy-start.54 = (s32[8]{0:T(128)S(1)}, s32[8]{0:T(128)}, u32[]{:S(2)}) copy-start(s32[8]{0:T(128)} %fusion.122) | copy-start | bytes 100
  55.5 16.8 %copy-start.44 = (s32[32]{0:T(128)S(1)}, s32[32]{0:T(128)}, u32[]{:S(2)}) copy-start(s32[32]{0:T(128)} %copy-done.43) | copy-start | bytes 388
  55.5 17.3 %copy-start.58 = (f32[16]{0:T(128)S(1)}, f32[16]{0:T(128)}, u32[]{:S(2)}) copy-start(f32[16]{0:T(128)} %param.31) | copy-start | bytes 196
  55.6 17.3 %copy-start.25 = (bf16[1,4,512]{2,1,0:T(4,128)(2,1)S(1)}, bf16[1,4,512]{2,1,0:T(4,128)(2,1)}, u32[]{:S(2)}) copy-start(bf16[1,4,512]{2,1,0:T(4,128)(2,1)} %copy.197) | copy-start | bytes 12292
  57.3 17.8 %copy-start.50 = (f32[16]{0:T(128)S(1)}, f32[16]{0:T(128)}, u32[]{:S(2)}) copy-start(f32[16]{0:T(128)} %param.32) | copy-start | bytes 196
  57.3 19.4 %copy-start.33 = (pred[8,32]{1,0:T(8,128)(4,1)S(1)}, pred[8,32]{1,0:T(8,128)(4,1)}, u32[]{:S(2)}) copy-start(pred[8,32]{1,0:T(8,128)(4,1)} %copy-done.32) | copy-start | bytes 772
  57.3 21.3 %copy-start.23 = (pred[8,32]{1,0:T(8,128)(4,1)S(1)}, pred[8,32]{1,0:T(8,128)(4,1)}, u32[]{:S(2)}) copy-start(pred[8,32]{1,0:T(8,128)(4,1)} %copy-done.22) | copy-start | bytes 772
  59.1 37.4 %all-to-all-start.1 = ((bf16[16,2,13824]{2,1,0:T(2,128)(2,1)}), bf16[16,2,13824]{2,1,0:T(2,128)(2,1)}, u32[]{:S(2)}, u32[]{:S(2)}) async-start(bf16[16,2,13824]{2,1,0:T(2,128)(2,1)} %pad_maximum_fusion), calls=%async_computation.1 | async-start | bytes 1769472 | tf_op jit(solution)/shard_map/all_to_all | solution.py:203
  131.2 96.8 %all-to-all-start.2 = ((f32[32,32,1024]{2,1,0:T(8,128)}), f32[32,32,1024]{2,1,0:T(8,128)}, u32[]{:S(2)}, u32[]{:S(2)}) async-start(f32[32,32,1024]{2,1,0:T(8,128)} %select_select_fusion), calls=%async_computation.2 | async-start | bytes 8388608 | tf_op jit(solution)/shard_map/all_to_all | solution.py:112
  136.1 12.0 %copy-start.29 = (s32[1024]{0:T(1024)}, s32[1024]{0:T(1024)S(1)}, u32[]{:S(2)}) copy-start(s32[1024]{0:T(1024)S(1)} %pad_clamp_fusion.1) | copy-start | bytes 12292
  238.9 2.5 %collective-permute-start = (f32[8,32,1]{1,0,2:T(8,128)S(1)}, f32[8,32,1]{1,0,2:T(8,128)S(1)}, u32[]{:S(2)}, u32[]{:S(2)}) collective-permute-start(f32[8,32,1]{1,0,2:T(8,128)S(1)} %bitcast.197), channel_id=1, source_target_pairs={{0,1},{1,0},{2,3},{3,2},{4,5},{5,4},{6,7},{7,6},{8,9},{9,8},{10,11... | collective-permute-start | bytes 3080 | tf_op jit(solution)/shard_map/ppermute | solution.py:258
  (41 other events, 131.9 us)

commit v3 on v2

--- a/solution.py
+++ b/solution.py
@@ -216,7 +216,7 @@
     carried_old = jnp.einsum(
         "btgn,bgqpn->btgqp", query_old, carry_state, preferred_element_type=jnp.float32
     ).reshape(reqs_dev, NODES, head_width)
-    carried = to_new(carried_old).reshape(reqs_dev, NODES, span_groups, span_heads, HEAD_DIM)
+    carried = to_new(carried_old.astype(jnp.bfloat16)).astype(jnp.float32).reshape(reqs_dev, NODES, span_groups, span_heads, HEAD_DIM)
     conv_heads = tree_conv(
         head_rows, tails_new[..., :head_width], new_tree, kernel_heads, shift_heads
     )

time: 247 us -> 184 us (0.74)
  waiting for transfers between devices: 96.4 us -> 49.6 us
  local copies, waits for them, and re-layouts: 59.6 us -> 47.4 us
  matrix products: 33.4 us -> 28.5 us
  other arithmetic: 29.4 us -> 32 us
    all_to_all x1, waiting for transfers between devices: 72.4 us -> 32.2 us  [to_new(): lax.all_to_all(placed, 'req', split_axis=0, concat_axis=0, tiled=True)]
    all_to_all x1, waiting for transfers between devices: 5.58 us -> 0.01 us  [shards(): lax.all_to_all(bundle, 'head', split_axis=0, concat_axis=0, tiled=True)]
    reshape x2, local copies, waits for them, and re-layouts: 3.57 us -> 0.29 us  [shards(): pieces[4].reshape(head_count, reqs_dev, local_nodes, 2 * own_width)]
    all_to_all x1, starting transfers between devices: 12.6 us -> 9.43 us  [shards(): lax.all_to_all(exchange, 'req', split_axis=0, concat_axis=0, tiled=True)]
    gather x5, local copies, waits for them, and re-layouts: 10.2 us -> 7.02 us  [place_slots(): taken = jnp.take(payload, chosen, axis=0)]
    transpose x1 -> x0, local copies, waits for them, and re-layouts: 2.79 us -> none  [shards(): jnp.einsum('btgn,bgqpn->btgqp', query_old, carry_state, preferred_element...]
    slice x2, local copies, waits for them, and re-layouts: 2.88 us -> 0.28 us  [shards(): pieces = [bundle[..., cuts[n]:cuts[n + 1]] for n in range(len(widths))]]
  transfers between devices with their start and end apart: 4 -> 4, of which waited for: 4 -> 3; matrix products, arithmetic and copies ran while one was open for 17% -> 29% of each run, Pallas kernels for 0% -> 0%
where the time goes in v3:
time: 184 us; the launch traced here: 182 us
  waiting for transfers between devices  49.6 us (27%)
  local copies, waits for them, and re-layouts  47.4 us (26%)
  other arithmetic  32 us (17%)
  matrix products  28.5 us (15%)
  starting transfers between devices  23.5 us (13%)
    all_to_all x1, waiting for transfers between devices, to_new(): lax.all_to_all(placed, 'req', split_axis=0, concat_axis=0, tiled=True)  32.2 us
    all_to_all x1, waiting for transfers between devices, shards(): lax.all_to_all(exchange, 'req', split_axis=0, concat_axis=0, tiled=True)  16.5 us
    all_to_all x1, starting transfers between devices, shards(): lax.all_to_all(exchange, 'req', split_axis=0, concat_axis=0, tiled=True)  9.43 us
    all_to_all x1, starting transfers between devices, shards(): lax.all_to_all(bundle, 'head', split_axis=0, concat_axis=0, tiled=True)  7.72 us
    dot_general x1, matrix products, shards(): jnp.einsum('btgn,bgqpn->btgqp', query_old, carry_state, preferred_element...  7.55 us
    dot_general x9, matrix products, tree_conv(): jnp.einsum('btj,bjc->btc', picked, tree_rows, preferred_element_type=jnp....  7.02 us
    gather x5, local copies, waits for them, and re-layouts, place_slots(): taken = jnp.take(payload, chosen, axis=0)  7.02 us
    select_n x3, other arithmetic, place_slots(): return jnp.where(filled, taken, jnp.zeros_like(taken))  6.03 us
  transfers between devices with their start and end apart: 4, of which 3 were waited for; matrix products, arithmetic and copies ran while one was open for 29% of the time, Pallas kernels for 0%

profile of v3, /device:TPU:1, one launch (start us, length us, event | category | flops | bytes accessed | tf_op | source)
XLA Modules:
  0.0 182.3 jit_solution(6693746527541423300)
XLA Ops:
  4.4 2.1 %concatenate.13 = bf16[16,16,3088]{2,1,0:T(8,128)(2,1)} concatenate(bf16[16,16,1024]{2,1,0:T(8,128)(2,1)S(1)} %get-tuple-element.55, bf16[16,16,1024]{2,1,0:T(8,128)(2,1)S(1)} %get-tuple-element.54, bf16[16,16,16]{2,1,0:T(8,128)(2,1)S(1)} %bitcast.179, bf16[16,16,512]{2,1,0:T(8,128)(2,1)S(1)} %get-tuple-element.43, bf16[16,16,512]{2,1,0:T(8,128)(2,1)S(1)} %get-tuple-element.42), dimensions={2} | concatenate | bytes 3162112 | tf_op jit(solution)/shard_map/concatenate | solution.py:176
  6.5 7.7 %all-to-all-start = ((bf16[16,16,3088]{2,1,0:T(8,128)(2,1)}), bf16[16,16,3088]{2,1,0:T(8,128)(2,1)S(1)}, u32[]{:S(2)}, u32[]{:S(2)}) async-start(bf16[16,16,3088]{2,1,0:T(8,128)(2,1)} %concatenate.13), calls=%async_computation | async-start | bytes 3276800 | tf_op jit(solution)/shard_map/all_to_all | solution.py:179
  37.8 1.9 %reshape.791 = f32[8,32,16,64]{3,2,1,0:T(8,128)} reshape(bf16[8,32,1024]{2,1,0:T(8,128)(2,1)S(1)} %copy-done.11) | data formatting | bytes 1572864 | tf_op jit(solution)/shard_map/convert_element_type | solution.py:150
  48.9 1.9 %gather_fusion.4 = bf16[32,9216]{1,0:T(8,128)(2,1)} fusion(bf16[8,9216]{1,0:T(8,128)(2,1)S(1)} %reshape.778, s32[1024]{0:T(1024)} %pad_clamp_fusion.2), kind=kCustom, calls=%fused_computation.4 | custom fusion | bytes 1179776 | tf_op jit(solution)/shard_map/jit(_take)/gather | solution.py:42
  54.9 1.7 pad_maximum_fusion
  56.6 9.4 %all-to-all-start.1 = ((bf16[16,2,13824]{2,1,0:T(2,128)(2,1)}), bf16[16,2,13824]{2,1,0:T(2,128)(2,1)}, u32[]{:S(2)}, u32[]{:S(2)}) async-start(bf16[16,2,13824]{2,1,0:T(2,128)(2,1)} %pad_maximum_fusion), calls=%async_computation.1 | async-start | bytes 1769472 | tf_op jit(solution)/shard_map/all_to_all | solution.py:203
  69.7 2.9 %reshape.797 = f32[8,32,1,16,64]{4,3,1,0,2:T(8,128)} reshape(f32[16,16,1024]{2,1,0:T(8,128)} %get-tuple-element.11) | data formatting | bytes 2097152 | tf_op jit(solution)/shard_map/convert_element_type | solution.py:254
  74.3 16.5 %all-to-all-done.1 = bf16[16,2,13824]{2,1,0:T(2,128)(2,1)} async-done(((bf16[16,2,13824]{2,1,0:T(2,128)(2,1)}), bf16[16,2,13824]{2,1,0:T(2,128)(2,1)}, u32[]{:S(2)}, u32[]{:S(2)}) %all-to-all-start.1) | async-done | bytes 884768 | tf_op jit(solution)/shard_map/all_to_all | solution.py:203
  90.8 2.5 %all_to_all.14 = bf16[32,13824]{1,0:T(8,128)(2,1)S(1)} reshape(bf16[16,2,13824]{2,1,0:T(2,128)(2,1)} %all-to-all-done.1) | data formatting | bytes 1769472 | tf_op jit(solution)/shard_map/all_to_all | solution.py:203
  97.1 7.5 %fusion.8 = bf16[8,32,1,16,64]{4,1,3,0,2:T(8,128)(2,1)} fusion(bf16[8,32,256,1]{2,1,3,0:T(8,128)(2,1)S(1)} %fusion.38, bf16[8,16,64,256]{3,2,1,0:T(8,128)(2,1)} %param.35, f32[8,16]{1,0:T(8,128)S(1)} %exp.60, f32[8,32,16,64]{3,2,1,0:T(8,128)} %reshape.791, f32[8,32,16]{1,2,0:T(8,128)S(1)} %copy-done.26, bf16[8,32,2048]{2,1,0:T(8,128)(2,1)S(1)} %copy-done, ...), kind=kOutput, calls=%fused_computation.26 | convolution fusion | flops 277610496 | bytes 6098948 | tf_op jit(solution)/shard_map/btgn,bgqpn->btgqp/dot_general | solution.py:216
  104.7 1.6 copy.134
  107.1 2.2 %gather_fusion.9 = bf16[32,32,1024]{2,1,0:T(8,128)(2,1)} fusion(bf16[8,32,1024]{2,1,0:T(8,128)(2,1)S(1)} %convert_element_type.280, s32[1024]{0:T(1024)} %pad_clamp_fusion.3), kind=kCustom, calls=%fused_computation.9 | custom fusion | bytes 4194432 | tf_op jit(solution)/shard_map/jit(_take)/gather | solution.py:42
  109.2 3.3 %select_select_fusion = bf16[32,32,1024]{2,1,0:T(8,128)(2,1)} fusion(bf16[32,32,1024]{2,1,0:T(8,128)(2,1)} %gather_fusion.9, pred[32]{0:T(512)(128)(4,1)S(1)} %copy-done.61, pred[32]{0:T(512)(128)(4,1)S(1)} %copy-done.55), kind=kLoop, calls=%fused_computation.23 | loop fusion | flops 2097152 | bytes 4194368 | tf_op jit(solution)/shard_map/jit(_where)/select_n | solution.py:43
  112.6 4.7 %all-to-all-start.2 = ((bf16[32,32,1024]{2,1,0:T(8,128)(2,1)}), bf16[32,32,1024]{2,1,0:T(8,128)(2,1)}, u32[]{:S(2)}, u32[]{:S(2)}) async-start(bf16[32,32,1024]{2,1,0:T(8,128)(2,1)} %select_select_fusion), calls=%async_computation.2 | async-start | bytes 4194304 | tf_op jit(solution)/shard_map/all_to_all | solution.py:112
  124.5 1.7 fusion.10
  127.4 1.9 %reshape.796 = f32[8,32,1,16,64]{4,3,1,0,2:T(8,128)} reshape(bf16[8,32,1024]{2,1,0:T(8,128)(2,1)S(1)} %multiply_convert_fusion.3) | data formatting | bytes 1572864 | tf_op jit(solution)/shard_map/convert_element_type | solution.py:252
  129.4 1.6 reshape.779
  132.8 32.2 %all-to-all-done.2 = bf16[32,32,1024]{2,1,0:T(8,128)(2,1)} async-done(((bf16[32,32,1024]{2,1,0:T(8,128)(2,1)}), bf16[32,32,1024]{2,1,0:T(8,128)(2,1)}, u32[]{:S(2)}, u32[]{:S(2)}) %all-to-all-start.2) | async-done | bytes 2097184 | tf_op jit(solution)/shard_map/all_to_all | solution.py:112
  165.0 3.1 %gather_fusion.10 = bf16[8,32,1024]{2,1,0:T(8,128)(2,1)} fusion(bf16[32,32,1024]{2,1,0:T(8,128)(2,1)} %all-to-all-done.2, s32[1024]{0:T(1024)} %pad_clamp_fusion.1), kind=kCustom, calls=%fused_computation.10 | custom fusion | bytes 1048608 | tf_op jit(solution)/shard_map/jit(_take)/gather | solution.py:113
  168.1 2.5 %gather.84 = bf16[8,32,1,16,64]{4,3,1,0,2:T(8,128)(2,1)} reshape(bf16[8,32,1024]{2,1,0:T(8,128)(2,1)} %gather_fusion.10) | data formatting | bytes 1048576 | tf_op jit(solution)/shard_map/jit(_take)/gather | solution.py:113
  170.6 5.2 %multiply_reduce_fusion = (f32[8,32]{1,0:T(8,128)S(1)}, f32[8,32,1,16,64]{4,1,3,0,2:T(8,128)}) fusion(f32[8,32,1,16,64]{4,3,1,0,2:T(8,128)} %reshape.797, f32[8,32,1,16,64]{4,3,1,0,2:T(8,128)S(1)} %copy-done.2, f32[16]{0:T(128)S(1)} %copy-done.69, bf16[8,32,1,16,64]{4,3,1,0,2:T(8,128)(2,1)} %gather.84, pred[8]{0:T(512)(128)(4,1)S(1)} %copy-done.56, ...), kind=kOutput, calls=%fused_computation.22 | convolution fusion | flops 20971264 | bytes 4285512 | tf_op jit(solution)/shard_map/btjgq,bjgqp->btgqp/dot_general | solution.py:246
  175.8 1.6 collective-permute-start
  178.4 1.9 %multiply_convert_fusion = bf16[8,32,1,16,64]{4,1,3,0,2:T(8,128)(2,1)S(1)} fusion(f32[8,32,1,16,64]{4,1,3,0,2:T(8,128)} %get-tuple-element.49, f32[16,64]{1,0:T(8,128)S(1)} %mul.356, f32[8,32]{1,0:T(8,128)S(1)} %rsqrt_bitcast_fusion), kind=kLoop, calls=%fused_computation.21 | loop fusion | flops 786432 | bytes 1577984 | tf_op jit(solution)/shard_map/convert_element_type | solution.py:274
  180.8 1.5 convert_element_type.287
  (279 shorter events, 61.8 us)
Async XLA Ops:
  0.0 97.1 %copy-start = (bf16[8,32,2048]{2,1,0:T(8,128)(2,1)S(1)}, bf16[8,32,2048]{2,1,0:T(8,128)(2,1)}, u32[]{:S(2)}) copy-start(bf16[8,32,2048]{2,1,0:T(8,128)(2,1)} %param.37) | copy-start | bytes 3145732
  6.5 15.8 %copy-start.65 = (s32[8]{0:T(128)S(1)}, s32[8]{0:T(128)}, u32[]{:S(2)}) copy-start(s32[8]{0:T(128)} %param.42) | copy-start | bytes 100
  6.5 15.9 %copy-start.5 = (s32[8,32,32]{2,1,0:T(8,128)S(1)}, s32[8,32,32]{2,1,0:T(8,128)}, u32[]{:S(2)}) copy-start(s32[8,32,32]{2,1,0:T(8,128)} %param.26) | copy-start | bytes 98308
  6.5 15.9 %copy-start.13 = (s32[8,32,32]{2,1,0:T(8,128)S(1)}, s32[8,32,32]{2,1,0:T(8,128)}, u32[]{:S(2)}) copy-start(s32[8,32,32]{2,1,0:T(8,128)} %param.41) | copy-start | bytes 98308
  6.5 22.7 %copy-start.31 = (bf16[4,4096]{1,0:T(4,128)(2,1)S(1)}, bf16[4,4096]{1,0:T(4,128)(2,1)}, u32[]{:S(2)}) copy-start(bf16[4,4096]{1,0:T(4,128)(2,1)} %param.29) | copy-start | bytes 98308
  6.5 23.5 %copy-start.37 = (f32[4096]{0:T(1024)S(1)}, f32[4096]{0:T(1024)}, u32[]{:S(2)}) copy-start(f32[4096]{0:T(1024)} %param.30) | copy-start | bytes 49156
  6.5 31.3 %copy-start.11 = (bf16[8,32,1024]{2,1,0:T(8,128)(2,1)S(1)}, bf16[8,32,1024]{2,1,0:T(8,128)(2,1)}, u32[]{:S(2)}) copy-start(bf16[8,32,1024]{2,1,0:T(8,128)(2,1)} %param.36) | copy-start | bytes 1572868
  6.5 38.1 %all-to-all-start = ((bf16[16,16,3088]{2,1,0:T(8,128)(2,1)}), bf16[16,16,3088]{2,1,0:T(8,128)(2,1)S(1)}, u32[]{:S(2)}, u32[]{:S(2)}) async-start(bf16[16,16,3088]{2,1,0:T(8,128)(2,1)} %concatenate.13), calls=%async_computation | async-start | bytes 3276800 | tf_op jit(solution)/shard_map/all_to_all | solution.py:179
  17.5 25.2 %copy-start.32 = (bf16[4,1024]{1,0:T(4,128)(2,1)S(1)}, bf16[4,1024]{1,0:T(4,128)(2,1)}, u32[]{:S(2)}) copy-start(bf16[4,1024]{1,0:T(4,128)(2,1)} %param.27) | copy-start | bytes 24580
  23.3 16.4 %copy-start.66 = (s32[8]{0:T(128)S(1)}, s32[8]{0:T(128)}, u32[]{:S(2)}) copy-start(s32[8]{0:T(128)} %fusion.122) | copy-start | bytes 100
  23.6 21.0 %copy-start.33 = (pred[8,32]{1,0:T(8,128)(4,1)}, pred[8,32]{1,0:T(8,128)(4,1)S(1)}, u32[]{:S(2)}) copy-start(pred[8,32]{1,0:T(8,128)(4,1)S(1)} %broadcast_compare_fusion.1) | copy-start | bytes 772
  54.8 11.4 %copy-start.18 = (f32[8,32,16]{1,2,0:T(8,128)S(1)}, f32[8,32,16]{1,2,0:T(8,128)}, u32[]{:S(2)}) copy-start(f32[8,32,16]{1,2,0:T(8,128)} %param.38) | copy-start | bytes 49156
  54.8 11.4 %copy-start.60 = (f32[16]{0:T(128)S(1)}, f32[16]{0:T(128)}, u32[]{:S(2)}) copy-start(f32[16]{0:T(128)} %param.32) | copy-start | bytes 196
  54.8 11.4 %copy-start.62 = (f32[16]{0:T(128)S(1)}, f32[16]{0:T(128)}, u32[]{:S(2)}) copy-start(f32[16]{0:T(128)} %exponential_negate_fusion) | copy-start | bytes 196
  54.8 12.1 %copy-start.14 = (s32[8,32,32]{2,1,0:T(8,128)S(1)}, s32[8,32,32]{2,1,0:T(8,128)}, u32[]{:S(2)}) copy-start(s32[8,32,32]{2,1,0:T(8,128)} %param.41) | copy-start | bytes 98308
  54.9 12.1 %copy-start.47 = (pred[8,32]{1,0:T(8,128)(4,1)S(1)}, pred[8,32]{1,0:T(8,128)(4,1)}, u32[]{:S(2)}) copy-start(pred[8,32]{1,0:T(8,128)(4,1)} %copy-done.46) | copy-start | bytes 772
  56.6 34.2 %all-to-all-start.1 = ((bf16[16,2,13824]{2,1,0:T(2,128)(2,1)}), bf16[16,2,13824]{2,1,0:T(2,128)(2,1)}, u32[]{:S(2)}, u32[]{:S(2)}) async-start(bf16[16,2,13824]{2,1,0:T(2,128)(2,1)} %pad_maximum_fusion), calls=%async_computation.1 | async-start | bytes 1769472 | tf_op jit(solution)/shard_map/all_to_all | solution.py:203
  112.6 52.4 %all-to-all-start.2 = ((bf16[32,32,1024]{2,1,0:T(8,128)(2,1)}), bf16[32,32,1024]{2,1,0:T(8,128)(2,1)}, u32[]{:S(2)}, u32[]{:S(2)}) async-start(bf16[32,32,1024]{2,1,0:T(8,128)(2,1)} %select_select_fusion), calls=%async_computation.2 | async-start | bytes 4194304 | tf_op jit(solution)/shard_map/all_to_all | solution.py:112
  132.5 38.1 %copy-start.2 = (f32[8,32,1,16,64]{4,3,1,0,2:T(8,128)S(1)}, f32[8,32,1,16,64]{4,3,1,0,2:T(8,128)}, u32[]{:S(2)}) copy-start(f32[8,32,1,16,64]{4,3,1,0,2:T(8,128)} %reshape.796) | copy-start | bytes 3145732
  132.5 38.1 %copy-start.24 = (f32[8,32,16]{1,2,0:T(8,128)S(1)}, f32[8,32,16]{1,2,0:T(8,128)}, u32[]{:S(2)}) copy-start(f32[8,32,16]{1,2,0:T(8,128)} %get-tuple-element.46) | copy-start | bytes 49156
  132.5 38.1 %copy-start.69 = (f32[16]{0:T(128)S(1)}, f32[16]{0:T(128)}, u32[]{:S(2)}) copy-start(f32[16]{0:T(128)} %param.33) | copy-start | bytes 196
  132.8 37.8 %copy-start.25 = (f32[8,32,16]{1,2,0:T(8,128)S(1)}, f32[8,32,16]{1,2,0:T(8,128)}, u32[]{:S(2)}) copy-start(f32[8,32,16]{1,2,0:T(8,128)} %get-tuple-element.47) | copy-start | bytes 49156
  132.8 37.8 %copy-start.27 = (f32[8,32,16]{1,2,0:T(8,128)S(1)}, f32[8,32,16]{1,2,0:T(8,128)}, u32[]{:S(2)}) copy-start(f32[8,32,16]{1,2,0:T(8,128)} %copy.129) | copy-start | bytes 49156
  175.8 2.6 %collective-permute-start = (f32[8,32,1]{1,0,2:T(8,128)S(1)}, f32[8,32,1]{1,0,2:T(8,128)S(1)}, u32[]{:S(2)}, u32[]{:S(2)}) collective-permute-start(f32[8,32,1]{1,0,2:T(8,128)S(1)} %bitcast.197), channel_id=1, source_target_pairs={{0,1},{1,0},{2,3},{3,2},{4,5},{5,4},{6,7},{7,6},{8,9},{9,8},{10,11... | collective-permute-start | bytes 3080 | tf_op jit(solution)/shard_map/ppermute | solution.py:258
  (52 other events, 183.1 us)

commit v4 on v3

--- a/solution.py
+++ b/solution.py
@@ -89,6 +89,7 @@
     span_heads = min(local_heads, per_group)
     span_groups = local_heads // span_heads
     per_dest = per_group // span_heads
+    assert span_groups == 1
     first_group = head_index * local_heads // per_group
     slot_count = req_count * MOST
     own_width = span_groups * STATE
@@ -107,15 +108,17 @@
     anchor = jnp.sum(jnp.where(match, all_ids[None, :], 0), axis=1)
     recv_pos = anchor // reqs_dev * MOST + jnp.take(arrival.reshape(-1), anchor)
 
-    def to_new(payload):
-        placed = place_slots(payload, send_pos, slot_count)
-        moved = lax.all_to_all(placed, "req", split_axis=0, concat_axis=0, tiled=True)
-        return jnp.take(moved, recv_pos, axis=0)
-
-    def to_old(payload):
-        placed = place_slots(payload, recv_pos, slot_count)
-        moved = lax.all_to_all(placed, "req", split_axis=0, concat_axis=0, tiled=True)
-        return jnp.take(moved, send_pos, axis=0)
+    slot_ids = jnp.arange(slot_count, dtype=jnp.int32)
+    send_hot = (send_pos[None, :] == slot_ids[:, None]).astype(jnp.bfloat16)
+    recv_hot = (recv_pos[None, :] == slot_ids[:, None]).astype(jnp.bfloat16)
+
+    def spread(hot, payload):
+        return jnp.einsum(
+            "pa,ac->pc", hot, payload, preferred_element_type=jnp.float32
+        ).astype(jnp.bfloat16)
+
+    def gather_back(hot, moved):
+        return jnp.einsum("pa,pc->ac", hot, moved, preferred_element_type=jnp.float32)
 
     decay_rates = -jnp.exp(log_rates)
     node_ids = jnp.arange(NODES, dtype=jnp.int32)
@@ -163,6 +166,7 @@
         * old_state.reshape(reqs_dev, span_groups, span_heads, HEAD_DIM, STATE).astype(jnp.float32)
         + update
     ).astype(jnp.bfloat16)
+    carry_state = lax.optimization_barrier(carry_state)
     tree_rows = tree_heads.shape[0]
     head_width = local_heads * HEAD_DIM
     split_heads = jnp.moveaxis(tree_heads.reshape(tree_rows, head_count, head_width), 1, 0)
@@ -197,12 +201,16 @@
     ).reshape(reqs_dev, -1)
     new_len = new_part.shape[-1]
     exchange = jnp.concatenate(
-        [place_slots(new_part, send_pos, slot_count), place_slots(old_part, recv_pos, slot_count)],
+        [spread(send_hot, new_part), spread(recv_hot, old_part)],
         axis=-1,
     )
     exchange = lax.all_to_all(exchange, "req", split_axis=0, concat_axis=0, tiled=True)
-    tails_new = jnp.take(exchange[:, :new_len], recv_pos, axis=0).reshape(reqs_dev, 3, -1)
-    rows_old = jnp.take(exchange[:, new_len:], send_pos, axis=0).reshape(reqs_dev, NODES, -1)
+    tails_new = (
+        gather_back(recv_hot, exchange[:, :new_len]).astype(jnp.bfloat16).reshape(reqs_dev, 3, -1)
+    )
+    rows_old = (
+        gather_back(send_hot, exchange[:, new_len:]).astype(jnp.bfloat16).reshape(reqs_dev, NODES, -1)
+    )
     tree_old = rows_old[..., own_width:].astype(jnp.int32)
     kernel_own = own_columns(kernel_groups, span_groups, head_count, per_dest)[head_index]
     shift_own = own_columns(shift_groups, span_groups, head_count, per_dest)[head_index]
@@ -214,9 +222,15 @@
         shift_own[own_width:],
     ).reshape(reqs_dev, NODES, span_groups, STATE)
     carried_old = jnp.einsum(
-        "btgn,bgqpn->btgqp", query_old, carry_state, preferred_element_type=jnp.float32
-    ).reshape(reqs_dev, NODES, head_width)
-    carried = to_new(carried_old.astype(jnp.bfloat16)).astype(jnp.float32).reshape(reqs_dev, NODES, span_groups, span_heads, HEAD_DIM)
+        "btn,bmn->btm",
+        query_old.reshape(reqs_dev, NODES, STATE),
+        carry_state.reshape(reqs_dev, head_width, STATE),
+        preferred_element_type=jnp.float32,
+    ).reshape(reqs_dev, NODES * head_width)
+    carried_moved = lax.all_to_all(
+        spread(send_hot, carried_old.astype(jnp.bfloat16)), "req", split_axis=0, concat_axis=0, tiled=True
+    )
+    carried = gather_back(recv_hot, carried_moved).reshape(reqs_dev, NODES, head_width).reshape(reqs_dev, NODES, span_groups, span_heads, HEAD_DIM)
     conv_heads = tree_conv(
         head_rows, tails_new[..., :head_width], new_tree, kernel_heads, shift_heads
     )

time: 184 us -> 173 us (0.940)
  other arithmetic: 32 us -> 14.3 us
  matrix products: 28.5 us -> 33.1 us
  starting transfers between devices: 23.5 us -> 25.6 us
  waiting for transfers between devices: 49.6 us -> 51.5 us
    gather x11 -> x0, local copies, waits for them, and re-layouts: 14.5 us -> none  [the longest x5 7.02 us: place_slots(): taken = jnp.take(payload, chosen, axis=0)]
    dot_general x1 -> x8, matrix products: 7.55 us -> 18.2 us  [the longest x3 6.12 us: gather_back(): jnp.einsum('pa,pc->ac', hot, moved, preferred_element_type=jnp.float32)]
    select_n x8 -> x0, other arithmetic: 9.27 us -> none  [the longest x3 6.03 us: place_slots(): return jnp.where(filled, taken, jnp.zeros_like(taken))]
    all_to_all x1, waiting for transfers between devices: 16.5 us -> 7.72 us  [shards(): lax.all_to_all(exchange, 'req', split_axis=0, concat_axis=0, tiled=True)]
    all_to_all x0 -> x2, local copies, waits for them, and re-layouts: none -> 7.15 us  [shards(): lax.all_to_all(spread(send_hot, carried_old.astype(jnp.bfloat16)), 'req',...]
    all_to_all x1, waiting for transfers between devices: 0.01 us -> 6.27 us  [shards(): lax.all_to_all(bundle, 'head', split_axis=0, concat_axis=0, tiled=True)]
    dot_general x0 -> x1, local copies, waits for them, and re-layouts: none -> 5.53 us  [gather_back(): jnp.einsum('pa,pc->ac', hot, moved, preferred_element_type=jnp.float32)]
    and x5 -> x0, other arithmetic: 4.07 us -> none  [the longest x3 2.34 us: place_slots(): taken = jnp.take(payload, chosen, axis=0)]
  transfers between devices with their start and end apart: 4 -> 4, of which waited for: 3 -> 4; matrix products, arithmetic and copies ran while one was open for 29% -> 26% of each run, Pallas kernels for 0% -> 0%
where the time goes in v4:
time: 173 us; the launch traced here: 172 us
  waiting for transfers between devices  51.5 us (30%)
  local copies, waits for them, and re-layouts  46 us (27%)
  matrix products  33.1 us (19%)
  starting transfers between devices  25.6 us (15%)
  other arithmetic  14.3 us (8%)
    all_to_all x1, waiting for transfers between devices, shards(): lax.all_to_all(spread(send_hot, carried_old.astype(jnp.bfloat16)), 'req',...  35.4 us
    all_to_all x1, starting transfers between devices, shards(): lax.all_to_all(exchange, 'req', split_axis=0, concat_axis=0, tiled=True)  12.8 us
    all_to_all x1, waiting for transfers between devices, shards(): lax.all_to_all(exchange, 'req', split_axis=0, concat_axis=0, tiled=True)  7.72 us
    all_to_all x1, starting transfers between devices, shards(): lax.all_to_all(bundle, 'head', split_axis=0, concat_axis=0, tiled=True)  7.72 us
    all_to_all x2, local copies, waits for them, and re-layouts, shards(): lax.all_to_all(spread(send_hot, carried_old.astype(jnp.bfloat16)), 'req',...  7.15 us
    all_to_all x1, waiting for transfers between devices, shards(): lax.all_to_all(bundle, 'head', split_axis=0, concat_axis=0, tiled=True)  6.27 us
    dot_general x3, matrix products, gather_back(): jnp.einsum('pa,pc->ac', hot, moved, preferred_element_type=jnp.float32)  6.12 us
    dot_general x1, matrix products, shards(): jnp.einsum('bjgqp,bjgn->bgqpn', weighted, key_slice, preferred_element_ty...  5.76 us
  transfers between devices with their start and end apart: 4, of which 4 were waited for; matrix products, arithmetic and copies ran while one was open for 26% of the time, Pallas kernels for 0%

profile of v4, /device:TPU:1, one launch (start us, length us, event | category | flops | bytes accessed | tf_op | source)
XLA Modules:
  0.0 171.6 jit_solution(2390897556445687427)
XLA Ops:
  4.4 2.1 %concatenate.12 = bf16[16,16,3088]{2,1,0:T(8,128)(2,1)} concatenate(bf16[16,16,1024]{2,1,0:T(8,128)(2,1)S(1)} %get-tuple-element.51, bf16[16,16,1024]{2,1,0:T(8,128)(2,1)S(1)} %get-tuple-element.50, bf16[16,16,16]{2,1,0:T(8,128)(2,1)S(1)} %bitcast.159, bf16[16,16,512]{2,1,0:T(8,128)(2,1)S(1)} %get-tuple-element.41, bf16[16,16,512]{2,1,0:T(8,128)(2,1)S(1)} %get-tuple-element.40), dimensions={2} | concatenate | bytes 3162112 | tf_op jit(solution)/shard_map/concatenate | solution.py:180
  6.5 7.7 %all-to-all-start = ((bf16[16,16,3088]{2,1,0:T(8,128)(2,1)}), bf16[16,16,3088]{2,1,0:T(8,128)(2,1)S(1)}, u32[]{:S(2)}, u32[]{:S(2)}) async-start(bf16[16,16,3088]{2,1,0:T(8,128)(2,1)} %concatenate.12), calls=%async_computation | async-start | bytes 3276800 | tf_op jit(solution)/shard_map/all_to_all | solution.py:183
  22.7 1.4 broadcast_select_fusion.2
  29.4 6.3 %all-to-all-done = bf16[16,16,3088]{2,1,0:T(8,128)(2,1)S(1)} async-done(((bf16[16,16,3088]{2,1,0:T(8,128)(2,1)}), bf16[16,16,3088]{2,1,0:T(8,128)(2,1)S(1)}, u32[]{:S(2)}, u32[]{:S(2)}) %all-to-all-start) | async-done | bytes 1581088 | tf_op jit(solution)/shard_map/all_to_all | solution.py:183
  44.1 12.8 %all-to-all-start.1 = ((bf16[16,2,13824]{2,1,0:T(2,128)(2,1)}), bf16[16,2,13824]{2,1,0:T(2,128)(2,1)}, u32[]{:S(2)}, u32[]{:S(2)}) async-start(bf16[16,2,13824]{2,1,0:T(2,128)(2,1)} %all_to_all.20), calls=%async_computation.1 | async-start | bytes 1769472 | tf_op jit(solution)/shard_map/all_to_all | solution.py:207
  58.2 1.6 reshape.590
  61.5 1.6 broadcast_multiply_fusion
  65.4 5.8 %fusion = bf16[8,1,16,64,256]{4,3,2,0,1:T(8,128)(2,1)} fusion(bf16[8,16,64,256]{3,2,1,0:T(8,128)(2,1)} %param.35, f32[8,16]{1,0:T(8,128)S(1)} %exp.61, f32[8,32,16,64]{3,2,1,0:T(8,128)S(1)} %reshape.590, f32[8,32,16]{1,2,0:T(8,128)S(1)} %bitcast_multiply_fusion, bf16[8,32,2048]{2,1,0:T(8,128)(2,1)S(1)} %copy-done, s32[]{:T(128)S(6)} %select_n.221), kind=kOutput, calls=%fused_computation.11 | convolution fusion | flops 143130624 | bytes 10686468 | tf_op jit(solution)/shard_map/bjgqp,bjgn->bgqpn/dot_general | solution.py:161
  72.0 1.9 %reshape.592 = f32[8,32,1,16,64]{4,3,1,0,2:T(8,128)} reshape(f32[16,16,1024]{2,1,0:T(8,128)S(1)} %get-tuple-element.9) | data formatting | bytes 2097152 | tf_op jit(solution)/shard_map/convert_element_type | solution.py:268
  73.9 7.7 %all-to-all-done.1 = bf16[16,2,13824]{2,1,0:T(2,128)(2,1)} async-done(((bf16[16,2,13824]{2,1,0:T(2,128)(2,1)}), bf16[16,2,13824]{2,1,0:T(2,128)(2,1)}, u32[]{:S(2)}, u32[]{:S(2)}) %all-to-all-start.1) | async-done | bytes 884768 | tf_op jit(solution)/shard_map/all_to_all | solution.py:207
  81.7 2.5 %all_to_all.22 = bf16[32,13824]{1,0:T(8,128)(2,1)S(1)} reshape(bf16[16,2,13824]{2,1,0:T(2,128)(2,1)} %all-to-all-done.1) | data formatting | bytes 1769472 | tf_op jit(solution)/shard_map/all_to_all | solution.py:207
  87.1 3.7 %fusion.12 = bf16[1,8,32,1024]{3,2,1,0:T(8,128)(2,1)S(1)} fusion(bf16[8,1024,256]{2,1,0:T(8,128)(2,1)} %bitcast.134, f32[8,32,256]{2,1,0:T(8,128)S(1)} %fusion.22, f32[8,32,256]{2,1,0:T(8,128)S(1)} %fusion.93, f32[256]{0:T(256)S(1)} %bitcast.173, bf16[8,32,288]{2,1,0:T(8,128)(2,1)S(1)} %reshape.575, s32[8,32]{1,0:T(8,128)S(1)} %get-tuple-element.23, ...), kind=kOutput, calls=%fused_computation.34 | convolution fusion | flops 139231232 | bytes 5393408 | tf_op jit(solution)/shard_map/btn,bmn->btm/dot_general | solution.py:224
  91.1 2.0 %convolution_convert_fusion = bf16[32,32768]{1,0:T(8,128)(2,1)} fusion(bf16[8,32768]{1,0:T(8,128)(2,1)S(1)} %bitcast.146, s32[8]{0:T(128)S(1)} %copy-done.33), kind=kOutput, calls=%fused_computation.5 | convolution fusion | flops 17826048 | bytes 2621472 | tf_op jit(solution)/shard_map/pa,ac->pc/dot_general | solution.py:116
  93.1 4.4 %all_to_all.23 = bf16[16,2,32768]{2,1,0:T(2,128)(2,1)} reshape(bf16[32,32768]{1,0:T(8,128)(2,1)} %convolution_convert_fusion) | data formatting | bytes 4194304 | tf_op jit(solution)/shard_map/all_to_all | solution.py:230
  97.5 4.7 %all-to-all-start.2 = ((bf16[16,2,32768]{2,1,0:T(2,128)(2,1)}), bf16[16,2,32768]{2,1,0:T(2,128)(2,1)}, u32[]{:S(2)}, u32[]{:S(2)}) async-start(bf16[16,2,32768]{2,1,0:T(2,128)(2,1)} %all_to_all.23), calls=%async_computation.2 | async-start | bytes 4194304 | tf_op jit(solution)/shard_map/all_to_all | solution.py:230
  109.6 2.0 %reshape.591 = f32[8,32,1,16,64]{4,3,1,0,2:T(8,128)} reshape(bf16[8,32,1024]{2,1,0:T(8,128)(2,1)S(1)} %multiply_convert_fusion.3) | data formatting | bytes 1572864 | tf_op jit(solution)/shard_map/convert_element_type | solution.py:266
  111.5 1.6 reshape.572
  114.5 35.4 %all-to-all-done.2 = bf16[16,2,32768]{2,1,0:T(2,128)(2,1)} async-done(((bf16[16,2,32768]{2,1,0:T(2,128)(2,1)}), bf16[16,2,32768]{2,1,0:T(2,128)(2,1)}, u32[]{:S(2)}, u32[]{:S(2)}) %all-to-all-start.2) | async-done | bytes 2097184 | tf_op jit(solution)/shard_map/all_to_all | solution.py:230
  150.0 2.8 %all_to_all.25 = bf16[32,32768]{1,0:T(8,128)(2,1)S(1)} reshape(bf16[16,2,32768]{2,1,0:T(2,128)(2,1)} %all-to-all-done.2) | data formatting | bytes 4194304 | tf_op jit(solution)/shard_map/all_to_all | solution.py:230
  152.7 5.5 %dot_general.141 = bf16[32,16,64,32]{2,1,0,3:T(8,128)(2,1)} reshape(bf16[32768,32]{0,1:T(8,128)(2,1)S(1)} %bitcast.139) | data formatting | bytes 4194304 | tf_op jit(solution)/shard_map/pa,pc->ac/dot_general | solution.py:121
  158.3 4.7 %fusion.1 = f32[8,32,16,64]{3,0,2,1:T(8,128)S(1)} fusion(bf16[32,16,64,32]{2,1,0,3:T(8,128)(2,1)} %dot_general.141, s32[8]{0:T(128)S(1)} %copy-done.35), kind=kOutput, calls=%fused_computation.12 | convolution fusion | flops 16777472 | bytes 3145760 | tf_op jit(solution)/shard_map/pa,pc->ac/dot_general | solution.py:121
  163.1 3.7 %multiply_reduce_fusion = (f32[8,32]{1,0:T(8,128)S(1)}, f32[8,32,1,16,64]{4,1,3,0,2:T(8,128)S(1)}) fusion(f32[8,32,1,16,64]{4,3,1,0,2:T(8,128)S(1)} %copy-done.5, f32[8,32,1,16,64]{4,3,1,0,2:T(8,128)S(1)} %copy-done.4, f32[16]{0:T(128)S(1)} %copy-done.53, f32[8,32,16,64]{3,0,2,1:T(8,128)S(1)} %fusion.1, f32[8,32,16]{1,2,0:T(8,128)S(1)} %copy-done.17, ...), kind=kOutput, calls=%fused_computation.22 | convolution fusion | flops 20446976 | bytes 4809792 | tf_op jit(solution)/shard_map/btjgq,bjgqp->btgqp/dot_general | solution.py:260
  167.2 2.1 %collective-permute-done = f32[8,32,1]{1,0,2:T(8,128)S(1)} collective-permute-done((f32[8,32,1]{1,0,2:T(8,128)S(1)}, f32[8,32,1]{1,0,2:T(8,128)S(1)}, u32[]{:S(2)}, u32[]{:S(2)}) %collective-permute-start) | collective-permute-done | bytes 1056 | tf_op jit(solution)/shard_map/ppermute | solution.py:272
  170.1 1.5 convert_element_type.292
  (222 shorter events, 45.1 us)
Async XLA Ops:
  0.0 65.4 %copy-start = (bf16[8,32,2048]{2,1,0:T(8,128)(2,1)S(1)}, bf16[8,32,2048]{2,1,0:T(8,128)(2,1)}, u32[]{:S(2)}) copy-start(bf16[8,32,2048]{2,1,0:T(8,128)(2,1)} %param.37) | copy-start | bytes 3145732
  6.5 7.8 %copy-start.51 = (s32[128]{0:T(128)S(1)}, s32[128]{0:T(128)}, u32[]{:S(2)}) copy-start(s32[128]{0:T(128)} %param.43) | copy-start | bytes 1540
  6.5 8.2 %copy-start.50 = (s32[8]{0:T(128)S(1)}, s32[8]{0:T(128)}, u32[]{:S(2)}) copy-start(s32[8]{0:T(128)} %param.42) | copy-start | bytes 100
  6.5 8.2 %copy-start.7 = (s32[8,32,32]{2,1,0:T(8,128)S(1)}, s32[8,32,32]{2,1,0:T(8,128)}, u32[]{:S(2)}) copy-start(s32[8,32,32]{2,1,0:T(8,128)} %param.26) | copy-start | bytes 98308
  6.5 8.2 %copy-start.12 = (s32[8,32,32]{2,1,0:T(8,128)S(1)}, s32[8,32,32]{2,1,0:T(8,128)}, u32[]{:S(2)}) copy-start(s32[8,32,32]{2,1,0:T(8,128)} %param.41) | copy-start | bytes 98308
  6.5 12.9 %copy-start.23 = (bf16[4,4096]{1,0:T(4,128)(2,1)S(1)}, bf16[4,4096]{1,0:T(4,128)(2,1)}, u32[]{:S(2)}) copy-start(bf16[4,4096]{1,0:T(4,128)(2,1)} %param.29) | copy-start | bytes 98308
  6.5 21.3 %copy-start.24 = (bf16[4,1024]{1,0:T(4,128)(2,1)S(1)}, bf16[4,1024]{1,0:T(4,128)(2,1)}, u32[]{:S(2)}) copy-start(bf16[4,1024]{1,0:T(4,128)(2,1)} %param.27) | copy-start | bytes 24580
  6.5 22.0 %copy-start.10 = (bf16[8,32,1024]{2,1,0:T(8,128)(2,1)S(1)}, bf16[8,32,1024]{2,1,0:T(8,128)(2,1)}, u32[]{:S(2)}) copy-start(bf16[8,32,1024]{2,1,0:T(8,128)(2,1)} %param.39) | copy-start | bytes 1572868
  6.5 29.1 %all-to-all-start = ((bf16[16,16,3088]{2,1,0:T(8,128)(2,1)}), bf16[16,16,3088]{2,1,0:T(8,128)(2,1)S(1)}, u32[]{:S(2)}, u32[]{:S(2)}) async-start(bf16[16,16,3088]{2,1,0:T(8,128)(2,1)} %concatenate.12), calls=%async_computation | async-start | bytes 3276800 | tf_op jit(solution)/shard_map/all_to_all | solution.py:183
  16.0 22.9 %copy-start.25 = (pred[8,32]{1,0:T(8,128)(4,1)}, pred[8,32]{1,0:T(8,128)(4,1)S(1)}, u32[]{:S(2)}) copy-start(pred[8,32]{1,0:T(8,128)(4,1)S(1)} %broadcast_compare_fusion.1) | copy-start | bytes 772
  29.4 11.4 %copy-start.15 = (bf16[8,3,1024]{2,1,0:T(4,128)(2,1)S(1)}, bf16[8,3,1024]{2,1,0:T(4,128)(2,1)}, u32[]{:S(2)}) copy-start(bf16[8,3,1024]{2,1,0:T(4,128)(2,1)} %convolution_convert_fusion.6) | copy-start | bytes 147460
  29.4 12.6 %copy-start.32 = (s32[8]{0:T(128)S(1)}, s32[8]{0:T(128)}, u32[]{:S(2)}) copy-start(s32[8]{0:T(128)} %dynamic-slice_reduce_fusion) | copy-start | bytes 100
  29.4 12.8 %copy-start.34 = (s32[8]{0:T(128)S(1)}, s32[8]{0:T(128)}, u32[]{:S(2)}) copy-start(s32[8]{0:T(128)} %fusion.124) | copy-start | bytes 100
  44.1 15.8 %slice-start = ((bf16[16,16,3088]{2,1,0:T(8,128)(2,1)}), bf16[16,16,16]{2,1,0:T(8,128)(2,1)S(1)}, s32[]{:S(2)}) async-start(bf16[16,16,3088]{2,1,0:T(8,128)(2,1)} %copy-done.1), calls=%async_computation.3 | async-start | bytes 131072 | tf_op jit(solution)/shard_map/slice | solution.py:187
  44.1 37.6 %all-to-all-start.1 = ((bf16[16,2,13824]{2,1,0:T(2,128)(2,1)}), bf16[16,2,13824]{2,1,0:T(2,128)(2,1)}, u32[]{:S(2)}, u32[]{:S(2)}) async-start(bf16[16,2,13824]{2,1,0:T(2,128)(2,1)} %all_to_all.20), calls=%async_computation.1 | async-start | bytes 1769472 | tf_op jit(solution)/shard_map/all_to_all | solution.py:207
  56.8 7.6 %copy-start.26 = (pred[8,32]{1,0:T(8,128)(4,1)S(1)}, pred[8,32]{1,0:T(8,128)(4,1)}, u32[]{:S(2)}) copy-start(pred[8,32]{1,0:T(8,128)(4,1)} %copy-done.25) | copy-start | bytes 772
  58.2 13.0 %copy-start.36 = (f32[1,512]{1,0:T(1,128)}, f32[1,512]{1,0:T(1,128)S(1)}, u32[]{:S(2)}) copy-start(f32[1,512]{1,0:T(1,128)S(1)} %broadcast_select_fusion.3) | copy-start | bytes 6148
  72.0 13.0 %copy-start.33 = (s32[8]{0:T(128)S(1)}, s32[8]{0:T(128)}, u32[]{:S(2)}) copy-start(s32[8]{0:T(128)} %dynamic-slice_reduce_fusion) | copy-start | bytes 100
  73.9 12.7 %slice-start.1 = ((f32[1,512]{1,0:T(1,128)}), f32[1,256]{1,0:T(1,128)S(1)}, s32[]{:S(2)}) async-start(f32[1,512]{1,0:T(1,128)} %copy-done.36), calls=%async_computation.4 | async-start | bytes 2048 | tf_op jit(solution)/shard_map/slice | solution.py:222
  73.9 12.7 %copy-start.41 = (f32[1,256]{1,0:T(1,128)S(1)}, f32[1,256]{1,0:T(1,128)}, u32[]{:S(2)}) copy-start(f32[1,256]{1,0:T(1,128)} %get-tuple-element.30) | copy-start | bytes 3076
  73.9 12.7 %copy-start.42 = (f32[1,256]{1,0:T(1,128)S(1)}, f32[1,256]{1,0:T(1,128)}, u32[]{:S(2)}) copy-start(f32[1,256]{1,0:T(1,128)} %get-tuple-element.31) | copy-start | bytes 3076
  73.9 12.9 %copy-start.40 = (f32[1,256]{1,0:T(1,128)S(1)}, f32[1,256]{1,0:T(1,128)}, u32[]{:S(2)}) copy-start(f32[1,256]{1,0:T(1,128)} %get-tuple-element.29) | copy-start | bytes 3076
  97.5 52.5 %all-to-all-start.2 = ((bf16[16,2,32768]{2,1,0:T(2,128)(2,1)}), bf16[16,2,32768]{2,1,0:T(2,128)(2,1)}, u32[]{:S(2)}, u32[]{:S(2)}) async-start(bf16[16,2,32768]{2,1,0:T(2,128)(2,1)} %all_to_all.23), calls=%async_computation.2 | async-start | bytes 4194304 | tf_op jit(solution)/shard_map/all_to_all | solution.py:230
  166.7 2.5 %collective-permute-start = (f32[8,32,1]{1,0,2:T(8,128)S(1)}, f32[8,32,1]{1,0,2:T(8,128)S(1)}, u32[]{:S(2)}, u32[]{:S(2)}) collective-permute-start(f32[8,32,1]{1,0,2:T(8,128)S(1)} %bitcast.177), channel_id=1, source_target_pairs={{0,1},{1,0},{2,3},{3,2},{4,5},{5,4},{6,7},{7,6},{8,9},{9,8},{10,11... | collective-permute-start | bytes 3080 | tf_op jit(solution)/shard_map/ppermute | solution.py:272
  (36 other events, 124.4 us)

commit v5 on v4

--- a/solution.py
+++ b/solution.py
@@ -114,11 +114,11 @@
 
     def spread(hot, payload):
         return jnp.einsum(
-            "pa,ac->pc", hot, payload, preferred_element_type=jnp.float32
+            "pa,a...->p...", hot, payload, preferred_element_type=jnp.float32
         ).astype(jnp.bfloat16)
 
     def gather_back(hot, moved):
-        return jnp.einsum("pa,pc->ac", hot, moved, preferred_element_type=jnp.float32)
+        return jnp.einsum("pa,p...->a...", hot, moved, preferred_element_type=jnp.float32)
 
     decay_rates = -jnp.exp(log_rates)
     node_ids = jnp.arange(NODES, dtype=jnp.int32)
@@ -195,10 +195,10 @@
     tail_groups = jnp.einsum(
         "bij,bjc->bic", tail_pick, prior_own, preferred_element_type=jnp.float32
     ).astype(jnp.bfloat16)
-    new_part = jnp.concatenate([tail_heads, tail_groups], axis=-1).reshape(reqs_dev, -1)
+    new_part = jnp.concatenate([tail_heads, tail_groups], axis=-1).reshape(reqs_dev, NODES, -1)
     old_part = jnp.concatenate(
         [group_rows[..., own_width:], new_tree.astype(jnp.bfloat16)], axis=-1
-    ).reshape(reqs_dev, -1)
+    )
     new_len = new_part.shape[-1]
     exchange = jnp.concatenate(
         [spread(send_hot, new_part), spread(recv_hot, old_part)],
@@ -206,11 +206,9 @@
     )
     exchange = lax.all_to_all(exchange, "req", split_axis=0, concat_axis=0, tiled=True)
     tails_new = (
-        gather_back(recv_hot, exchange[:, :new_len]).astype(jnp.bfloat16).reshape(reqs_dev, 3, -1)
-    )
-    rows_old = (
-        gather_back(send_hot, exchange[:, new_len:]).astype(jnp.bfloat16).reshape(reqs_dev, NODES, -1)
-    )
+        gather_back(recv_hot, exchange[..., :new_len]).astype(jnp.bfloat16).reshape(reqs_dev, 3, -1)
+    )
+    rows_old = gather_back(send_hot, exchange[..., new_len:]).astype(jnp.bfloat16)
     tree_old = rows_old[..., own_width:].astype(jnp.int32)
     kernel_own = own_columns(kernel_groups, span_groups, head_count, per_dest)[head_index]
     shift_own = own_columns(shift_groups, span_groups, head_count, per_dest)[head_index]
@@ -226,11 +224,11 @@
         query_old.reshape(reqs_dev, NODES, STATE),
         carry_state.reshape(reqs_dev, head_width, STATE),
         preferred_element_type=jnp.float32,
-    ).reshape(reqs_dev, NODES * head_width)
+    )
     carried_moved = lax.all_to_all(
         spread(send_hot, carried_old.astype(jnp.bfloat16)), "req", split_axis=0, concat_axis=0, tiled=True
     )
-    carried = gather_back(recv_hot, carried_moved).reshape(reqs_dev, NODES, head_width).reshape(reqs_dev, NODES, span_groups, span_heads, HEAD_DIM)
+    carried = gather_back(recv_hot, carried_moved).reshape(reqs_dev, NODES, span_groups, span_heads, HEAD_DIM)
     conv_heads = tree_conv(
         head_rows, tails_new[..., :head_width], new_tree, kernel_heads, shift_heads
     )

time: 173 us -> 172 us (level)
  waiting for transfers between devices: 51.5 us -> 46.8 us
  matrix products: 33.1 us -> 36.2 us
  other arithmetic: 14.3 us -> 16.4 us
    all_to_all x4 -> x0, local copies, waits for them, and re-layouts: 11 us -> none  [the longest x2 7.15 us: shards(): lax.all_to_all(spread(send_hot, carried_old.astype(jnp.bfloat16)), 'req',...]
    all_to_all x1, waiting for transfers between devices: 35.4 us -> 29.6 us  [shards(): lax.all_to_all(spread(send_hot, carried_old.astype(jnp.bfloat16)), 'req',...]
    dot_general x1 -> x0, local copies, waits for them, and re-layouts: 5.53 us -> none  [gather_back(): jnp.einsum('pa,pc->ac', hot, moved, preferred_element_type=jnp.float32)]
    reshape x2 -> x3, local copies, waits for them, and re-layouts: 0.55 us -> 3.9 us  [the longest x1 1.9 us: shards(): gather_back(recv_hot, carried_moved)]
    convert_element_type x0 -> x2, local copies, waits for them, and re-layouts: none -> 3.2 us  [the longest x1 2.51 us: spread(): return jnp.einsum('pa,a...->p...', hot, payload, preferred_element_type=j...]
    unnamed x114 -> x121, local copies, waits for them, and re-layouts: 2.11 us -> 4.92 us
    all_to_all x1, waiting for transfers between devices: 7.72 us -> 10.3 us  [shards(): lax.all_to_all(exchange, 'req', split_axis=0, concat_axis=0, tiled=True)]
    dot_general x1, matrix products: 3.67 us -> 6.26 us  [shards(): jnp.einsum('btjgq,bjgqp->btgqp', mixing, values, preferred_element_type=j...]
  transfers between devices with their start and end apart: 4 -> 4, of which waited for: 4 -> 4; matrix products, arithmetic and copies ran while one was open for 26% -> 30% of each run, Pallas kernels for 0% -> 0%
where the time goes in v5:
time: 172 us; the launch traced here: 170 us
  waiting for transfers between devices  46.8 us (27%)
  local copies, waits for them, and re-layouts  44.6 us (26%)
  matrix products  36.2 us (21%)
  starting transfers between devices  25.5 us (15%)
  other arithmetic  16.4 us (10%)
    all_to_all x1, waiting for transfers between devices, shards(): lax.all_to_all(spread(send_hot, carried_old.astype(jnp.bfloat16)), 'req',...  29.6 us
    all_to_all x1, starting transfers between devices, shards(): lax.all_to_all(exchange, 'req', split_axis=0, concat_axis=0, tiled=True)  12.8 us
    all_to_all x1, waiting for transfers between devices, shards(): lax.all_to_all(exchange, 'req', split_axis=0, concat_axis=0, tiled=True)  10.3 us
    all_to_all x1, starting transfers between devices, shards(): lax.all_to_all(bundle, 'head', split_axis=0, concat_axis=0, tiled=True)  7.72 us
    dot_general x1, matrix products, shards(): jnp.einsum('btjgq,bjgqp->btgqp', mixing, values, preferred_element_type=j...  6.26 us
    dot_general x1, matrix products, shards(): jnp.einsum('bjgqp,bjgn->bgqpn', weighted, key_slice, preferred_element_ty...  5.79 us
    dot_general x9, matrix products, tree_conv(): jnp.einsum('btj,bjc->btc', picked, tree_rows, preferred_element_type=jnp....  5.6 us
    unnamed x121, local copies, waits for them, and re-layouts  4.92 us
  transfers between devices with their start and end apart: 4, of which 4 were waited for; matrix products, arithmetic and copies ran while one was open for 30% of the time, Pallas kernels for 0%

profile of v5, /device:TPU:1, one launch (start us, length us, event | category | flops | bytes accessed | tf_op | source)
XLA Modules:
  0.0 170.5 jit_solution(9409402918112720772)
XLA Ops:
  3.7 2.1 %copy.494 = bf16[2,8,16,1024]{3,2,1,0:T(8,128)(2,1)} copy(bf16[2,8,16,1024]{3,1,2,0:T(8,128)(2,1)} %bitcast.141) | data formatting | bytes 1048576
  6.8 2.4 %concatenate.12 = bf16[16,16,3088]{2,0,1:T(8,128)(2,1)S(1)} concatenate(bf16[16,16,1024]{2,0,1:T(8,128)(2,1)S(1)} %bitcast.135, bf16[16,16,1024]{2,0,1:T(8,128)(2,1)} %bitcast.136, bf16[16,16,16]{2,0,1:T(8,128)(2,1)S(1)} %bitcast.144, bf16[16,16,512]{2,0,1:T(8,128)(2,1)} %get-tuple-element.46, bf16[16,16,512]{2,0,1:T(8,128)(2,1)S(1)} %get-tuple-element.45), dimensions={2} | concatenate | bytes 3162112 | tf_op jit(solution)/shard_map/concatenate | solution.py:180
  10.7 7.7 %all-to-all-start = ((bf16[16,16,3088]{2,1,0:T(8,128)(2,1)}), bf16[16,16,3088]{2,1,0:T(8,128)(2,1)S(1)}, u32[]{:S(2)}, u32[]{:S(2)}) async-start(bf16[16,16,3088]{2,1,0:T(8,128)(2,1)} %copy.412), calls=%async_computation | async-start | bytes 3276800 | tf_op jit(solution)/shard_map/all_to_all | solution.py:183
  35.0 4.8 %all-to-all-done = bf16[16,16,3088]{2,1,0:T(8,128)(2,1)S(1)} async-done(((bf16[16,16,3088]{2,1,0:T(8,128)(2,1)}), bf16[16,16,3088]{2,1,0:T(8,128)(2,1)S(1)}, u32[]{:S(2)}, u32[]{:S(2)}) %all-to-all-start) | async-done | bytes 1581088 | tf_op jit(solution)/shard_map/all_to_all | solution.py:183
  46.2 1.6 copy.425
  47.8 12.8 %all-to-all-start.1 = ((bf16[32,32,432]{2,1,0:T(8,128)(2,1)}), bf16[32,32,432]{2,1,0:T(8,128)(2,1)}, u32[]{:S(2)}, u32[]{:S(2)}) async-start(bf16[32,32,432]{2,1,0:T(8,128)(2,1)} %copy.425), calls=%async_computation.1 | async-start | bytes 2097152 | tf_op jit(solution)/shard_map/all_to_all | solution.py:207
  62.6 1.6 reshape.589
  65.9 1.6 broadcast_multiply_fusion
  69.8 5.8 %fusion = bf16[8,1,16,64,256]{4,3,2,0,1:T(8,128)(2,1)} fusion(bf16[8,16,64,256]{3,2,1,0:T(8,128)(2,1)} %param.35, f32[8,16]{1,0:T(8,128)S(1)} %exp.61, f32[8,32,16,64]{3,2,1,0:T(8,128)S(1)} %reshape.589, f32[8,32,16]{1,2,0:T(8,128)S(1)} %bitcast_multiply_fusion, bf16[8,32,2048]{2,1,0:T(8,128)(2,1)S(1)} %copy-done, s32[]{:T(128)S(6)} %select_n.221), kind=kOutput, calls=%fused_computation.6 | convolution fusion | flops 143130624 | bytes 10686468 | tf_op jit(solution)/shard_map/bjgqp,bjgn->bgqpn/dot_general | solution.py:161
  76.4 1.9 %reshape.591 = f32[8,32,1,16,64]{4,3,1,0,2:T(8,128)} reshape(f32[16,16,1024]{2,1,0:T(8,128)S(1)} %get-tuple-element.11) | data formatting | bytes 2097152 | tf_op jit(solution)/shard_map/convert_element_type | solution.py:266
  78.3 10.3 %all-to-all-done.1 = bf16[32,32,432]{2,1,0:T(8,128)(2,1)} async-done(((bf16[32,32,432]{2,1,0:T(8,128)(2,1)}), bf16[32,32,432]{2,1,0:T(8,128)(2,1)}, u32[]{:S(2)}, u32[]{:S(2)}) %all-to-all-start.1) | async-done | bytes 884768 | tf_op jit(solution)/shard_map/all_to_all | solution.py:207
  94.0 3.5 %convolution_convert_fusion.2 = bf16[8,32,1024]{2,1,0:T(8,128)(2,1)S(1)} fusion(bf16[8,1024,256]{2,1,0:T(8,128)(2,1)} %bitcast.124, bf16[8,32,256]{2,0,1:T(8,128)(2,1)S(1)} %multiply_convert_fusion.5), kind=kOutput, calls=%fused_computation.30 | convolution fusion | flops 134479872 | bytes 4849664 | tf_op jit(solution)/shard_map/btn,bmn->btm/dot_general | solution.py:222
  98.3 2.5 %copy.471 = bf16[32,32,1024]{2,1,0:T(8,128)(2,1)} copy(bf16[32,32,1024]{2,0,1:T(8,128)(2,1)S(1)} %convolution_convert_fusion) | data formatting | bytes 4194304 | tf_op jit(solution)/shard_map/convert_element_type | solution.py:118
  100.9 4.7 %all-to-all-start.2 = ((bf16[32,32,1024]{2,1,0:T(8,128)(2,1)}), bf16[32,32,1024]{2,1,0:T(8,128)(2,1)}, u32[]{:S(2)}, u32[]{:S(2)}) async-start(bf16[32,32,1024]{2,1,0:T(8,128)(2,1)} %copy.471), calls=%async_computation.2 | async-start | bytes 4194304 | tf_op jit(solution)/shard_map/all_to_all | solution.py:228
  113.9 1.8 %reshape.570 = bf16[8,3,1536]{2,1,0:T(4,128)(2,1)} reshape(bf16[8,32,144]{2,1,0:T(8,128)(2,1)} %copy.427) | data formatting | bytes 147456 | tf_op jit(solution)/shard_map/reshape | solution.py:209
  115.7 1.7 %fusion.6 = f32[8,32,1024]{2,1,0:T(8,128)S(1)} fusion(f32[8,32,1024]{2,1,0:T(8,128)} %fusion.59, f32[1024]{0:T(1024)S(1)} %bitcast.152, bf16[8,3,1536]{2,1,0:T(4,128)(2,1)} %reshape.570, s32[8,32]{1,0:T(8,128)S(1)} %get-tuple-element.32), kind=kOutput, calls=%fused_computation.22 | convolution fusion | flops 2097920 | bytes 2167808 | tf_op jit(solution)/shard_map/bti,bic->btc/dot_general | solution.py:29
  118.6 1.9 %reshape.590 = f32[8,32,1,16,64]{4,3,1,0,2:T(8,128)} reshape(bf16[8,32,1024]{2,1,0:T(8,128)(2,1)S(1)} %multiply_convert_fusion.3) | data formatting | bytes 1572864 | tf_op jit(solution)/shard_map/convert_element_type | solution.py:264
  120.6 1.6 reshape.571
  124.0 29.6 %all-to-all-done.2 = bf16[32,32,1024]{2,1,0:T(8,128)(2,1)} async-done(((bf16[32,32,1024]{2,1,0:T(8,128)(2,1)}), bf16[32,32,1024]{2,1,0:T(8,128)(2,1)}, u32[]{:S(2)}, u32[]{:S(2)}) %all-to-all-start.2) | async-done | bytes 2097184 | tf_op jit(solution)/shard_map/all_to_all | solution.py:228
  153.6 3.9 %fusion.3 = f32[8,32,1024]{2,0,1:T(8,128)S(1)} fusion(bf16[32,32,1024]{2,1,0:T(8,128)(2,1)} %all-to-all-done.2, s32[8]{0:T(128)S(1)} %copy-done.40), kind=kOutput, calls=%fused_computation.12 | convolution fusion | flops 16777472 | bytes 3145760 | tf_op jit(solution)/shard_map/pa,p...->a.../dot_general | solution.py:121
  157.5 1.9 %reshape.638 = f32[8,32,1,16,64]{4,3,0,1,2:T(8,128)} reshape(f32[8,32,1024]{2,0,1:T(8,128)S(1)} %fusion.3) | data formatting | bytes 2097152 | tf_op jit(solution)/shard_map/reshape | solution.py:231
  159.4 6.3 %multiply_reduce_fusion = (f32[8,32]{1,0:T(8,128)S(1)}, f32[8,32,1,16,64]{4,1,3,0,2:T(8,128)S(1)}) fusion(f32[8,32,1,16,64]{4,3,1,0,2:T(8,128)} %reshape.591, f32[8,32,1,16,64]{4,3,1,0,2:T(8,128)} %reshape.590, f32[16]{0:T(128)S(1)} %copy-done.56, f32[8,32,1,16,64]{4,3,0,1,2:T(8,128)} %reshape.638, f32[8,32,16]{1,2,0:T(8,128)S(1)} %copy-done.21, ...), kind=kOutput, calls=%fused_computation.17 | convolution fusion | flops 20446976 | bytes 4809792 | tf_op jit(solution)/shard_map/btjgq,bjgqp->btgqp/dot_general | solution.py:258
  166.1 2.1 %collective-permute-done = f32[8,32,1]{1,0,2:T(8,128)S(1)} collective-permute-done((f32[8,32,1]{1,0,2:T(8,128)S(1)}, f32[8,32,1]{1,0,2:T(8,128)S(1)}, u32[]{:S(2)}, u32[]{:S(2)}) %collective-permute-start) | collective-permute-done | bytes 1056 | tf_op jit(solution)/shard_map/ppermute | solution.py:270
  169.0 1.5 convert_element_type.288
  (242 shorter events, 53.7 us)
Async XLA Ops:
  0.0 69.8 %copy-start = (bf16[8,32,2048]{2,1,0:T(8,128)(2,1)S(1)}, bf16[8,32,2048]{2,1,0:T(8,128)(2,1)}, u32[]{:S(2)}) copy-start(bf16[8,32,2048]{2,1,0:T(8,128)(2,1)} %param.37) | copy-start | bytes 3145732
  10.6 7.8 %copy-start.54 = (s32[128]{0:T(128)S(1)}, s32[128]{0:T(128)}, u32[]{:S(2)}) copy-start(s32[128]{0:T(128)} %param.43) | copy-start | bytes 1540
  10.6 8.2 %copy-start.53 = (s32[8]{0:T(128)S(1)}, s32[8]{0:T(128)}, u32[]{:S(2)}) copy-start(s32[8]{0:T(128)} %param.42) | copy-start | bytes 100
  10.6 8.2 %copy-start.12 = (s32[8,32,32]{2,1,0:T(8,128)S(1)}, s32[8,32,32]{2,1,0:T(8,128)}, u32[]{:S(2)}) copy-start(s32[8,32,32]{2,1,0:T(8,128)} %param.41) | copy-start | bytes 98308
  10.6 10.9 %copy-start.4 = (s32[8,32,32]{2,1,0:T(8,128)S(1)}, s32[8,32,32]{2,1,0:T(8,128)}, u32[]{:S(2)}) copy-start(s32[8,32,32]{2,1,0:T(8,128)} %param.26) | copy-start | bytes 98308
  10.6 13.0 %copy-start.24 = (bf16[4,4096]{1,0:T(4,128)(2,1)S(1)}, bf16[4,4096]{1,0:T(4,128)(2,1)}, u32[]{:S(2)}) copy-start(bf16[4,4096]{1,0:T(4,128)(2,1)} %param.29) | copy-start | bytes 98308
  10.6 20.7 %copy-start.26 = (bf16[4,1024]{1,0:T(4,128)(2,1)S(1)}, bf16[4,1024]{1,0:T(4,128)(2,1)}, u32[]{:S(2)}) copy-start(bf16[4,1024]{1,0:T(4,128)(2,1)} %param.27) | copy-start | bytes 24580
  10.6 22.9 %copy-start.9 = (bf16[8,32,1024]{2,1,0:T(8,128)(2,1)S(1)}, bf16[8,32,1024]{2,1,0:T(8,128)(2,1)}, u32[]{:S(2)}) copy-start(bf16[8,32,1024]{2,1,0:T(8,128)(2,1)} %param.39) | copy-start | bytes 1572868
  10.7 29.1 %all-to-all-start = ((bf16[16,16,3088]{2,1,0:T(8,128)(2,1)}), bf16[16,16,3088]{2,1,0:T(8,128)(2,1)S(1)}, u32[]{:S(2)}, u32[]{:S(2)}) async-start(bf16[16,16,3088]{2,1,0:T(8,128)(2,1)} %copy.412), calls=%async_computation | async-start | bytes 3276800 | tf_op jit(solution)/shard_map/all_to_all | solution.py:183
  24.5 19.6 %copy-start.27 = (pred[8,32]{1,0:T(8,128)(4,1)S(1)}, pred[8,32]{1,0:T(8,128)(4,1)}, u32[]{:S(2)}) copy-start(pred[8,32]{1,0:T(8,128)(4,1)} %broadcast_compare_fusion) | copy-start | bytes 772
  35.0 9.3 %copy-start.19 = (bf16[8,3,1024]{2,1,0:T(4,128)(2,1)S(1)}, bf16[8,3,1024]{2,1,0:T(4,128)(2,1)}, u32[]{:S(2)}) copy-start(bf16[8,3,1024]{2,1,0:T(4,128)(2,1)} %convolution_convert_fusion.6) | copy-start | bytes 147460
  35.0 9.7 %copy-start.35 = (s32[8]{0:T(128)S(1)}, s32[8]{0:T(128)}, u32[]{:S(2)}) copy-start(s32[8]{0:T(128)} %dynamic-slice_reduce_fusion) | copy-start | bytes 100
  35.0 10.2 %copy-start.18 = (bf16[8,32,32]{2,0,1:T(8,128)(2,1)S(1)}, bf16[8,32,32]{2,0,1:T(8,128)(2,1)}, u32[]{:S(2)}) copy-start(bf16[8,32,32]{2,0,1:T(8,128)(2,1)} %copy_convert_fusion) | copy-start | bytes 49156
  35.0 10.2 %copy-start.39 = (s32[8]{0:T(128)S(1)}, s32[8]{0:T(128)}, u32[]{:S(2)}) copy-start(s32[8]{0:T(128)} %fusion.116) | copy-start | bytes 100
  46.1 15.8 %copy-start.16 = (pred[8,32,32]{2,0,1:T(8,128)(4,1)S(1)}, pred[8,32,32]{2,0,1:T(8,128)(4,1)}, u32[]{:S(2)}) copy-start(pred[8,32,32]{2,0,1:T(8,128)(4,1)} %copy-done.15) | copy-start | bytes 24580
  47.8 16.5 %slice-start = ((bf16[16,16,3088]{2,1,0:T(8,128)(2,1)}), bf16[16,16,16]{2,1,0:T(8,128)(2,1)S(1)}, s32[]{:S(2)}) async-start(bf16[16,16,3088]{2,1,0:T(8,128)(2,1)} %copy-done.1), calls=%async_computation.3 | async-start | bytes 131072 | tf_op jit(solution)/shard_map/slice | solution.py:187
  47.8 40.9 %all-to-all-start.1 = ((bf16[32,32,432]{2,1,0:T(8,128)(2,1)}), bf16[32,32,432]{2,1,0:T(8,128)(2,1)}, u32[]{:S(2)}, u32[]{:S(2)}) async-start(bf16[32,32,432]{2,1,0:T(8,128)(2,1)} %copy.425), calls=%async_computation.1 | async-start | bytes 2097152 | tf_op jit(solution)/shard_map/all_to_all | solution.py:207
  60.5 8.3 %copy-start.28 = (pred[8,32]{1,0:T(8,128)(4,1)S(1)}, pred[8,32]{1,0:T(8,128)(4,1)}, u32[]{:S(2)}) copy-start(pred[8,32]{1,0:T(8,128)(4,1)} %broadcast_compare_fusion) | copy-start | bytes 772
  61.9 13.6 %copy-start.37 = (f32[1,512]{1,0:T(1,128)}, f32[1,512]{1,0:T(1,128)S(1)}, u32[]{:S(2)}) copy-start(f32[1,512]{1,0:T(1,128)S(1)} %broadcast_select_fusion.3) | copy-start | bytes 6148
  76.4 13.8 %copy-start.36 = (s32[8]{0:T(128)S(1)}, s32[8]{0:T(128)}, u32[]{:S(2)}) copy-start(s32[8]{0:T(128)} %dynamic-slice_reduce_fusion) | copy-start | bytes 100
  100.9 6.7 %copy-start.13 = (pred[8,32,32]{2,0,1:T(8,128)(4,1)S(1)}, pred[8,32,32]{2,0,1:T(8,128)(4,1)}, u32[]{:S(2)}) copy-start(pred[8,32,32]{2,0,1:T(8,128)(4,1)} %get-tuple-element.18) | copy-start | bytes 24580
  100.9 52.7 %all-to-all-start.2 = ((bf16[32,32,1024]{2,1,0:T(8,128)(2,1)}), bf16[32,32,1024]{2,1,0:T(8,128)(2,1)}, u32[]{:S(2)}, u32[]{:S(2)}) async-start(bf16[32,32,1024]{2,1,0:T(8,128)(2,1)} %copy.471), calls=%async_computation.2 | async-start | bytes 4194304 | tf_op jit(solution)/shard_map/all_to_all | solution.py:228
  159.4 6.6 %copy-start.46 = (f32[1024]{0:T(1024)S(1)}, f32[1024]{0:T(1024)}, u32[]{:S(2)}) copy-start(f32[1024]{0:T(1024)} %param.34) | copy-start | bytes 12292
  165.7 2.5 %collective-permute-start = (f32[8,32,1]{1,0,2:T(8,128)S(1)}, f32[8,32,1]{1,0,2:T(8,128)S(1)}, u32[]{:S(2)}, u32[]{:S(2)}) collective-permute-start(f32[8,32,1]{1,0,2:T(8,128)S(1)} %bitcast.162), channel_id=1, source_target_pairs={{0,1},{1,0},{2,3},{3,2},{4,5},{5,4},{6,7},{7,6},{8,9},{9,8},{10,11... | collective-permute-start | bytes 3080 | tf_op jit(solution)/shard_map/ppermute | solution.py:270
  (39 other events, 121.2 us)

commit v6 on v5

--- a/solution.py
+++ b/solution.py
@@ -195,20 +195,17 @@
     tail_groups = jnp.einsum(
         "bij,bjc->bic", tail_pick, prior_own, preferred_element_type=jnp.float32
     ).astype(jnp.bfloat16)
-    new_part = jnp.concatenate([tail_heads, tail_groups], axis=-1).reshape(reqs_dev, NODES, -1)
+    tails_all = lax.all_gather(
+        jnp.concatenate([tail_heads, tail_groups], axis=-1), "req", axis=0, tiled=True
+    )
+    tails_new = jnp.take(tails_all, anchor, axis=0)
     old_part = jnp.concatenate(
         [group_rows[..., own_width:], new_tree.astype(jnp.bfloat16)], axis=-1
     )
-    new_len = new_part.shape[-1]
-    exchange = jnp.concatenate(
-        [spread(send_hot, new_part), spread(recv_hot, old_part)],
-        axis=-1,
-    )
-    exchange = lax.all_to_all(exchange, "req", split_axis=0, concat_axis=0, tiled=True)
-    tails_new = (
-        gather_back(recv_hot, exchange[..., :new_len]).astype(jnp.bfloat16).reshape(reqs_dev, 3, -1)
-    )
-    rows_old = gather_back(send_hot, exchange[..., new_len:]).astype(jnp.bfloat16)
+    exchange = lax.all_to_all(
+        spread(recv_hot, old_part), "req", split_axis=0, concat_axis=0, tiled=True
+    )
+    rows_old = gather_back(send_hot, exchange).astype(jnp.bfloat16)
     tree_old = rows_old[..., own_width:].astype(jnp.int32)
     kernel_own = own_columns(kernel_groups, span_groups, head_count, per_dest)[head_index]
     shift_own = own_columns(shift_groups, span_groups, head_count, per_dest)[head_index]

time: 172 us -> 184 us (1.070)
  between operations: 1.08 us -> 14.4 us
  waiting for transfers between devices: 46.8 us -> 37.9 us
  other arithmetic: 16.4 us -> 21.3 us
  matrix products: 36.2 us -> 38.2 us
    all_to_all x1, waiting for transfers between devices: 4.75 us -> 0.01 us  [shards(): lax.all_to_all(bundle, 'head', split_axis=0, concat_axis=0, tiled=True)]
    unnamed x121 -> x106, local copies, waits for them, and re-layouts: 4.92 us -> 0.86 us
    all_gather x0 -> x1, local copies, waits for them, and re-layouts: none -> 3.48 us  [shards(): lax.all_gather(jnp.concatenate([tail_heads, tail_groups], axis=-1), 'req'...]
    gather x0 -> x1, local copies, waits for them, and re-layouts: none -> 2.8 us  [shards(): tails_new = jnp.take(tails_all, anchor, axis=0)]
    slice x2 -> x0, local copies, waits for them, and re-layouts: 2.58 us -> none  [the longest x1 1.5 us: shards(): exchange[..., new_len:]]
    reshape x2 -> x0, local copies, waits for them, and re-layouts: 2 us -> none  [the longest x1 1.77 us: shards(): gather_back(recv_hot, exchange[..., :new_len]).astype(jnp.bfloat16)]
    all_to_all x1, waiting for transfers between devices: 10.3 us -> 8.36 us  [shards(): lax.all_to_all(spread(recv_hot, old_part), 'req', split_axis=0, concat_ax...]
    concatenate x2 -> x1, local copies, waits for them, and re-layouts: 3.84 us -> 2.08 us  [shards(): jnp.concatenate([split_heads, split_gates, split_steps, split_groups, spl...]
  transfers between devices with their start and end apart: 4 -> 5, of which waited for: 4 -> 3; matrix products, arithmetic and copies ran while one was open for 30% -> 40% of each run, Pallas kernels for 0% -> 0%
where the time goes in v6:
time: 184 us; the launch traced here: 183 us
  local copies, waits for them, and re-layouts  45.9 us (25%)
  matrix products  38.2 us (21%)
  waiting for transfers between devices  37.9 us (21%)
  starting transfers between devices  25.4 us (14%)
  other arithmetic  21.3 us (12%)
  between operations  14.4 us (8%)
    all_to_all x1, waiting for transfers between devices, shards(): lax.all_to_all(spread(send_hot, carried_old.astype(jnp.bfloat16)), 'req',...  27.9 us
    all_to_all x1, starting transfers between devices, shards(): lax.all_to_all(spread(recv_hot, old_part), 'req', split_axis=0, concat_ax...  12.2 us
    all_to_all x1, waiting for transfers between devices, shards(): lax.all_to_all(spread(recv_hot, old_part), 'req', split_axis=0, concat_ax...  8.36 us
    all_to_all x1, starting transfers between devices, shards(): lax.all_to_all(bundle, 'head', split_axis=0, concat_axis=0, tiled=True)  7.76 us
    dot_general x1, matrix products, shards(): jnp.einsum('btjgq,bjgqp->btgqp', mixing, values, preferred_element_type=j...  6.26 us
    dot_general x1, matrix products, shards(): jnp.einsum('bjgqp,bjgn->bgqpn', weighted, key_slice, preferred_element_ty...  5.66 us
    dot_general x9, matrix products, tree_conv(): jnp.einsum('btj,bjc->btc', picked, tree_rows, preferred_element_type=jnp....  5.55 us
    dot_general x2, matrix products, gather_back(): jnp.einsum('pa,p...->a...', hot, moved, preferred_element_type=jnp.float32)  5.36 us
  transfers between devices with their start and end apart: 5, of which 3 were waited for; matrix products, arithmetic and copies ran while one was open for 40% of the time, Pallas kernels for 0%

profile of v6, /device:TPU:1, one launch (start us, length us, event | category | flops | bytes accessed | tf_op | source)
XLA Modules:
  0.0 183.2 jit_solution(1869094349857233025)
XLA Ops:
  10.9 2.1 %concatenate.9 = bf16[16,16,3088]{2,1,0:T(8,128)(2,1)} concatenate(bf16[16,16,1024]{2,1,0:T(8,128)(2,1)S(1)} %get-tuple-element.56, bf16[16,16,1024]{2,1,0:T(8,128)(2,1)S(1)} %get-tuple-element.55, bf16[16,16,16]{2,1,0:T(8,128)(2,1)S(1)} %bitcast.143, bf16[16,16,512]{2,1,0:T(8,128)(2,1)S(1)} %get-tuple-element.48, bf16[16,16,512]{2,1,0:T(8,128)(2,1)S(1)} %get-tuple-element.47), dimensions={2} | concatenate | bytes 3162112 | tf_op jit(solution)/shard_map/concatenate | solution.py:180
  13.0 7.8 %all-to-all-start = ((bf16[16,16,3088]{2,1,0:T(8,128)(2,1)}), bf16[16,16,3088]{2,1,0:T(8,128)(2,1)}, u32[]{:S(2)}, u32[]{:S(2)}) async-start(bf16[16,16,3088]{2,1,0:T(8,128)(2,1)} %concatenate.9), calls=%async_computation | async-start | bytes 3276800 | tf_op jit(solution)/shard_map/all_to_all | solution.py:183
  31.2 1.6 reshape.581
  40.8 1.9 %convolution_convert_fusion.4 = bf16[8,3,1024]{2,1,0:T(4,128)(2,1)} fusion(bf16[8,32,1024]{2,1,0:T(8,128)(2,1)} %param.39, s32[8,3]{1,0:T(8,128)S(1)} %iota_add_fusion, s32[8,32]{1,0:T(8,128)S(1)} %get-tuple-element.44, pred[8,32]{1,0:T(8,128)(4,1)S(1)} %broadcast_compare_fusion), kind=kOutput, calls=%fused_computation.43 | convolution fusion | flops 1598976 | bytes 574816 | tf_op jit(solution)/shard_map/bij,bjc->bic/dot_general | solution.py:135
  42.7 2.0 %fusion.111 = (bf16[16,16,512]{2,1,0:T(8,128)(2,1)S(1)}, bf16[16,16,512]{2,1,0:T(8,128)(2,1)}) fusion(bf16[16,16,3088]{2,1,0:T(8,128)(2,1)} %all-to-all-done), kind=kLoop, calls=%fused_computation.245 | loop fusion | bytes 1048576 | tf_op jit(solution)/shard_map/slice | solution.py:187
  44.7 1.8 reshape.558
  46.5 1.8 %copy.629 = bf16[16,8,2,512]{3,2,0,1:T(2,128)(2,1)} copy(bf16[16,8,2,512]{3,2,1,0:T(2,128)(2,1)} %reshape.558) | data formatting | bytes 524288 | tf_op jit(solution)/shard_map/reshape | solution.py:193
  48.3 1.8 reshape.559
  56.6 12.2 %all-to-all-start.1 = ((bf16[32,32,288]{2,1,0:T(8,128)(2,1)}), bf16[32,32,288]{2,1,0:T(8,128)(2,1)}, u32[]{:S(2)}, u32[]{:S(2)}) async-start(bf16[32,32,288]{2,1,0:T(8,128)(2,1)} %copy.476), calls=%async_computation.1 | async-start | bytes 1572864 | tf_op jit(solution)/shard_map/all_to_all | solution.py:205
  75.9 5.7 %fusion = bf16[8,1,16,64,256]{4,3,2,0,1:T(8,128)(2,1)} fusion(bf16[8,16,64,256]{3,2,1,0:T(8,128)(2,1)} %param.35, f32[8,16]{1,0:T(8,128)S(1)} %exp.61, f32[8,32,16,64]{3,2,1,0:T(8,128)S(1)} %reshape.581, f32[8,32,16]{1,2,0:T(8,128)S(1)} %bitcast_multiply_fusion, bf16[8,32,2048]{2,1,0:T(8,128)(2,1)S(1)} %copy-done, s32[]{:T(128)S(6)} %select_n.228), kind=kOutput, calls=%fused_computation.7 | convolution fusion | flops 143130624 | bytes 10686468 | tf_op jit(solution)/shard_map/bjgqp,bjgn->bgqpn/dot_general | solution.py:161
  83.5 1.9 %reshape.583 = f32[8,32,1,16,64]{4,3,1,0,2:T(8,128)} reshape(f32[16,16,1024]{2,1,0:T(8,128)S(1)} %get-tuple-element.11) | data formatting | bytes 2097152 | tf_op jit(solution)/shard_map/convert_element_type | solution.py:263
  86.4 8.4 %all-to-all-done.1 = bf16[32,32,288]{2,1,0:T(8,128)(2,1)} async-done(((bf16[32,32,288]{2,1,0:T(8,128)(2,1)}), bf16[32,32,288]{2,1,0:T(8,128)(2,1)}, u32[]{:S(2)}, u32[]{:S(2)}) %all-to-all-start.1) | async-done | bytes 589856 | tf_op jit(solution)/shard_map/all_to_all | solution.py:205
  99.7 3.5 %convolution_convert_fusion.2 = bf16[8,32,1024]{2,1,0:T(8,128)(2,1)S(1)} fusion(bf16[8,1024,256]{2,1,0:T(8,128)(2,1)} %bitcast.124, bf16[8,32,256]{2,0,1:T(8,128)(2,1)S(1)} %multiply_convert_fusion.5), kind=kOutput, calls=%fused_computation.31 | convolution fusion | flops 134479872 | bytes 4849664 | tf_op jit(solution)/shard_map/btn,bmn->btm/dot_general | solution.py:219
  104.1 2.5 %copy.504 = bf16[32,32,1024]{2,1,0:T(8,128)(2,1)} copy(bf16[32,32,1024]{2,0,1:T(8,128)(2,1)S(1)} %convolution_convert_fusion) | data formatting | bytes 4194304 | tf_op jit(solution)/shard_map/convert_element_type | solution.py:118
  106.6 4.7 %all-to-all-start.2 = ((bf16[32,32,1024]{2,1,0:T(8,128)(2,1)}), bf16[32,32,1024]{2,1,0:T(8,128)(2,1)}, u32[]{:S(2)}, u32[]{:S(2)}) async-start(bf16[32,32,1024]{2,1,0:T(8,128)(2,1)} %copy.504), calls=%async_computation.2 | async-start | bytes 4194304 | tf_op jit(solution)/shard_map/all_to_all | solution.py:225
  116.4 3.5 %copy.453 = bf16[128,3,1536]{2,1,0:T(4,128)(2,1)} copy(bf16[128,3,1536]{2,0,1:T(8,128)(2,1)} %all-gather.2.cloned.1.call-done) | data formatting | bytes 2359296 | tf_op jit(solution)/shard_map/all_gather | solution.py:198
  119.9 2.8 %gather_fusion.2 = bf16[8,3,1536]{2,1,0:T(4,128)(2,1)} fusion(bf16[128,3,1536]{2,1,0:T(4,128)(2,1)} %copy.453, s32[1024]{0:T(1024)} %copy-done.29), kind=kCustom, calls=%fused_computation.2 | custom fusion | bytes 147488 | tf_op jit(solution)/shard_map/jit(_take)/gather | solution.py:201
  123.7 1.7 fusion.6
  126.6 2.0 %reshape.582 = f32[8,32,1,16,64]{4,3,1,0,2:T(8,128)} reshape(bf16[8,32,1024]{2,1,0:T(8,128)(2,1)S(1)} %multiply_convert_fusion.3) | data formatting | bytes 1572864 | tf_op jit(solution)/shard_map/convert_element_type | solution.py:261
  131.5 27.9 %all-to-all-done.2 = bf16[32,32,1024]{2,1,0:T(8,128)(2,1)} async-done(((bf16[32,32,1024]{2,1,0:T(8,128)(2,1)}), bf16[32,32,1024]{2,1,0:T(8,128)(2,1)}, u32[]{:S(2)}, u32[]{:S(2)}) %all-to-all-start.2) | async-done | bytes 2097184 | tf_op jit(solution)/shard_map/all_to_all | solution.py:225
  159.4 3.9 %fusion.3 = f32[8,32,1024]{2,0,1:T(8,128)S(1)} fusion(bf16[32,32,1024]{2,1,0:T(8,128)(2,1)} %all-to-all-done.2, s32[8]{0:T(128)S(1)} %copy-done.45), kind=kOutput, calls=%fused_computation.13 | convolution fusion | flops 16777472 | bytes 3145760 | tf_op jit(solution)/shard_map/pa,p...->a.../dot_general | solution.py:121
  163.3 1.9 %reshape.636 = f32[8,32,1,16,64]{4,3,0,1,2:T(8,128)} reshape(f32[8,32,1024]{2,0,1:T(8,128)S(1)} %fusion.3) | data formatting | bytes 2097152 | tf_op jit(solution)/shard_map/reshape | solution.py:228
  165.3 6.3 %multiply_reduce_fusion = (f32[8,32]{1,0:T(8,128)S(1)}, f32[8,32,1,16,64]{4,1,3,0,2:T(8,128)S(1)}) fusion(f32[8,32,1,16,64]{4,3,1,0,2:T(8,128)} %reshape.583, f32[8,32,1,16,64]{4,3,1,0,2:T(8,128)} %reshape.582, f32[16]{0:T(128)S(1)} %copy-done.50, f32[8,32,1,16,64]{4,3,0,1,2:T(8,128)} %reshape.636, f32[8,32,16]{1,2,0:T(8,128)S(1)} %copy-done.14, ...), kind=kOutput, calls=%fused_computation.18 | convolution fusion | flops 20446976 | bytes 4809792 | tf_op jit(solution)/shard_map/btjgq,bjgqp->btgqp/dot_general | solution.py:255
  172.4 1.7 collective-permute-done
  (226 shorter events, 57.8 us)
Async XLA Ops:
  6.5 69.3 %copy-start = (bf16[8,32,2048]{2,1,0:T(8,128)(2,1)S(1)}, bf16[8,32,2048]{2,1,0:T(8,128)(2,1)}, u32[]{:S(2)}) copy-start(bf16[8,32,2048]{2,1,0:T(8,128)(2,1)} %param.37) | copy-start | bytes 3145732
  13.0 9.5 %copy-start.2 = (s32[8,32,32]{2,1,0:T(8,128)S(1)}, s32[8,32,32]{2,1,0:T(8,128)}, u32[]{:S(2)}) copy-start(s32[8,32,32]{2,1,0:T(8,128)} %param.26) | copy-start | bytes 98308
  13.0 12.3 %copy-start.48 = (s32[8]{0:T(128)S(1)}, s32[8]{0:T(128)}, u32[]{:S(2)}) copy-start(s32[8]{0:T(128)} %param.42) | copy-start | bytes 100
  13.0 12.4 %copy-start.5 = (s32[8,32,32]{2,1,0:T(8,128)S(1)}, s32[8,32,32]{2,1,0:T(8,128)}, u32[]{:S(2)}) copy-start(s32[8,32,32]{2,1,0:T(8,128)} %param.41) | copy-start | bytes 98308
  13.0 14.0 %copy-start.18 = (bf16[4,4096]{1,0:T(4,128)(2,1)S(1)}, bf16[4,4096]{1,0:T(4,128)(2,1)}, u32[]{:S(2)}) copy-start(bf16[4,4096]{1,0:T(4,128)(2,1)} %param.29) | copy-start | bytes 98308
  13.0 14.8 %copy-start.25 = (f32[4096]{0:T(1024)S(1)}, f32[4096]{0:T(1024)}, u32[]{:S(2)}) copy-start(f32[4096]{0:T(1024)} %param.30) | copy-start | bytes 49156
  13.0 29.7 %all-to-all-start = ((bf16[16,16,3088]{2,1,0:T(8,128)(2,1)}), bf16[16,16,3088]{2,1,0:T(8,128)(2,1)}, u32[]{:S(2)}, u32[]{:S(2)}) async-start(bf16[16,16,3088]{2,1,0:T(8,128)(2,1)} %concatenate.9), calls=%async_computation | async-start | bytes 3276800 | tf_op jit(solution)/shard_map/all_to_all | solution.py:183
  20.8 95.6 %all-gather.2.cloned.1.call-start = ((), (), s32[]{:S(2)}) async-start(), calls=%async_computation.3 | async-start | bytes 1253376 | tf_op jit(solution)/shard_map/all_gather | solution.py:198
  27.0 11.6 %copy-start.20 = (bf16[4,1024]{1,0:T(4,128)(2,1)S(1)}, bf16[4,1024]{1,0:T(4,128)(2,1)}, u32[]{:S(2)}) copy-start(bf16[4,1024]{1,0:T(4,128)(2,1)} %param.27) | copy-start | bytes 24580
  29.9 12.8 %copy-start.30 = (f32[1,512]{1,0:T(1,128)}, f32[1,512]{1,0:T(1,128)S(1)}, u32[]{:S(2)}) copy-start(f32[1,512]{1,0:T(1,128)S(1)} %broadcast_select_fusion.4) | copy-start | bytes 6148
  55.4 18.2 %copy-start.34 = (pred[8,32]{1,0:T(8,128)(4,1)S(1)}, pred[8,32]{1,0:T(8,128)(4,1)}, u32[]{:S(2)}) copy-start(pred[8,32]{1,0:T(8,128)(4,1)} %copy-done.33) | copy-start | bytes 772
  55.4 19.5 %copy-start.22 = (pred[8,32]{1,0:T(8,128)(4,1)S(1)}, pred[8,32]{1,0:T(8,128)(4,1)}, u32[]{:S(2)}) copy-start(pred[8,32]{1,0:T(8,128)(4,1)} %copy-done.21) | copy-start | bytes 772
  56.6 38.2 %all-to-all-start.1 = ((bf16[32,32,288]{2,1,0:T(8,128)(2,1)}), bf16[32,32,288]{2,1,0:T(8,128)(2,1)}, u32[]{:S(2)}, u32[]{:S(2)}) async-start(bf16[32,32,288]{2,1,0:T(8,128)(2,1)} %copy.476), calls=%async_computation.1 | async-start | bytes 1572864 | tf_op jit(solution)/shard_map/all_to_all | solution.py:205
  83.5 11.3 %copy-start.32 = (s32[8]{0:T(128)S(1)}, s32[8]{0:T(128)}, u32[]{:S(2)}) copy-start(s32[8]{0:T(128)} %dynamic-slice_reduce_fusion) | copy-start | bytes 100
  83.5 13.5 %copy-start.8 = (bf16[8,3,512]{2,1,0:T(4,128)(2,1)S(1)}, bf16[8,3,512]{2,1,0:T(4,128)(2,1)}, u32[]{:S(2)}) copy-start(bf16[8,3,512]{2,1,0:T(4,128)(2,1)} %copy-done.7) | copy-start | bytes 73732
  85.4 13.2 %slice-start = ((f32[1,512]{1,0:T(1,128)}), f32[1,256]{1,0:T(1,128)S(1)}, s32[]{:S(2)}) async-start(f32[1,512]{1,0:T(1,128)} %copy-done.30), calls=%async_computation.4 | async-start | bytes 2048 | tf_op jit(solution)/shard_map/slice | solution.py:217
  85.4 13.2 %copy-start.35 = (f32[1,256]{1,0:T(1,128)S(1)}, f32[1,256]{1,0:T(1,128)}, u32[]{:S(2)}) copy-start(f32[1,256]{1,0:T(1,128)} %get-tuple-element.35) | copy-start | bytes 3076
  85.4 13.2 %copy-start.36 = (f32[1,256]{1,0:T(1,128)S(1)}, f32[1,256]{1,0:T(1,128)}, u32[]{:S(2)}) copy-start(f32[1,256]{1,0:T(1,128)} %get-tuple-element.36) | copy-start | bytes 3076
  85.5 13.2 %copy-start.37 = (f32[1,256]{1,0:T(1,128)S(1)}, f32[1,256]{1,0:T(1,128)}, u32[]{:S(2)}) copy-start(f32[1,256]{1,0:T(1,128)} %get-tuple-element.37) | copy-start | bytes 3076
  85.5 13.2 %copy-start.38 = (f32[1,256]{1,0:T(1,128)S(1)}, f32[1,256]{1,0:T(1,128)}, u32[]{:S(2)}) copy-start(f32[1,256]{1,0:T(1,128)} %get-tuple-element.38) | copy-start | bytes 3076
  106.6 52.8 %all-to-all-start.2 = ((bf16[32,32,1024]{2,1,0:T(8,128)(2,1)}), bf16[32,32,1024]{2,1,0:T(8,128)(2,1)}, u32[]{:S(2)}, u32[]{:S(2)}) async-start(bf16[32,32,1024]{2,1,0:T(8,128)(2,1)} %copy.504), calls=%async_computation.2 | async-start | bytes 4194304 | tf_op jit(solution)/shard_map/all_to_all | solution.py:225
  116.4 9.0 %copy-start.23 = (f32[1,1024]{1,0:T(1,128)S(1)}, f32[1,1024]{1,0:T(1,128)}, u32[]{:S(2)}) copy-start(f32[1,1024]{1,0:T(1,128)} %get-tuple-element.29) | copy-start | bytes 12292
  130.8 28.6 %copy-start.45 = (s32[8]{0:T(128)S(1)}, s32[8]{0:T(128)}, u32[]{:S(2)}) copy-start(s32[8]{0:T(128)} %select_add_fusion) | copy-start | bytes 100
  171.5 2.5 %collective-permute-start = (f32[8,32,1]{1,0,2:T(8,128)S(1)}, f32[8,32,1]{1,0,2:T(8,128)S(1)}, u32[]{:S(2)}, u32[]{:S(2)}) collective-permute-start(f32[8,32,1]{1,0,2:T(8,128)S(1)} %bitcast.162), channel_id=1, source_target_pairs={{0,1},{1,0},{2,3},{3,2},{4,5},{5,4},{6,7},{7,6},{8,9},{9,8},{10,11... | collective-permute-start | bytes 3080 | tf_op jit(solution)/shard_map/ppermute | solution.py:267
  (33 other events, 115.5 us)
Sparse Core Ops, SparseCore 0:
  53.5 47.3 all-gather.1

commit v7 on v5

--- a/solution.py
+++ b/solution.py
@@ -176,25 +176,30 @@
     split_prior = own_columns(prior_groups, span_groups, head_count, per_dest).reshape(
         head_count, reqs_dev * local_nodes, 2 * own_width
     )
-    widths = [head_width, head_width, local_heads, 2 * own_width, 2 * own_width]
+    widths = [2 * own_width, 2 * own_width, head_width, head_width, local_heads]
     bundle = jnp.concatenate(
-        [split_heads, split_gates, split_steps, split_groups, split_prior.astype(jnp.bfloat16)], axis=-1
+        [split_groups, split_prior.astype(jnp.bfloat16), split_heads, split_gates, split_steps], axis=-1
     )
     bundle = lax.all_to_all(bundle, "head", split_axis=0, concat_axis=0, tiled=True)
     cuts = [0]
     for width in widths:
         cuts.append(cuts[-1] + width)
     pieces = [bundle[..., cuts[n] : cuts[n + 1]] for n in range(len(widths))]
-    head_rows = pieces[0].reshape(reqs_dev, NODES, head_width)
-    gate_rows = pieces[1].reshape(reqs_dev, NODES, span_groups, span_heads, HEAD_DIM)
-    step_rows = pieces[2].reshape(reqs_dev, NODES, local_heads)
-    group_rows = pieces[3].reshape(reqs_dev, NODES, 2 * own_width)
-    prior_own = jnp.moveaxis(
-        pieces[4].reshape(head_count, reqs_dev, local_nodes, 2 * own_width), 0, 1
-    ).reshape(reqs_dev, NODES, 2 * own_width)
-    tail_groups = jnp.einsum(
-        "bij,bjc->bic", tail_pick, prior_own, preferred_element_type=jnp.float32
-    ).astype(jnp.bfloat16)
+    group_rows = pieces[0].reshape(reqs_dev, NODES, 2 * own_width)
+    prior_flat = pieces[1].reshape(head_count * reqs_dev * local_nodes, 2 * own_width)
+    head_rows = pieces[2].reshape(reqs_dev, NODES, head_width)
+    gate_rows = pieces[3].reshape(reqs_dev, NODES, span_groups, span_heads, HEAD_DIM)
+    step_rows = pieces[4].reshape(reqs_dev, NODES, local_heads)
+    pick_split = tail_pick.reshape(reqs_dev, 3, head_count, local_nodes)
+    same_slot = (local_ids[:, None] == local_ids[None, :]).astype(jnp.bfloat16)
+    pick_rows = (
+        pick_split[:, :, :, None, :] * same_slot[:, None, None, :, None]
+    ).reshape(reqs_dev * 3, head_count * reqs_dev * local_nodes)
+    tail_groups = (
+        jnp.dot(pick_rows, prior_flat, preferred_element_type=jnp.float32)
+        .astype(jnp.bfloat16)
+        .reshape(reqs_dev, 3, 2 * own_width)
+    )
     new_part = jnp.concatenate([tail_heads, tail_groups], axis=-1).reshape(reqs_dev, NODES, -1)
     old_part = jnp.concatenate(
         [group_rows[..., own_width:], new_tree.astype(jnp.bfloat16)], axis=-1

time: 172 us -> 168 us (0.977)
  local copies, waits for them, and re-layouts: 44.6 us -> 38.2 us
  waiting for transfers between devices: 46.8 us -> 50.5 us
    all_to_all x1, waiting for transfers between devices: 4.75 us -> 8.41 us  [shards(): lax.all_to_all(bundle, 'head', split_axis=0, concat_axis=0, tiled=True)]
    reshape x3 -> x1, local copies, waits for them, and re-layouts: 3.01 us -> 0.03 us  [shards(): tail_groups = jnp.dot(pick_rows, prior_flat, preferred_element_type=jnp.f...]
    concatenate x2, local copies, waits for them, and re-layouts: 3.84 us -> 1.49 us  [shards(): jnp.concatenate([split_groups, split_prior.astype(jnp.bfloat16), split_he...]
    unnamed x121 -> x119, local copies, waits for them, and re-layouts: 4.92 us -> 6.26 us
    gather x10 -> x9, local copies, waits for them, and re-layouts: 3.51 us -> 2.86 us  [own_columns(): jnp.take(moved, picks.reshape(-1), axis=0)]
  transfers between devices with their start and end apart: 4 -> 4, of which waited for: 4 -> 4; matrix products, arithmetic and copies ran while one was open for 30% -> 29% of each run, Pallas kernels for 0% -> 0%
where the time goes in v7:
time: 168 us; the launch traced here: 167 us
  waiting for transfers between devices  50.5 us (30%)
  local copies, waits for them, and re-layouts  38.2 us (23%)
  matrix products  35.9 us (21%)
  starting transfers between devices  25.6 us (15%)
  other arithmetic  15.3 us (9%)
    all_to_all x1, waiting for transfers between devices, shards(): lax.all_to_all(spread(send_hot, carried_old.astype(jnp.bfloat16)), 'req',...  29.6 us
    all_to_all x1, starting transfers between devices, shards(): lax.all_to_all(exchange, 'req', split_axis=0, concat_axis=0, tiled=True)  12.8 us
    all_to_all x1, waiting for transfers between devices, shards(): lax.all_to_all(exchange, 'req', split_axis=0, concat_axis=0, tiled=True)  10.4 us
    all_to_all x1, waiting for transfers between devices, shards(): lax.all_to_all(bundle, 'head', split_axis=0, concat_axis=0, tiled=True)  8.41 us
    all_to_all x1, starting transfers between devices, shards(): lax.all_to_all(bundle, 'head', split_axis=0, concat_axis=0, tiled=True)  7.72 us
    unnamed x119, local copies, waits for them, and re-layouts  6.26 us
    dot_general x1, matrix products, shards(): jnp.einsum('btjgq,bjgqp->btgqp', mixing, values, preferred_element_type=j...  6.26 us
    dot_general x1, matrix products, shards(): jnp.einsum('bjgqp,bjgn->bgqpn', weighted, key_slice, preferred_element_ty...  5.78 us
  transfers between devices with their start and end apart: 4, of which 4 were waited for; matrix products, arithmetic and copies ran while one was open for 29% of the time, Pallas kernels for 0%

profile of v7, /device:TPU:1, one launch (start us, length us, event | category | flops | bytes accessed | tf_op | source)
XLA Modules:
  0.0 166.6 jit_solution(9188109270367512053)
XLA Ops:
  4.7 2.1 %copy.625 = bf16[2,8,16,1024]{3,2,1,0:T(8,128)(2,1)} copy(bf16[2,8,16,1024]{3,1,2,0:T(8,128)(2,1)} %bitcast.147) | data formatting | bytes 1048576
  11.1 7.7 %all-to-all-start = ((bf16[16,16,3088]{2,1,0:T(8,128)(2,1)}), bf16[16,16,3088]{2,1,0:T(8,128)(2,1)S(1)}, u32[]{:S(2)}, u32[]{:S(2)}) async-start(bf16[16,16,3088]{2,1,0:T(8,128)(2,1)} %copy.545), calls=%async_computation | async-start | bytes 3276800 | tf_op jit(solution)/shard_map/all_to_all | solution.py:183
  31.8 8.4 %all-to-all-done = bf16[16,16,3088]{2,1,0:T(8,128)(2,1)S(1)} async-done(((bf16[16,16,3088]{2,1,0:T(8,128)(2,1)}), bf16[16,16,3088]{2,1,0:T(8,128)(2,1)S(1)}, u32[]{:S(2)}, u32[]{:S(2)}) %all-to-all-start) | async-done | bytes 1581088 | tf_op jit(solution)/shard_map/all_to_all | solution.py:183
  42.3 1.6 copy.559
  43.9 12.8 %all-to-all-start.1 = ((bf16[32,32,432]{2,1,0:T(8,128)(2,1)}), bf16[32,32,432]{2,1,0:T(8,128)(2,1)}, u32[]{:S(2)}, u32[]{:S(2)}) async-start(bf16[32,32,432]{2,1,0:T(8,128)(2,1)} %copy.559), calls=%async_computation.1 | async-start | bytes 2097152 | tf_op jit(solution)/shard_map/all_to_all | solution.py:212
  58.6 1.6 reshape.632
  61.9 1.6 broadcast_multiply_fusion.1
  65.8 5.8 %fusion = bf16[8,1,16,64,256]{4,3,2,0,1:T(8,128)(2,1)} fusion(bf16[8,16,64,256]{3,2,1,0:T(8,128)(2,1)} %param.35, f32[8,16]{1,0:T(8,128)S(1)} %exp.61, f32[8,32,16,64]{3,2,1,0:T(8,128)S(1)} %reshape.632, f32[8,32,16]{1,2,0:T(8,128)S(1)} %bitcast_multiply_fusion, bf16[8,32,2048]{2,1,0:T(8,128)(2,1)S(1)} %copy-done, s32[]{:T(128)S(6)} %select_n.221), kind=kOutput, calls=%fused_computation.6 | convolution fusion | flops 143130624 | bytes 10686468 | tf_op jit(solution)/shard_map/bjgqp,bjgn->bgqpn/dot_general | solution.py:161
  72.4 1.9 %reshape.634 = f32[8,32,1,16,64]{4,3,1,0,2:T(8,128)} reshape(f32[16,16,1024]{2,1,0:T(8,128)S(1)} %get-tuple-element.11) | data formatting | bytes 2097152 | tf_op jit(solution)/shard_map/convert_element_type | solution.py:271
  74.3 10.4 %all-to-all-done.1 = bf16[32,32,432]{2,1,0:T(8,128)(2,1)} async-done(((bf16[32,32,432]{2,1,0:T(8,128)(2,1)}), bf16[32,32,432]{2,1,0:T(8,128)(2,1)}, u32[]{:S(2)}, u32[]{:S(2)}) %all-to-all-start.1) | async-done | bytes 884768 | tf_op jit(solution)/shard_map/all_to_all | solution.py:212
  84.7 1.5 slice.147
  90.1 3.5 %convolution_convert_fusion.2 = bf16[8,32,1024]{2,1,0:T(8,128)(2,1)S(1)} fusion(bf16[8,1024,256]{2,1,0:T(8,128)(2,1)} %bitcast.129, bf16[8,32,256]{2,0,1:T(8,128)(2,1)S(1)} %multiply_convert_fusion.5), kind=kOutput, calls=%fused_computation.30 | convolution fusion | flops 134479872 | bytes 4849664 | tf_op jit(solution)/shard_map/btn,bmn->btm/dot_general | solution.py:227
  94.4 2.5 %copy.605 = bf16[32,32,1024]{2,1,0:T(8,128)(2,1)} copy(bf16[32,32,1024]{2,0,1:T(8,128)(2,1)S(1)} %convolution_convert_fusion) | data formatting | bytes 4194304 | tf_op jit(solution)/shard_map/convert_element_type | solution.py:118
  97.0 4.7 %all-to-all-start.2 = ((bf16[32,32,1024]{2,1,0:T(8,128)(2,1)}), bf16[32,32,1024]{2,1,0:T(8,128)(2,1)}, u32[]{:S(2)}, u32[]{:S(2)}) async-start(bf16[32,32,1024]{2,1,0:T(8,128)(2,1)} %copy.605), calls=%async_computation.2 | async-start | bytes 4194304 | tf_op jit(solution)/shard_map/all_to_all | solution.py:233
  110.0 1.8 %reshape.613 = bf16[8,3,1536]{2,1,0:T(4,128)(2,1)} reshape(bf16[8,32,144]{2,1,0:T(8,128)(2,1)} %copy.561) | data formatting | bytes 147456 | tf_op jit(solution)/shard_map/reshape | solution.py:214
  111.8 1.7 %fusion.6 = f32[8,32,1024]{2,1,0:T(8,128)S(1)} fusion(f32[8,32,1024]{2,1,0:T(8,128)} %fusion.59, f32[1024]{0:T(1024)S(1)} %bitcast.159, bf16[8,3,1536]{2,1,0:T(4,128)(2,1)} %reshape.613, s32[8,32]{1,0:T(8,128)S(1)} %get-tuple-element.32), kind=kOutput, calls=%fused_computation.22 | convolution fusion | flops 2097920 | bytes 2167808 | tf_op jit(solution)/shard_map/bti,bic->btc/dot_general | solution.py:29
  114.7 2.0 %reshape.633 = f32[8,32,1,16,64]{4,3,1,0,2:T(8,128)} reshape(bf16[8,32,1024]{2,1,0:T(8,128)(2,1)S(1)} %multiply_convert_fusion.3) | data formatting | bytes 1572864 | tf_op jit(solution)/shard_map/convert_element_type | solution.py:269
  116.6 1.6 reshape.614
  120.0 29.6 %all-to-all-done.2 = bf16[32,32,1024]{2,1,0:T(8,128)(2,1)} async-done(((bf16[32,32,1024]{2,1,0:T(8,128)(2,1)}), bf16[32,32,1024]{2,1,0:T(8,128)(2,1)}, u32[]{:S(2)}, u32[]{:S(2)}) %all-to-all-start.2) | async-done | bytes 2097184 | tf_op jit(solution)/shard_map/all_to_all | solution.py:233
  149.6 3.9 %fusion.3 = f32[8,32,1024]{2,0,1:T(8,128)S(1)} fusion(bf16[32,32,1024]{2,1,0:T(8,128)(2,1)} %all-to-all-done.2, s32[8]{0:T(128)S(1)} %copy-done.33), kind=kOutput, calls=%fused_computation.12 | convolution fusion | flops 16777472 | bytes 3145760 | tf_op jit(solution)/shard_map/pa,p...->a.../dot_general | solution.py:121
  153.6 1.9 %reshape.679 = f32[8,32,1,16,64]{4,3,0,1,2:T(8,128)} reshape(f32[8,32,1024]{2,0,1:T(8,128)S(1)} %fusion.3) | data formatting | bytes 2097152 | tf_op jit(solution)/shard_map/reshape | solution.py:236
  155.5 6.3 %multiply_reduce_fusion = (f32[8,32]{1,0:T(8,128)S(1)}, f32[8,32,1,16,64]{4,1,3,0,2:T(8,128)S(1)}) fusion(f32[8,32,1,16,64]{4,3,1,0,2:T(8,128)} %reshape.634, f32[8,32,1,16,64]{4,3,1,0,2:T(8,128)} %reshape.633, f32[16]{0:T(128)S(1)} %copy-done.51, f32[8,32,1,16,64]{4,3,0,1,2:T(8,128)} %reshape.679, f32[8,32,16]{1,2,0:T(8,128)S(1)} %copy-done.16, ...), kind=kOutput, calls=%fused_computation.17 | convolution fusion | flops 20446976 | bytes 4809792 | tf_op jit(solution)/shard_map/btjgq,bjgqp->btgqp/dot_general | solution.py:263
  162.2 2.1 %collective-permute-done = f32[8,32,1]{1,0,2:T(8,128)S(1)} collective-permute-done((f32[8,32,1]{1,0,2:T(8,128)S(1)}, f32[8,32,1]{1,0,2:T(8,128)S(1)}, u32[]{:S(2)}, u32[]{:S(2)}) %collective-permute-start) | collective-permute-done | bytes 1056 | tf_op jit(solution)/shard_map/ppermute | solution.py:275
  165.1 1.5 convert_element_type.303
  (243 shorter events, 46.9 us)
Async XLA Ops:
  0.0 65.8 %copy-start = (bf16[8,32,2048]{2,1,0:T(8,128)(2,1)S(1)}, bf16[8,32,2048]{2,1,0:T(8,128)(2,1)}, u32[]{:S(2)}) copy-start(bf16[8,32,2048]{2,1,0:T(8,128)(2,1)} %param.37) | copy-start | bytes 3145732
  11.0 7.8 %copy-start.47 = (s32[128]{0:T(128)S(1)}, s32[128]{0:T(128)}, u32[]{:S(2)}) copy-start(s32[128]{0:T(128)} %param.43) | copy-start | bytes 1540
  11.0 8.2 %copy-start.48 = (s32[8]{0:T(128)S(1)}, s32[8]{0:T(128)}, u32[]{:S(2)}) copy-start(s32[8]{0:T(128)} %param.42) | copy-start | bytes 100
  11.0 8.3 %copy-start.10 = (s32[8,32,32]{2,1,0:T(8,128)S(1)}, s32[8,32,32]{2,1,0:T(8,128)}, u32[]{:S(2)}) copy-start(s32[8,32,32]{2,1,0:T(8,128)} %param.41) | copy-start | bytes 98308
  11.0 9.9 %copy-start.53 = (s32[8]{0:T(128)S(1)}, s32[8]{0:T(128)}, u32[]{:S(2)}) copy-start(s32[8]{0:T(128)} %copy-done.52) | copy-start | bytes 100
  11.0 10.4 %copy-start.4 = (s32[8,32,32]{2,1,0:T(8,128)S(1)}, s32[8,32,32]{2,1,0:T(8,128)}, u32[]{:S(2)}) copy-start(s32[8,32,32]{2,1,0:T(8,128)} %param.26) | copy-start | bytes 98308
  11.0 11.2 %copy-start.46 = (pred[16]{0:T(512)(128)(4,1)S(1)}, pred[16]{0:T(512)(128)(4,1)}, u32[]{:S(2)}) copy-start(pred[16]{0:T(512)(128)(4,1)} %copy-done.45) | copy-start | bytes 52
  11.0 11.8 %copy-start.19 = (bf16[4,4096]{1,0:T(4,128)(2,1)S(1)}, bf16[4,4096]{1,0:T(4,128)(2,1)}, u32[]{:S(2)}) copy-start(bf16[4,4096]{1,0:T(4,128)(2,1)} %param.29) | copy-start | bytes 98308
  11.1 14.1 %copy-start.50 = (f32[16]{0:T(128)S(1)}, f32[16]{0:T(128)}, u32[]{:S(2)}) copy-start(f32[16]{0:T(128)} %param.31) | copy-start | bytes 196
  11.1 29.1 %all-to-all-start = ((bf16[16,16,3088]{2,1,0:T(8,128)(2,1)}), bf16[16,16,3088]{2,1,0:T(8,128)(2,1)S(1)}, u32[]{:S(2)}, u32[]{:S(2)}) async-start(bf16[16,16,3088]{2,1,0:T(8,128)(2,1)} %copy.545), calls=%async_computation | async-start | bytes 3276800 | tf_op jit(solution)/shard_map/all_to_all | solution.py:183
  18.8 8.1 %copy-start.23 = (f32[4096]{0:T(1024)S(1)}, f32[4096]{0:T(1024)}, u32[]{:S(2)}) copy-start(f32[4096]{0:T(1024)} %param.30) | copy-start | bytes 49156
  18.8 10.1 %copy-start.21 = (bf16[4,1024]{1,0:T(4,128)(2,1)S(1)}, bf16[4,1024]{1,0:T(4,128)(2,1)}, u32[]{:S(2)}) copy-start(bf16[4,1024]{1,0:T(4,128)(2,1)} %param.27) | copy-start | bytes 24580
  26.6 13.6 %copy-start.14 = (bf16[24,256]{0,1:T(8,128)(2,1)S(1)}, bf16[24,256]{0,1:T(8,128)(2,1)}, u32[]{:S(2)}) copy-start(bf16[24,256]{0,1:T(8,128)(2,1)} %mul.313) | copy-start | bytes 36868
  28.3 13.0 %copy-start.27 = (s32[8]{0:T(128)}, s32[8]{0:T(128)S(1)}, u32[]{:S(2)}) copy-start(s32[8]{0:T(128)S(1)} %dynamic-slice_reduce_fusion) | copy-start | bytes 100
  29.5 11.8 %copy-start.31 = (s32[8]{0:T(128)S(1)}, s32[8]{0:T(128)}, u32[]{:S(2)}) copy-start(s32[8]{0:T(128)} %fusion.116) | copy-start | bytes 100
  43.9 16.4 %slice-start = ((bf16[16,16,3088]{2,1,0:T(8,128)(2,1)}), bf16[16,16,16]{2,1,0:T(8,128)(2,1)S(1)}, s32[]{:S(2)}) async-start(bf16[16,16,3088]{2,1,0:T(8,128)(2,1)} %copy-done.1), calls=%async_computation.3 | async-start | bytes 131072 | tf_op jit(solution)/shard_map/slice | solution.py:187
  43.9 40.9 %all-to-all-start.1 = ((bf16[32,32,432]{2,1,0:T(8,128)(2,1)}), bf16[32,32,432]{2,1,0:T(8,128)(2,1)}, u32[]{:S(2)}, u32[]{:S(2)}) async-start(bf16[32,32,432]{2,1,0:T(8,128)(2,1)} %copy.559), calls=%async_computation.1 | async-start | bytes 2097152 | tf_op jit(solution)/shard_map/all_to_all | solution.py:212
  65.8 6.4 %copy-start.2 = (bf16[16,16,3088]{2,1,0:T(8,128)(2,1)S(1)}, bf16[16,16,3088]{2,1,0:T(8,128)(2,1)}, u32[]{:S(2)}) copy-start(bf16[16,16,3088]{2,1,0:T(8,128)(2,1)} %copy-done.1) | copy-start | bytes 4743172
  72.4 13.9 %copy-start.28 = (s32[8]{0:T(128)S(1)}, s32[8]{0:T(128)}, u32[]{:S(2)}) copy-start(s32[8]{0:T(128)} %copy-done.27) | copy-start | bytes 100
  96.9 6.7 %copy-start.11 = (pred[8,32,32]{2,0,1:T(8,128)(4,1)S(1)}, pred[8,32,32]{2,0,1:T(8,128)(4,1)}, u32[]{:S(2)}) copy-start(pred[8,32,32]{2,0,1:T(8,128)(4,1)} %get-tuple-element.18) | copy-start | bytes 24580
  97.0 52.7 %all-to-all-start.2 = ((bf16[32,32,1024]{2,1,0:T(8,128)(2,1)}), bf16[32,32,1024]{2,1,0:T(8,128)(2,1)}, u32[]{:S(2)}, u32[]{:S(2)}) async-start(bf16[32,32,1024]{2,1,0:T(8,128)(2,1)} %copy.605), calls=%async_computation.2 | async-start | bytes 4194304 | tf_op jit(solution)/shard_map/all_to_all | solution.py:233
  118.9 30.8 %copy-start.33 = (s32[8]{0:T(128)S(1)}, s32[8]{0:T(128)}, u32[]{:S(2)}) copy-start(s32[8]{0:T(128)} %fusion.116) | copy-start | bytes 100
  155.5 6.6 %copy-start.39 = (f32[1024]{0:T(1024)S(1)}, f32[1024]{0:T(1024)}, u32[]{:S(2)}) copy-start(f32[1024]{0:T(1024)} %param.34) | copy-start | bytes 12292
  161.8 2.5 %collective-permute-start = (f32[8,32,1]{1,0,2:T(8,128)S(1)}, f32[8,32,1]{1,0,2:T(8,128)S(1)}, u32[]{:S(2)}, u32[]{:S(2)}) collective-permute-start(f32[8,32,1]{1,0,2:T(8,128)S(1)} %bitcast.169), channel_id=1, source_target_pairs={{0,1},{1,0},{2,3},{3,2},{4,5},{5,4},{6,7},{7,6},{8,9},{9,8},{10,11... | collective-permute-start | bytes 3080 | tf_op jit(solution)/shard_map/ppermute | solution.py:275
  (36 other events, 98.5 us)

commit v8 on v7

--- a/solution.py
+++ b/solution.py
@@ -52,6 +52,16 @@
     )[None, :]
     taken = jnp.take(moved, picks.reshape(-1), axis=0).reshape((dest_count, span_groups) + lead + (2, STATE))
     return jnp.moveaxis(taken, 1, -2).reshape((dest_count,) + lead + (2 * span_groups * STATE,))
+
+
+def columns_by_dest(rows, span_groups, dest_count, per_dest):
+    count = rows.shape[0]
+    split = rows.reshape(count, 2, GROUPS, STATE)
+    picks = (jnp.arange(dest_count, dtype=jnp.int32) // per_dest)[:, None] * span_groups + jnp.arange(
+        span_groups, dtype=jnp.int32
+    )[None, :]
+    taken = jnp.take(split, picks.reshape(-1), axis=2).reshape(count, 2, dest_count, span_groups, STATE)
+    return jnp.moveaxis(taken, 2, 1).reshape(count, dest_count, 2 * span_groups * STATE)
 
 
 def shards(
@@ -169,24 +179,27 @@
     carry_state = lax.optimization_barrier(carry_state)
     tree_rows = tree_heads.shape[0]
     head_width = local_heads * HEAD_DIM
-    split_heads = jnp.moveaxis(tree_heads.reshape(tree_rows, head_count, head_width), 1, 0)
-    split_gates = jnp.moveaxis(tree_gates.reshape(tree_rows, head_count, head_width), 1, 0)
-    split_steps = jnp.moveaxis(tree_steps.reshape(tree_rows, head_count, local_heads), 1, 0)
-    split_groups = own_columns(tree_groups, span_groups, head_count, per_dest)
-    split_prior = own_columns(prior_groups, span_groups, head_count, per_dest).reshape(
-        head_count, reqs_dev * local_nodes, 2 * own_width
-    )
     widths = [2 * own_width, 2 * own_width, head_width, head_width, local_heads]
     bundle = jnp.concatenate(
-        [split_groups, split_prior.astype(jnp.bfloat16), split_heads, split_gates, split_steps], axis=-1
-    )
-    bundle = lax.all_to_all(bundle, "head", split_axis=0, concat_axis=0, tiled=True)
+        [
+            columns_by_dest(tree_groups, span_groups, head_count, per_dest),
+            columns_by_dest(
+                prior_groups.reshape(reqs_dev * local_nodes, -1), span_groups, head_count, per_dest
+            ),
+            tree_heads.reshape(tree_rows, head_count, head_width),
+            tree_gates.reshape(tree_rows, head_count, head_width),
+            tree_steps.reshape(tree_rows, head_count, local_heads),
+        ],
+        axis=-1,
+    )
+    bundle = lax.all_to_all(bundle, "head", split_axis=1, concat_axis=0, tiled=True)
+    bundle = bundle.reshape(head_count * tree_rows, -1)
     cuts = [0]
     for width in widths:
         cuts.append(cuts[-1] + width)
     pieces = [bundle[..., cuts[n] : cuts[n + 1]] for n in range(len(widths))]
     group_rows = pieces[0].reshape(reqs_dev, NODES, 2 * own_width)
-    prior_flat = pieces[1].reshape(head_count * reqs_dev * local_nodes, 2 * own_width)
+    prior_flat = pieces[1]
     head_rows = pieces[2].reshape(reqs_dev, NODES, head_width)
     gate_rows = pieces[3].reshape(reqs_dev, NODES, span_groups, span_heads, HEAD_DIM)
     step_rows = pieces[4].reshape(reqs_dev, NODES, local_heads)

time: 168 us -> 166 us (0.988)
  waiting for transfers between devices: 50.5 us -> 43.1 us
  local copies, waits for them, and re-layouts: 38.2 us -> 42 us
  other arithmetic: 15.3 us -> 17.6 us
    all_to_all x1, waiting for transfers between devices: 8.41 us -> 4.06 us  [shards(): lax.all_to_all(bundle, 'head', split_axis=1, concat_axis=0, tiled=True)]
    all_to_all x1, waiting for transfers between devices: 10.4 us -> 6.25 us  [shards(): lax.all_to_all(exchange, 'req', split_axis=0, concat_axis=0, tiled=True)]
    unnamed x119 -> x112, local copies, waits for them, and re-layouts: 6.26 us -> 6.67 us
  transfers between devices with their start and end apart: 4 -> 4, of which waited for: 4 -> 4; matrix products, arithmetic and copies ran while one was open for 29% -> 34% of each run, Pallas kernels for 0% -> 0%
where the time goes in v8:
time: 166 us; the launch traced here: 165 us
  waiting for transfers between devices  43.1 us (26%)
  local copies, waits for them, and re-layouts  42 us (25%)
  matrix products  35.5 us (21%)
  starting transfers between devices  25.4 us (15%)
  other arithmetic  17.6 us (11%)
    all_to_all x1, waiting for transfers between devices, shards(): lax.all_to_all(spread(send_hot, carried_old.astype(jnp.bfloat16)), 'req',...  30.7 us
    all_to_all x1, starting transfers between devices, shards(): lax.all_to_all(exchange, 'req', split_axis=0, concat_axis=0, tiled=True)  12.6 us
    all_to_all x1, starting transfers between devices, shards(): lax.all_to_all(bundle, 'head', split_axis=1, concat_axis=0, tiled=True)  7.7 us
    unnamed x112, local copies, waits for them, and re-layouts  6.67 us
    dot_general x1, matrix products, shards(): jnp.einsum('btjgq,bjgqp->btgqp', mixing, values, preferred_element_type=j...  6.26 us
    all_to_all x1, waiting for transfers between devices, shards(): lax.all_to_all(exchange, 'req', split_axis=0, concat_axis=0, tiled=True)  6.25 us
    dot_general x1, matrix products, shards(): jnp.einsum('bjgqp,bjgn->bgqpn', weighted, key_slice, preferred_element_ty...  5.77 us
    dot_general x9, matrix products, tree_conv(): jnp.einsum('btj,bjc->btc', picked, tree_rows, preferred_element_type=jnp....  5.6 us
  transfers between devices with their start and end apart: 4, of which 4 were waited for; matrix products, arithmetic and copies ran while one was open for 34% of the time, Pallas kernels for 0%

profile of v8, /device:TPU:1, one launch (start us, length us, event | category | flops | bytes accessed | tf_op | source)
XLA Modules:
  0.0 164.7 jit_solution(2738890851146619957)
XLA Ops:
  8.4 7.7 %all-to-all-start = ((bf16[16,16,3088]{2,0,1:T(8,128)(2,1)}), bf16[16,16,3088]{2,0,1:T(8,128)(2,1)S(1)}, u32[]{:S(2)}, u32[]{:S(2)}) async-start(bf16[16,16,3088]{2,0,1:T(8,128)(2,1)} %copy_dynamic-update-slice_fusion), calls=%async_computation | async-start | bytes 3276800 | tf_op jit(solution)/shard_map/all_to_all | solution.py:195
  33.5 4.1 %all-to-all-done = bf16[16,16,3088]{2,0,1:T(8,128)(2,1)S(1)} async-done(((bf16[16,16,3088]{2,0,1:T(8,128)(2,1)}), bf16[16,16,3088]{2,0,1:T(8,128)(2,1)S(1)}, u32[]{:S(2)}, u32[]{:S(2)}) %all-to-all-start) | async-done | bytes 1581088 | tf_op jit(solution)/shard_map/all_to_all | solution.py:195
  40.4 1.6 copy.656
  42.1 12.6 %all-to-all-start.1 = ((bf16[32,32,432]{2,1,0:T(8,128)(2,1)}), bf16[32,32,432]{2,1,0:T(8,128)(2,1)}, u32[]{:S(2)}, u32[]{:S(2)}) async-start(bf16[32,32,432]{2,1,0:T(8,128)(2,1)} %copy.656), calls=%async_computation.1 | async-start | bytes 2097152 | tf_op jit(solution)/shard_map/all_to_all | solution.py:225
  56.8 1.6 reshape.639
  59.8 1.5 compare_and_fusion.4
  61.3 1.5 slice.132
  64.4 1.6 broadcast_multiply_fusion.1
  68.1 5.8 %fusion = bf16[8,1,16,64,256]{4,3,2,0,1:T(8,128)(2,1)} fusion(bf16[8,16,64,256]{3,2,1,0:T(8,128)(2,1)} %param.37, f32[8,16]{1,0:T(8,128)S(1)} %exp.61, f32[8,32,16,64]{3,2,1,0:T(8,128)S(1)} %reshape.639, f32[8,32,16]{1,2,0:T(8,128)S(1)} %bitcast_multiply_fusion, bf16[8,32,2048]{2,1,0:T(8,128)(2,1)S(1)} %copy-done, s32[]{:T(128)S(6)} %select_n.199), kind=kOutput, calls=%fused_computation.6 | convolution fusion | flops 143130624 | bytes 10686468 | tf_op jit(solution)/shard_map/bjgqp,bjgn->bgqpn/dot_general | solution.py:171
  74.6 1.9 %reshape.641 = f32[8,32,1,16,64]{4,3,1,0,2:T(8,128)} reshape(f32[256,1024]{1,0:T(8,128)S(1)} %get-tuple-element.12) | data formatting | bytes 2097152 | tf_op jit(solution)/shard_map/convert_element_type | solution.py:284
  76.5 6.2 %all-to-all-done.1 = bf16[32,32,432]{2,1,0:T(8,128)(2,1)} async-done(((bf16[32,32,432]{2,1,0:T(8,128)(2,1)}), bf16[32,32,432]{2,1,0:T(8,128)(2,1)}, u32[]{:S(2)}, u32[]{:S(2)}) %all-to-all-start.1) | async-done | bytes 884768 | tf_op jit(solution)/shard_map/all_to_all | solution.py:225
  82.8 1.5 slice.147
  88.2 3.5 %convolution_convert_fusion.2 = bf16[8,32,1024]{2,1,0:T(8,128)(2,1)S(1)} fusion(bf16[8,1024,256]{2,1,0:T(8,128)(2,1)} %bitcast.134, bf16[8,32,256]{2,0,1:T(8,128)(2,1)S(1)} %multiply_convert_fusion.5), kind=kOutput, calls=%fused_computation.30 | convolution fusion | flops 134479872 | bytes 4849664 | tf_op jit(solution)/shard_map/btn,bmn->btm/dot_general | solution.py:240
  92.5 2.5 %copy.702 = bf16[32,32,1024]{2,1,0:T(8,128)(2,1)} copy(bf16[32,32,1024]{2,0,1:T(8,128)(2,1)S(1)} %convolution_convert_fusion) | data formatting | bytes 4194304 | tf_op jit(solution)/shard_map/convert_element_type | solution.py:128
  95.0 4.7 %all-to-all-start.2 = ((bf16[32,32,1024]{2,1,0:T(8,128)(2,1)}), bf16[32,32,1024]{2,1,0:T(8,128)(2,1)}, u32[]{:S(2)}, u32[]{:S(2)}) async-start(bf16[32,32,1024]{2,1,0:T(8,128)(2,1)} %copy.702), calls=%async_computation.2 | async-start | bytes 4194304 | tf_op jit(solution)/shard_map/all_to_all | solution.py:246
  109.2 1.7 %fusion.6 = f32[8,32,1024]{2,1,0:T(8,128)S(1)} fusion(f32[8,32,1024]{2,1,0:T(8,128)} %fusion.60, f32[1024]{0:T(1024)S(1)} %bitcast.160, bf16[8,3,1536]{2,1,0:T(4,128)(2,1)S(1)} %reshape.620, s32[8,32]{1,0:T(8,128)S(1)} %get-tuple-element.31), kind=kOutput, calls=%fused_computation.22 | convolution fusion | flops 2097920 | bytes 2170880 | tf_op jit(solution)/shard_map/bti,bic->btc/dot_general | solution.py:29
  112.1 2.0 %reshape.640 = f32[8,32,1,16,64]{4,3,1,0,2:T(8,128)} reshape(bf16[8,32,1024]{2,1,0:T(8,128)(2,1)S(1)} %multiply_convert_fusion.3) | data formatting | bytes 1572864 | tf_op jit(solution)/shard_map/convert_element_type | solution.py:282
  114.1 1.6 reshape.621
  117.1 30.7 %all-to-all-done.2 = bf16[32,32,1024]{2,1,0:T(8,128)(2,1)} async-done(((bf16[32,32,1024]{2,1,0:T(8,128)(2,1)}), bf16[32,32,1024]{2,1,0:T(8,128)(2,1)}, u32[]{:S(2)}, u32[]{:S(2)}) %all-to-all-start.2) | async-done | bytes 2097184 | tf_op jit(solution)/shard_map/all_to_all | solution.py:246
  147.7 3.9 %fusion.3 = f32[8,32,1024]{2,0,1:T(8,128)S(1)} fusion(bf16[32,32,1024]{2,1,0:T(8,128)(2,1)} %all-to-all-done.2, s32[8]{0:T(128)S(1)} %copy-done.34), kind=kOutput, calls=%fused_computation.12 | convolution fusion | flops 16777472 | bytes 3145760 | tf_op jit(solution)/shard_map/pa,p...->a.../dot_general | solution.py:131
  151.6 1.9 %reshape.693 = f32[8,32,1,16,64]{4,3,0,1,2:T(8,128)} reshape(f32[8,32,1024]{2,0,1:T(8,128)S(1)} %fusion.3) | data formatting | bytes 2097152 | tf_op jit(solution)/shard_map/reshape | solution.py:249
  153.6 6.3 %multiply_reduce_fusion = (f32[8,32]{1,0:T(8,128)S(1)}, f32[8,32,1,16,64]{4,1,3,0,2:T(8,128)S(1)}) fusion(f32[8,32,1,16,64]{4,3,1,0,2:T(8,128)} %reshape.641, f32[8,32,1,16,64]{4,3,1,0,2:T(8,128)} %reshape.640, f32[16]{0:T(128)S(1)} %copy-done.50, f32[8,32,1,16,64]{4,3,0,1,2:T(8,128)} %reshape.693, f32[8,32,16]{1,2,0:T(8,128)S(1)} %copy-done.18, ...), kind=kOutput, calls=%fused_computation.17 | convolution fusion | flops 20446976 | bytes 4809792 | tf_op jit(solution)/shard_map/btjgq,bjgqp->btgqp/dot_general | solution.py:276
  160.3 2.1 %collective-permute-done = f32[8,32,1]{1,0,2:T(8,128)S(1)} collective-permute-done((f32[8,32,1]{1,0,2:T(8,128)S(1)}, f32[8,32,1]{1,0,2:T(8,128)S(1)}, u32[]{:S(2)}, u32[]{:S(2)}) %collective-permute-start) | collective-permute-done | bytes 1056 | tf_op jit(solution)/shard_map/ppermute | solution.py:288
  163.1 1.5 convert_element_type.303
  (236 shorter events, 53.6 us)
Async XLA Ops:
  0.0 68.0 %copy-start = (bf16[8,32,2048]{2,1,0:T(8,128)(2,1)S(1)}, bf16[8,32,2048]{2,1,0:T(8,128)(2,1)}, u32[]{:S(2)}) copy-start(bf16[8,32,2048]{2,1,0:T(8,128)(2,1)} %param.39) | copy-start | bytes 3145732
  6.8 9.9 %copy-start.48 = (s32[128]{0:T(128)S(1)}, s32[128]{0:T(128)}, u32[]{:S(2)}) copy-start(s32[128]{0:T(128)} %param.45) | copy-start | bytes 1540
  6.8 10.9 %copy-start.47 = (s32[8]{0:T(128)S(1)}, s32[8]{0:T(128)}, u32[]{:S(2)}) copy-start(s32[8]{0:T(128)} %param.44) | copy-start | bytes 100
  6.8 11.0 %copy-start.10 = (s32[8,32,32]{2,1,0:T(8,128)S(1)}, s32[8,32,32]{2,1,0:T(8,128)}, u32[]{:S(2)}) copy-start(s32[8,32,32]{2,1,0:T(8,128)} %param.43) | copy-start | bytes 98308
  8.4 13.2 %copy-start.4 = (s32[8,32,32]{2,1,0:T(8,128)S(1)}, s32[8,32,32]{2,1,0:T(8,128)}, u32[]{:S(2)}) copy-start(s32[8,32,32]{2,1,0:T(8,128)} %param.28) | copy-start | bytes 98308
  8.4 15.4 %copy-start.21 = (bf16[4,4096]{1,0:T(4,128)(2,1)S(1)}, bf16[4,4096]{1,0:T(4,128)(2,1)}, u32[]{:S(2)}) copy-start(bf16[4,4096]{1,0:T(4,128)(2,1)} %param.31) | copy-start | bytes 98308
  8.4 29.1 %all-to-all-start = ((bf16[16,16,3088]{2,0,1:T(8,128)(2,1)}), bf16[16,16,3088]{2,0,1:T(8,128)(2,1)S(1)}, u32[]{:S(2)}, u32[]{:S(2)}) async-start(bf16[16,16,3088]{2,0,1:T(8,128)(2,1)} %copy_dynamic-update-slice_fusion), calls=%async_computation | async-start | bytes 3276800 | tf_op jit(solution)/shard_map/all_to_all | solution.py:195
  18.6 19.0 %copy-start.23 = (pred[8,32]{1,0:T(8,128)(4,1)}, pred[8,32]{1,0:T(8,128)(4,1)S(1)}, u32[]{:S(2)}) copy-start(pred[8,32]{1,0:T(8,128)(4,1)S(1)} %broadcast_compare_fusion) | copy-start | bytes 772
  21.7 17.8 %copy-start.33 = (s32[8]{0:T(128)}, s32[8]{0:T(128)S(1)}, u32[]{:S(2)}) copy-start(s32[8]{0:T(128)S(1)} %fusion.117) | copy-start | bytes 100
  28.7 11.2 %copy-start.29 = (s32[8]{0:T(128)}, s32[8]{0:T(128)S(1)}, u32[]{:S(2)}) copy-start(s32[8]{0:T(128)S(1)} %dynamic-slice_reduce_fusion) | copy-start | bytes 100
  42.1 40.7 %all-to-all-start.1 = ((bf16[32,32,432]{2,1,0:T(8,128)(2,1)}), bf16[32,32,432]{2,1,0:T(8,128)(2,1)}, u32[]{:S(2)}, u32[]{:S(2)}) async-start(bf16[32,32,432]{2,1,0:T(8,128)(2,1)} %copy.656), calls=%async_computation.1 | async-start | bytes 2097152 | tf_op jit(solution)/shard_map/all_to_all | solution.py:225
  54.7 11.4 %copy-start.11 = (s32[8,32,32]{2,1,0:T(8,128)S(1)}, s32[8,32,32]{2,1,0:T(8,128)}, u32[]{:S(2)}) copy-start(s32[8,32,32]{2,1,0:T(8,128)} %param.43) | copy-start | bytes 98308
  68.1 6.4 %copy-start.2 = (bf16[16,16,3088]{2,0,1:T(8,128)(2,1)S(1)}, bf16[16,16,3088]{2,0,1:T(8,128)(2,1)}, u32[]{:S(2)}) copy-start(bf16[16,16,3088]{2,0,1:T(8,128)(2,1)} %copy-done.1) | copy-start | bytes 4743172
  74.6 9.7 %copy-start.30 = (s32[8]{0:T(128)S(1)}, s32[8]{0:T(128)}, u32[]{:S(2)}) copy-start(s32[8]{0:T(128)} %copy-done.29) | copy-start | bytes 100
  76.5 8.9 %copy-start.13 = (bf16[8,3,512]{2,1,0:T(4,128)(2,1)S(1)}, bf16[8,3,512]{2,1,0:T(4,128)(2,1)}, u32[]{:S(2)}) copy-start(bf16[8,3,512]{2,1,0:T(4,128)(2,1)} %copy-done.12) | copy-start | bytes 73732
  95.0 4.7 %copy-start.5 = (s32[8,32,32]{2,1,0:T(8,128)S(1)}, s32[8,32,32]{2,1,0:T(8,128)}, u32[]{:S(2)}) copy-start(s32[8,32,32]{2,1,0:T(8,128)} %param.28) | copy-start | bytes 98308
  95.0 4.7 %copy-start.17 = (f32[8,32,16]{1,0,2:T(8,128)S(1)}, f32[8,32,16]{1,0,2:T(8,128)}, u32[]{:S(2)}) copy-start(f32[8,32,16]{1,0,2:T(8,128)} %get-tuple-element.8) | copy-start | bytes 49156
  95.0 5.7 %copy-start.16 = (pred[8,32,32]{2,0,1:T(8,128)(4,1)S(1)}, pred[8,32,32]{2,0,1:T(8,128)(4,1)}, u32[]{:S(2)}) copy-start(pred[8,32,32]{2,0,1:T(8,128)(4,1)} %get-tuple-element.18) | copy-start | bytes 24580
  95.0 6.7 %copy-start.15 = (pred[8,32,32]{2,0,1:T(8,128)(4,1)S(1)}, pred[8,32,32]{2,0,1:T(8,128)(4,1)}, u32[]{:S(2)}) copy-start(pred[8,32,32]{2,0,1:T(8,128)(4,1)} %get-tuple-element.17) | copy-start | bytes 24580
  95.0 6.9 %copy-start.14 = (pred[8,32,32]{2,0,1:T(8,128)(4,1)S(1)}, pred[8,32,32]{2,0,1:T(8,128)(4,1)}, u32[]{:S(2)}) copy-start(pred[8,32,32]{2,0,1:T(8,128)(4,1)} %get-tuple-element.10) | copy-start | bytes 24580
  95.0 52.7 %all-to-all-start.2 = ((bf16[32,32,1024]{2,1,0:T(8,128)(2,1)}), bf16[32,32,1024]{2,1,0:T(8,128)(2,1)}, u32[]{:S(2)}, u32[]{:S(2)}) async-start(bf16[32,32,1024]{2,1,0:T(8,128)(2,1)} %copy.702), calls=%async_computation.2 | async-start | bytes 4194304 | tf_op jit(solution)/shard_map/all_to_all | solution.py:246
  105.9 5.0 %copy-start.24 = (f32[1,1024]{1,0:T(1,128)S(1)}, f32[1,1024]{1,0:T(1,128)}, u32[]{:S(2)}) copy-start(f32[1,1024]{1,0:T(1,128)} %get-tuple-element.26) | copy-start | bytes 12292
  153.6 6.7 %copy-start.40 = (f32[1024]{0:T(1024)S(1)}, f32[1024]{0:T(1024)}, u32[]{:S(2)}) copy-start(f32[1024]{0:T(1024)} %param.36) | copy-start | bytes 12292
  159.8 2.5 %collective-permute-start = (f32[8,32,1]{1,0,2:T(8,128)S(1)}, f32[8,32,1]{1,0,2:T(8,128)S(1)}, u32[]{:S(2)}, u32[]{:S(2)}) collective-permute-start(f32[8,32,1]{1,0,2:T(8,128)S(1)} %bitcast.170), channel_id=1, source_target_pairs={{0,1},{1,0},{2,3},{3,2},{4,5},{5,4},{6,7},{7,6},{8,9},{9,8},{10,11... | collective-permute-start | bytes 3080 | tf_op jit(solution)/shard_map/ppermute | solution.py:288
  (32 other events, 79.2 us)

commit v9 on v8

--- a/solution.py
+++ b/solution.py
@@ -276,6 +276,7 @@
     inner_part = jnp.einsum(
         "btjgq,bjgqp->btgqp", mixing, values, preferred_element_type=jnp.float32
     )
+    inner_part = lax.optimization_barrier(inner_part)
     output = (
         inner_part
         + jnp.exp(decay_sum).reshape(reqs_dev, NODES, span_groups, span_heads, 1) * carried

time: 166 us -> 171 us (1.030)
  other arithmetic: 17.6 us -> 22.8 us
  matrix products: 35.5 us -> 38.9 us
  local copies, waits for them, and re-layouts: 42 us -> 38.8 us
    reduce_sum x1 -> x2, other arithmetic: 0.26 us -> 6.8 us  [the longest x1 6.53 us: shards(): group_power = jnp.sum(gated_out * gated_out, axis=(3, 4))]
    all_to_all x1, waiting for transfers between devices: 30.7 us -> 26.1 us  [shards(): lax.all_to_all(spread(send_hot, carried_old.astype(jnp.bfloat16)), 'req',...]
    all_to_all x1, waiting for transfers between devices: 4.06 us -> 7.53 us  [shards(): lax.all_to_all(bundle, 'head', split_axis=1, concat_axis=0, tiled=True)]
    dot_general x1, matrix products: 6.26 us -> 3.59 us  [shards(): jnp.einsum('btjgq,bjgqp->btgqp', mixing, values, preferred_element_type=j...]
    dot_general x9, matrix products: 4.47 us -> 6.62 us  [tree_conv(): jnp.einsum('bti,bic->btc', older_rows, tail_rows, preferred_element_type=...]
    unnamed x112 -> x102, local copies, waits for them, and re-layouts: 6.67 us -> 7.17 us
  transfers between devices with their start and end apart: 4 -> 4, of which waited for: 4 -> 4; matrix products, arithmetic and copies ran while one was open for 34% -> 32% of each run, Pallas kernels for 0% -> 0%
where the time goes in v9:
time: 171 us; the launch traced here: 170 us
  waiting for transfers between devices  43.1 us (25%)
  matrix products  38.9 us (23%)
  local copies, waits for them, and re-layouts  38.8 us (23%)
  starting transfers between devices  25.3 us (15%)
  other arithmetic  22.8 us (13%)
    all_to_all x1, waiting for transfers between devices, shards(): lax.all_to_all(spread(send_hot, carried_old.astype(jnp.bfloat16)), 'req',...  26.1 us
    all_to_all x1, starting transfers between devices, shards(): lax.all_to_all(exchange, 'req', split_axis=0, concat_axis=0, tiled=True)  12.6 us
    all_to_all x1, starting transfers between devices, shards(): lax.all_to_all(bundle, 'head', split_axis=1, concat_axis=0, tiled=True)  7.7 us
    all_to_all x1, waiting for transfers between devices, shards(): lax.all_to_all(bundle, 'head', split_axis=1, concat_axis=0, tiled=True)  7.53 us
    all_to_all x1, waiting for transfers between devices, shards(): lax.all_to_all(exchange, 'req', split_axis=0, concat_axis=0, tiled=True)  7.4 us
    unnamed x102, local copies, waits for them, and re-layouts  7.17 us
    dot_general x9, matrix products, tree_conv(): jnp.einsum('bti,bic->btc', older_rows, tail_rows, preferred_element_type=...  6.62 us
    reduce_sum x1, other arithmetic, shards(): group_power = jnp.sum(gated_out * gated_out, axis=(3, 4))  6.53 us
  transfers between devices with their start and end apart: 4, of which 4 were waited for; matrix products, arithmetic and copies ran while one was open for 32% of the time, Pallas kernels for 0%

profile of v9, /device:TPU:1, one launch (start us, length us, event | category | flops | bytes accessed | tf_op | source)
XLA Modules:
  0.0 169.9 jit_solution(13972466886165617963)
XLA Ops:
  8.3 7.7 %all-to-all-start = ((bf16[16,16,3088]{2,0,1:T(8,128)(2,1)}), bf16[16,16,3088]{2,0,1:T(8,128)(2,1)S(1)}, u32[]{:S(2)}, u32[]{:S(2)}) async-start(bf16[16,16,3088]{2,0,1:T(8,128)(2,1)} %copy_dynamic-update-slice_fusion), calls=%async_computation | async-start | bytes 3276800 | tf_op jit(solution)/shard_map/all_to_all | solution.py:195
  29.9 7.5 %all-to-all-done = bf16[16,16,3088]{2,0,1:T(8,128)(2,1)S(1)} async-done(((bf16[16,16,3088]{2,0,1:T(8,128)(2,1)}), bf16[16,16,3088]{2,0,1:T(8,128)(2,1)S(1)}, u32[]{:S(2)}, u32[]{:S(2)}) %all-to-all-start) | async-done | bytes 1581088 | tf_op jit(solution)/shard_map/all_to_all | solution.py:195
  41.5 1.7 copy.656
  43.2 12.6 %all-to-all-start.1 = ((bf16[32,32,432]{2,1,0:T(8,128)(2,1)}), bf16[32,32,432]{2,1,0:T(8,128)(2,1)}, u32[]{:S(2)}, u32[]{:S(2)}) async-start(bf16[32,32,432]{2,1,0:T(8,128)(2,1)} %copy.656), calls=%async_computation.1 | async-start | bytes 2097152 | tf_op jit(solution)/shard_map/all_to_all | solution.py:225
  58.3 1.6 reshape.639
  63.1 1.6 broadcast_multiply_fusion.1
  67.0 5.8 %fusion = bf16[8,1,16,64,256]{4,3,2,0,1:T(8,128)(2,1)} fusion(bf16[8,16,64,256]{3,2,1,0:T(8,128)(2,1)} %param.37, f32[8,16]{1,0:T(8,128)S(1)} %exp.61, f32[8,32,16,64]{3,2,1,0:T(8,128)S(1)} %reshape.639, f32[8,32,16]{1,2,0:T(8,128)S(1)} %bitcast_multiply_fusion, bf16[8,32,2048]{2,1,0:T(8,128)(2,1)S(1)} %copy-done, s32[]{:T(128)S(6)} %select_n.199), kind=kOutput, calls=%fused_computation.6 | convolution fusion | flops 143130624 | bytes 10686468 | tf_op jit(solution)/shard_map/bjgqp,bjgn->bgqpn/dot_general | solution.py:171
  73.6 1.9 %reshape.641 = f32[8,32,1,16,64]{4,3,1,0,2:T(8,128)} reshape(f32[256,1024]{1,0:T(8,128)S(1)} %get-tuple-element.15) | data formatting | bytes 2097152 | tf_op jit(solution)/shard_map/convert_element_type | solution.py:285
  76.5 7.4 %all-to-all-done.1 = bf16[32,32,432]{2,1,0:T(8,128)(2,1)} async-done(((bf16[32,32,432]{2,1,0:T(8,128)(2,1)}), bf16[32,32,432]{2,1,0:T(8,128)(2,1)}, u32[]{:S(2)}, u32[]{:S(2)}) %all-to-all-start.1) | async-done | bytes 884768 | tf_op jit(solution)/shard_map/all_to_all | solution.py:225
  88.1 1.6 multiply_convert_fusion.5
  89.7 3.5 %convolution_convert_fusion.2 = bf16[8,32,1024]{2,1,0:T(8,128)(2,1)S(1)} fusion(bf16[8,1024,256]{2,1,0:T(8,128)(2,1)} %bitcast.130, bf16[8,32,256]{2,0,1:T(8,128)(2,1)S(1)} %multiply_convert_fusion.5), kind=kOutput, calls=%fused_computation.31 | convolution fusion | flops 134479872 | bytes 4849664 | tf_op jit(solution)/shard_map/btn,bmn->btm/dot_general | solution.py:240
  94.1 2.5 %copy.702 = bf16[32,32,1024]{2,1,0:T(8,128)(2,1)} copy(bf16[32,32,1024]{2,0,1:T(8,128)(2,1)S(1)} %convolution_convert_fusion) | data formatting | bytes 4194304 | tf_op jit(solution)/shard_map/convert_element_type | solution.py:128
  96.6 4.7 %all-to-all-start.2 = ((bf16[32,32,1024]{2,1,0:T(8,128)(2,1)}), bf16[32,32,1024]{2,1,0:T(8,128)(2,1)}, u32[]{:S(2)}, u32[]{:S(2)}) async-start(bf16[32,32,1024]{2,1,0:T(8,128)(2,1)} %copy.702), calls=%async_computation.2 | async-start | bytes 4194304 | tf_op jit(solution)/shard_map/all_to_all | solution.py:246
  109.1 1.7 fusion.7
  112.7 1.7 reshape.621
  114.4 1.6 reshape.640
  119.6 3.6 %convolution_bitcast_fusion = f32[8,32,1,16,64]{4,1,3,0,2:T(8,128)} fusion(bf16[8,32,16,64]{3,2,1,0:T(8,128)(2,1)} %reshape.621, f32[8,32,16]{1,2,0:T(8,128)} %copy.673, f32[8,32,32]{2,1,0:T(8,128)S(1)} %copy.672, f32[8,32,16]{1,2,0:T(8,128)} %get-tuple-element.51, pred[8,32,32]{2,1,0:T(8,128)(4,1)S(1)} %copy-done.18), kind=kOutput, calls=%fused_computation.20 | convolution fusion | flops 17563648 | bytes 1646592 | tf_op jit(solution)/shard_map/btjgq,bjgqp->btgqp/dot_general | solution.py:276
  123.2 26.1 %all-to-all-done.2 = bf16[32,32,1024]{2,1,0:T(8,128)(2,1)} async-done(((bf16[32,32,1024]{2,1,0:T(8,128)(2,1)}), bf16[32,32,1024]{2,1,0:T(8,128)(2,1)}, u32[]{:S(2)}, u32[]{:S(2)}) %all-to-all-start.2) | async-done | bytes 2097184 | tf_op jit(solution)/shard_map/all_to_all | solution.py:246
  149.3 4.9 %fusion.4 = f32[8,32,1024]{2,0,1:T(8,128)} fusion(bf16[32,32,1024]{2,1,0:T(8,128)(2,1)} %all-to-all-done.2, s32[8]{0:T(128)S(1)} %copy-done.32), kind=kOutput, calls=%fused_computation.12 | convolution fusion | flops 16777472 | bytes 3145760 | tf_op jit(solution)/shard_map/pa,p...->a.../dot_general | solution.py:131
  154.1 2.9 %reshape.693 = f32[8,32,1,16,64]{4,3,0,1,2:T(8,128)} reshape(f32[8,32,1024]{2,0,1:T(8,128)} %fusion.4) | data formatting | bytes 2097152 | tf_op jit(solution)/shard_map/reshape | solution.py:249
  157.0 6.5 %multiply_reduce_fusion = (f32[8,32]{1,0:T(8,128)S(1)}, f32[8,32,1,16,64]{4,1,3,0,2:T(8,128)}) fusion(f32[8,32,1,16,64]{4,3,1,0,2:T(8,128)} %reshape.641, f32[8,32,1,16,64]{4,3,1,0,2:T(8,128)S(1)} %reshape.640, f32[16]{0:T(128)S(1)} %copy-done.41, f32[8,32,1,16,64]{4,1,3,0,2:T(8,128)} %convolution_bitcast_fusion, f32[8,32,1,16,64]{4,3,0,1,2:T(8,128)} %reshape.693, ...), kind=kLoop, calls=%fused_computation.17 | loop fusion | flops 2883328 | bytes 5260352 | tf_op jit(solution)/shard_map/reduce_sum | solution.py:286
  163.9 2.1 %collective-permute-done = f32[8,32,1]{1,0,2:T(8,128)S(1)} collective-permute-done((f32[8,32,1]{1,0,2:T(8,128)S(1)}, f32[8,32,1]{1,0,2:T(8,128)S(1)}, u32[]{:S(2)}, u32[]{:S(2)}) %collective-permute-start) | collective-permute-done | bytes 1056 | tf_op jit(solution)/shard_map/ppermute | solution.py:289
  166.0 1.9 %multiply_convert_fusion = bf16[8,32,1,16,64]{4,1,3,0,2:T(8,128)(2,1)S(1)} fusion(f32[8,32,1,16,64]{4,1,3,0,2:T(8,128)} %get-tuple-element.9, f32[16,64]{1,0:T(8,128)S(1)} %mul.365, f32[8,32]{1,0:T(8,128)S(1)} %rsqrt_bitcast_fusion), kind=kLoop, calls=%fused_computation.16 | loop fusion | flops 786432 | bytes 1577984 | tf_op jit(solution)/shard_map/convert_element_type | solution.py:305
  168.4 1.5 convert_element_type.303
  (226 shorter events, 54.3 us)
Async XLA Ops:
  0.0 67.0 %copy-start = (bf16[8,32,2048]{2,1,0:T(8,128)(2,1)S(1)}, bf16[8,32,2048]{2,1,0:T(8,128)(2,1)}, u32[]{:S(2)}) copy-start(bf16[8,32,2048]{2,1,0:T(8,128)(2,1)} %param.39) | copy-start | bytes 3145732
  6.8 9.3 %copy-start.43 = (s32[128]{0:T(128)S(1)}, s32[128]{0:T(128)}, u32[]{:S(2)}) copy-start(s32[128]{0:T(128)} %param.45) | copy-start | bytes 1540
  6.8 9.7 %copy-start.42 = (s32[8]{0:T(128)S(1)}, s32[8]{0:T(128)}, u32[]{:S(2)}) copy-start(s32[8]{0:T(128)} %param.44) | copy-start | bytes 100
  6.8 9.7 %copy-start.9 = (s32[8,32,32]{2,1,0:T(8,128)S(1)}, s32[8,32,32]{2,1,0:T(8,128)}, u32[]{:S(2)}) copy-start(s32[8,32,32]{2,1,0:T(8,128)} %param.43) | copy-start | bytes 98308
  8.3 10.6 %copy-start.17 = (bf16[4,4096]{1,0:T(4,128)(2,1)S(1)}, bf16[4,4096]{1,0:T(4,128)(2,1)}, u32[]{:S(2)}) copy-start(bf16[4,4096]{1,0:T(4,128)(2,1)} %param.31) | copy-start | bytes 98308
  8.3 12.6 %copy-start.4 = (s32[8,32,32]{2,1,0:T(8,128)S(1)}, s32[8,32,32]{2,1,0:T(8,128)}, u32[]{:S(2)}) copy-start(s32[8,32,32]{2,1,0:T(8,128)} %param.28) | copy-start | bytes 98308
  8.3 13.7 %copy-start.45 = (f32[16]{0:T(128)S(1)}, f32[16]{0:T(128)}, u32[]{:S(2)}) copy-start(f32[16]{0:T(128)} %param.33) | copy-start | bytes 196
  8.3 29.1 %all-to-all-start = ((bf16[16,16,3088]{2,0,1:T(8,128)(2,1)}), bf16[16,16,3088]{2,0,1:T(8,128)(2,1)S(1)}, u32[]{:S(2)}, u32[]{:S(2)}) async-start(bf16[16,16,3088]{2,0,1:T(8,128)(2,1)} %copy_dynamic-update-slice_fusion), calls=%async_computation | async-start | bytes 3276800 | tf_op jit(solution)/shard_map/all_to_all | solution.py:195
  16.0 7.5 %copy-start.23 = (f32[4096]{0:T(1024)S(1)}, f32[4096]{0:T(1024)}, u32[]{:S(2)}) copy-start(f32[4096]{0:T(1024)} %param.32) | copy-start | bytes 49156
  16.0 9.8 %copy-start.19 = (bf16[4,1024]{1,0:T(4,128)(2,1)S(1)}, bf16[4,1024]{1,0:T(4,128)(2,1)}, u32[]{:S(2)}) copy-start(bf16[4,1024]{1,0:T(4,128)(2,1)} %param.29) | copy-start | bytes 24580
  17.1 20.3 %copy-start.20 = (pred[8,32]{1,0:T(8,128)(4,1)}, pred[8,32]{1,0:T(8,128)(4,1)S(1)}, u32[]{:S(2)}) copy-start(pred[8,32]{1,0:T(8,128)(4,1)S(1)} %broadcast_compare_fusion) | copy-start | bytes 772
  18.3 21.4 %copy-start.31 = (s32[8]{0:T(128)}, s32[8]{0:T(128)S(1)}, u32[]{:S(2)}) copy-start(s32[8]{0:T(128)S(1)} %fusion.118) | copy-start | bytes 100
  25.2 15.9 %copy-start.27 = (s32[8]{0:T(128)}, s32[8]{0:T(128)S(1)}, u32[]{:S(2)}) copy-start(s32[8]{0:T(128)S(1)} %dynamic-slice_reduce_fusion) | copy-start | bytes 100
  43.2 40.7 %all-to-all-start.1 = ((bf16[32,32,432]{2,1,0:T(8,128)(2,1)}), bf16[32,32,432]{2,1,0:T(8,128)(2,1)}, u32[]{:S(2)}, u32[]{:S(2)}) async-start(bf16[32,32,432]{2,1,0:T(8,128)(2,1)} %copy.656), calls=%async_computation.1 | async-start | bytes 2097152 | tf_op jit(solution)/shard_map/all_to_all | solution.py:225
  67.0 6.4 %copy-start.2 = (bf16[16,16,3088]{2,0,1:T(8,128)(2,1)S(1)}, bf16[16,16,3088]{2,0,1:T(8,128)(2,1)}, u32[]{:S(2)}) copy-start(bf16[16,16,3088]{2,0,1:T(8,128)(2,1)} %copy-done.1) | copy-start | bytes 4743172
  73.5 11.9 %copy-start.28 = (s32[8]{0:T(128)S(1)}, s32[8]{0:T(128)}, u32[]{:S(2)}) copy-start(s32[8]{0:T(128)} %copy-done.27) | copy-start | bytes 100
  75.5 11.0 %copy-start.11 = (bf16[8,3,512]{2,1,0:T(4,128)(2,1)S(1)}, bf16[8,3,512]{2,1,0:T(4,128)(2,1)}, u32[]{:S(2)}) copy-start(bf16[8,3,512]{2,1,0:T(4,128)(2,1)} %copy-done.10) | copy-start | bytes 73732
  96.6 4.7 %copy-start.16 = (f32[8,32,16]{1,0,2:T(8,128)S(1)}, f32[8,32,16]{1,0,2:T(8,128)}, u32[]{:S(2)}) copy-start(f32[8,32,16]{1,0,2:T(8,128)} %get-tuple-element.10) | copy-start | bytes 49156
  96.6 5.7 %copy-start.13 = (pred[8,32,32]{2,0,1:T(8,128)(4,1)S(1)}, pred[8,32,32]{2,0,1:T(8,128)(4,1)}, u32[]{:S(2)}) copy-start(pred[8,32,32]{2,0,1:T(8,128)(4,1)} %get-tuple-element.19) | copy-start | bytes 24580
  96.6 6.7 %copy-start.12 = (pred[8,32,32]{2,0,1:T(8,128)(4,1)S(1)}, pred[8,32,32]{2,0,1:T(8,128)(4,1)}, u32[]{:S(2)}) copy-start(pred[8,32,32]{2,0,1:T(8,128)(4,1)} %get-tuple-element.12) | copy-start | bytes 24580
  96.6 52.7 %all-to-all-start.2 = ((bf16[32,32,1024]{2,1,0:T(8,128)(2,1)}), bf16[32,32,1024]{2,1,0:T(8,128)(2,1)}, u32[]{:S(2)}, u32[]{:S(2)}) async-start(bf16[32,32,1024]{2,1,0:T(8,128)(2,1)} %copy.702), calls=%async_computation.2 | async-start | bytes 4194304 | tf_op jit(solution)/shard_map/all_to_all | solution.py:246
  114.4 4.4 %copy-start.30 = (f32[1,512]{1,0:T(1,128)S(1)}, f32[1,512]{1,0:T(1,128)}, u32[]{:S(2)}) copy-start(f32[1,512]{1,0:T(1,128)} %copy-done.29) | copy-start | bytes 6148
  157.0 6.8 %copy-start.34 = (f32[1024]{0:T(1024)S(1)}, f32[1024]{0:T(1024)}, u32[]{:S(2)}) copy-start(f32[1024]{0:T(1024)} %param.36) | copy-start | bytes 12292
  163.6 2.5 %collective-permute-start = (f32[8,32,1]{1,0,2:T(8,128)S(1)}, f32[8,32,1]{1,0,2:T(8,128)S(1)}, u32[]{:S(2)}, u32[]{:S(2)}) collective-permute-start(f32[8,32,1]{1,0,2:T(8,128)S(1)} %bitcast.155), channel_id=1, source_target_pairs={{0,1},{1,0},{2,3},{3,2},{4,5},{5,4},{6,7},{7,6},{8,9},{9,8},{10,11... | collective-permute-start | bytes 3080 | tf_op jit(solution)/shard_map/ppermute | solution.py:289
  (26 other events, 61.8 us)

commit v10 on v8

--- a/solution.py
+++ b/solution.py
@@ -99,7 +99,7 @@
     span_heads = min(local_heads, per_group)
     span_groups = local_heads // span_heads
     per_dest = per_group // span_heads
-    assert span_groups == 1
+    assert span_groups == 1 and per_dest == 2
     first_group = head_index * local_heads // per_group
     slot_count = req_count * MOST
     own_width = span_groups * STATE
@@ -246,7 +246,7 @@
     carried_moved = lax.all_to_all(
         spread(send_hot, carried_old.astype(jnp.bfloat16)), "req", split_axis=0, concat_axis=0, tiled=True
     )
-    carried = gather_back(recv_hot, carried_moved).reshape(reqs_dev, NODES, span_groups, span_heads, HEAD_DIM)
+    carried = gather_back(recv_hot, carried_moved)
     conv_heads = tree_conv(
         head_rows, tails_new[..., :head_width], new_tree, kernel_heads, shift_heads
     )
@@ -276,32 +276,22 @@
     inner_part = jnp.einsum(
         "btjgq,bjgqp->btgqp", mixing, values, preferred_element_type=jnp.float32
     )
+    flat_width = local_heads * HEAD_DIM
+    inner_flat = inner_part.reshape(reqs_dev, NODES, flat_width)
+    decay_flat = jnp.repeat(jnp.exp(decay_sum), HEAD_DIM, axis=-1)
+    skip_flat = jnp.repeat(skip_gain, HEAD_DIM)
     output = (
-        inner_part
-        + jnp.exp(decay_sum).reshape(reqs_dev, NODES, span_groups, span_heads, 1) * carried
-        + skip_gain.reshape(1, 1, span_groups, span_heads, 1) * values.astype(jnp.float32)
-    )
-    gated_out = output * jax.nn.silu(gate_rows.astype(jnp.float32))
-    group_power = jnp.sum(gated_out * gated_out, axis=(3, 4))
-    if per_dest == 2:
-        partner = [(d, d ^ 1) for d in range(head_count)]
-        power_own = group_power + lax.ppermute(group_power, "head", partner)
-    else:
-        zero_index = jnp.zeros((), jnp.int32)
-        power_full = lax.dynamic_update_slice(
-            jnp.zeros((reqs_dev, NODES, GROUPS), jnp.float32),
-            group_power,
-            (zero_index, zero_index, first_group),
-        )
-        power_total = lax.psum(power_full, "head")
-        power_own = lax.dynamic_slice_in_dim(power_total, first_group, span_groups, 2)
+        inner_flat
+        + decay_flat * carried
+        + skip_flat * conv_heads.astype(jnp.float32)
+    )
+    gated_out = output * jax.nn.silu(gate_rows.reshape(reqs_dev, NODES, flat_width).astype(jnp.float32))
+    group_power = jnp.sum(gated_out * gated_out, axis=-1)
+    partner = [(d, d ^ 1) for d in range(head_count)]
+    power_own = group_power + lax.ppermute(group_power, "head", partner)
     scale_factor = lax.rsqrt(power_own / (per_group * HEAD_DIM) + EPSILON)
-    normed = (
-        gated_out
-        * scale_factor[..., None, None]
-        * norm_gain.reshape(1, 1, span_groups, span_heads, HEAD_DIM)
-    )
-    return normed.reshape(reqs_dev * NODES, local_heads * HEAD_DIM).astype(jnp.bfloat16)
+    normed = gated_out * scale_factor[..., None] * norm_gain
+    return normed.reshape(reqs_dev * NODES, flat_width).astype(jnp.bfloat16)
 
 
 def solution(mesh):

time: 166 us -> 159 us (0.958)
  local copies, waits for them, and re-layouts: 42 us -> 38.3 us
  matrix products: 35.5 us -> 33.1 us
    convert_element_type x4 -> x0, local copies, waits for them, and re-layouts: 5.82 us -> none  [the longest x1 1.97 us: shards(): values.astype(jnp.float32)]
    dot_general x1, matrix products: 6.26 us -> 1.39 us  [shards(): jnp.einsum('btjgq,bjgqp->btgqp', mixing, values, preferred_element_type=j...]
    all_to_all x1, waiting for transfers between devices: 4.06 us -> 6.43 us  [shards(): lax.all_to_all(bundle, 'head', split_axis=1, concat_axis=0, tiled=True)]
    all_to_all x1, waiting for transfers between devices: 30.7 us -> 28.3 us  [shards(): lax.all_to_all(spread(send_hot, carried_old.astype(jnp.bfloat16)), 'req',...]
    unnamed x112 -> x124, local copies, waits for them, and re-layouts: 6.67 us -> 7.68 us
  transfers between devices with their start and end apart: 4 -> 4, of which waited for: 4 -> 4; matrix products, arithmetic and copies ran while one was open for 34% -> 35% of each run, Pallas kernels for 0% -> 0%
where the time goes in v10:
time: 159 us; the launch traced here: 158 us
  waiting for transfers between devices  43.3 us (27%)
  local copies, waits for them, and re-layouts  38.3 us (24%)
  matrix products  33.1 us (21%)
  starting transfers between devices  25.4 us (16%)
  other arithmetic  16.4 us (10%)
    all_to_all x1, waiting for transfers between devices, shards(): lax.all_to_all(spread(send_hot, carried_old.astype(jnp.bfloat16)), 'req',...  28.3 us
    all_to_all x1, starting transfers between devices, shards(): lax.all_to_all(exchange, 'req', split_axis=0, concat_axis=0, tiled=True)  12.6 us
    all_to_all x1, starting transfers between devices, shards(): lax.all_to_all(bundle, 'head', split_axis=1, concat_axis=0, tiled=True)  7.7 us
    unnamed x124, local copies, waits for them, and re-layouts  7.68 us
    dot_general x9, matrix products, tree_conv(): jnp.einsum('btj,bjc->btc', picked, tree_rows, preferred_element_type=jnp....  6.48 us
    all_to_all x1, waiting for transfers between devices, shards(): lax.all_to_all(bundle, 'head', split_axis=1, concat_axis=0, tiled=True)  6.43 us
    all_to_all x1, waiting for transfers between devices, shards(): lax.all_to_all(exchange, 'req', split_axis=0, concat_axis=0, tiled=True)  6.38 us
    dot_general x1, matrix products, shards(): jnp.einsum('bjgqp,bjgn->bgqpn', weighted, key_slice, preferred_element_ty...  5.69 us
  transfers between devices with their start and end apart: 4, of which 4 were waited for; matrix products, arithmetic and copies ran while one was open for 35% of the time, Pallas kernels for 0%

profile of v10, /device:TPU:1, one launch (start us, length us, event | category | flops | bytes accessed | tf_op | source)
XLA Modules:
  0.0 157.6 jit_solution(8431362187993502836)
XLA Ops:
  8.3 7.7 %all-to-all-start = ((bf16[16,16,3088]{2,0,1:T(8,128)(2,1)}), bf16[16,16,3088]{2,0,1:T(8,128)(2,1)S(1)}, u32[]{:S(2)}, u32[]{:S(2)}) async-start(bf16[16,16,3088]{2,0,1:T(8,128)(2,1)} %copy_dynamic-update-slice_fusion), calls=%async_computation | async-start | bytes 3276800 | tf_op jit(solution)/shard_map/all_to_all | solution.py:195
  26.2 1.2 exponential_negate_fusion
  31.0 6.4 %all-to-all-done = bf16[16,16,3088]{2,0,1:T(8,128)(2,1)S(1)} async-done(((bf16[16,16,3088]{2,0,1:T(8,128)(2,1)}), bf16[16,16,3088]{2,0,1:T(8,128)(2,1)S(1)}, u32[]{:S(2)}, u32[]{:S(2)}) %all-to-all-start) | async-done | bytes 1581088 | tf_op jit(solution)/shard_map/all_to_all | solution.py:195
  41.8 1.7 %copy.635 = bf16[32,32,432]{2,1,0:T(8,128)(2,1)} copy(bf16[32,32,432]{2,0,1:T(8,128)(2,1)S(1)} %pad_maximum_fusion) | data formatting | bytes 1769472 | tf_op jit(solution)/shard_map/concatenate | solution.py:221
  43.5 12.6 %all-to-all-start.1 = ((bf16[32,32,432]{2,1,0:T(8,128)(2,1)}), bf16[32,32,432]{2,1,0:T(8,128)(2,1)}, u32[]{:S(2)}, u32[]{:S(2)}) async-start(bf16[32,32,432]{2,1,0:T(8,128)(2,1)} %copy.635), calls=%async_computation.1 | async-start | bytes 2097152 | tf_op jit(solution)/shard_map/all_to_all | solution.py:225
  56.1 1.4 broadcast_select_fusion.1
  58.1 1.6 %reshape.567 = f32[8,32,16,64]{3,2,1,0:T(8,128)S(1)} reshape(bf16[8,32,1024]{2,1,0:T(8,128)(2,1)} %param.38) | data formatting | bytes 1572864 | tf_op jit(solution)/shard_map/convert_element_type | solution.py:163
  61.1 1.5 slice.132
  67.3 5.7 %fusion = bf16[8,1,16,64,256]{4,3,2,0,1:T(8,128)(2,1)} fusion(bf16[8,16,64,256]{3,2,1,0:T(8,128)(2,1)} %param.37, f32[8,16]{1,0:T(8,128)S(1)} %exp.52, f32[8,32,16,64]{3,2,1,0:T(8,128)S(1)} %reshape.567, f32[8,32,16]{1,2,0:T(8,128)S(1)} %bitcast_multiply_fusion, bf16[8,32,2048]{2,1,0:T(8,128)(2,1)S(1)} %copy-done, s32[]{:T(128)S(6)} %select_n.199), kind=kOutput, calls=%fused_computation.6 | convolution fusion | flops 143130624 | bytes 10686468 | tf_op jit(solution)/shard_map/bjgqp,bjgn->bgqpn/dot_general | solution.py:171
  75.3 1.5 reshape.552
  77.8 6.4 %all-to-all-done.1 = bf16[32,32,432]{2,1,0:T(8,128)(2,1)} async-done(((bf16[32,32,432]{2,1,0:T(8,128)(2,1)}), bf16[32,32,432]{2,1,0:T(8,128)(2,1)}, u32[]{:S(2)}, u32[]{:S(2)}) %all-to-all-start.1) | async-done | bytes 884768 | tf_op jit(solution)/shard_map/all_to_all | solution.py:225
  84.2 1.5 slice.147
  89.5 3.5 %convolution_convert_fusion.2 = bf16[8,32,1024]{2,1,0:T(8,128)(2,1)S(1)} fusion(bf16[8,1024,256]{2,1,0:T(8,128)(2,1)} %bitcast.129, bf16[8,32,256]{2,0,1:T(8,128)(2,1)S(1)} %multiply_convert_fusion.5), kind=kOutput, calls=%fused_computation.26 | convolution fusion | flops 134479872 | bytes 4849664 | tf_op jit(solution)/shard_map/btn,bmn->btm/dot_general | solution.py:240
  93.9 2.5 %copy.683 = bf16[32,32,1024]{2,1,0:T(8,128)(2,1)} copy(bf16[32,32,1024]{2,0,1:T(8,128)(2,1)S(1)} %convolution_convert_fusion) | data formatting | bytes 4194304 | tf_op jit(solution)/shard_map/convert_element_type | solution.py:128
  96.4 4.7 %all-to-all-start.2 = ((bf16[32,32,1024]{2,1,0:T(8,128)(2,1)}), bf16[32,32,1024]{2,1,0:T(8,128)(2,1)}, u32[]{:S(2)}, u32[]{:S(2)}) async-start(bf16[32,32,1024]{2,1,0:T(8,128)(2,1)} %copy.683), calls=%async_computation.2 | async-start | bytes 4194304 | tf_op jit(solution)/shard_map/all_to_all | solution.py:246
  104.1 1.4 fusion.64
  105.8 1.3 fusion.72
  110.7 1.3 fusion.14
  112.9 1.7 %fusion.4 = f32[8,32,1024]{2,1,0:T(8,128)S(1)} fusion(f32[8,32,1024]{2,1,0:T(8,128)} %fusion.64, f32[1024]{0:T(1024)S(1)} %bitcast.156, bf16[8,3,1536]{2,1,0:T(4,128)(2,1)S(1)} %reshape.547, s32[8,32]{1,0:T(8,128)S(1)} %get-tuple-element.42), kind=kOutput, calls=%fused_computation.16 | convolution fusion | flops 2097920 | bytes 2170880 | tf_op jit(solution)/shard_map/bti,bic->btc/dot_general | solution.py:29
  116.6 1.4 convolution_bitcast_fusion
  119.2 1.6 reshape.551
  120.8 28.3 %all-to-all-done.2 = bf16[32,32,1024]{2,1,0:T(8,128)(2,1)} async-done(((bf16[32,32,1024]{2,1,0:T(8,128)(2,1)}), bf16[32,32,1024]{2,1,0:T(8,128)(2,1)}, u32[]{:S(2)}, u32[]{:S(2)}) %all-to-all-start.2) | async-done | bytes 2097184 | tf_op jit(solution)/shard_map/all_to_all | solution.py:246
  149.1 4.0 %fusion.1 = f32[8,32,1024]{2,0,1:T(8,128)S(1)} fusion(bf16[32,32,1024]{2,1,0:T(8,128)(2,1)} %all-to-all-done.2, s32[8]{0:T(128)S(1)} %copy-done.42), kind=kOutput, calls=%fused_computation.7 | convolution fusion | flops 16777472 | bytes 3145760 | tf_op jit(solution)/shard_map/pa,p...->a.../dot_general | solution.py:131
  154.5 2.2 %collective-permute-done = f32[8,32]{1,0:T(8,128)S(1)} collective-permute-done((f32[8,32]{1,0:T(8,128)S(1)}, f32[8,32]{1,0:T(8,128)S(1)}, u32[]{:S(2)}, u32[]{:S(2)}) %collective-permute-start) | collective-permute-done | bytes 1056 | tf_op jit(solution)/shard_map/ppermute | solution.py:291
  (250 shorter events, 53.5 us)
Async XLA Ops:
  0.0 67.2 %copy-start = (bf16[8,32,2048]{2,1,0:T(8,128)(2,1)S(1)}, bf16[8,32,2048]{2,1,0:T(8,128)(2,1)}, u32[]{:S(2)}) copy-start(bf16[8,32,2048]{2,1,0:T(8,128)(2,1)} %param.39) | copy-start | bytes 3145732
  6.8 9.3 %copy-start.55 = (s32[128]{0:T(128)S(1)}, s32[128]{0:T(128)}, u32[]{:S(2)}) copy-start(s32[128]{0:T(128)} %param.45) | copy-start | bytes 1540
  6.8 9.7 %copy-start.54 = (s32[8]{0:T(128)S(1)}, s32[8]{0:T(128)}, u32[]{:S(2)}) copy-start(s32[8]{0:T(128)} %param.44) | copy-start | bytes 100
  6.8 9.8 %copy-start.16 = (s32[8,32,32]{2,1,0:T(8,128)S(1)}, s32[8,32,32]{2,1,0:T(8,128)}, u32[]{:S(2)}) copy-start(s32[8,32,32]{2,1,0:T(8,128)} %param.43) | copy-start | bytes 98308
  8.3 12.6 %copy-start.26 = (bf16[4,4096]{1,0:T(4,128)(2,1)S(1)}, bf16[4,4096]{1,0:T(4,128)(2,1)}, u32[]{:S(2)}) copy-start(bf16[4,4096]{1,0:T(4,128)(2,1)} %param.31) | copy-start | bytes 98308
  8.3 29.1 %all-to-all-start = ((bf16[16,16,3088]{2,0,1:T(8,128)(2,1)}), bf16[16,16,3088]{2,0,1:T(8,128)(2,1)S(1)}, u32[]{:S(2)}, u32[]{:S(2)}) async-start(bf16[16,16,3088]{2,0,1:T(8,128)(2,1)} %copy_dynamic-update-slice_fusion), calls=%async_computation | async-start | bytes 3276800 | tf_op jit(solution)/shard_map/all_to_all | solution.py:195
  16.0 6.4 %copy-start.33 = (f32[4096]{0:T(1024)S(1)}, f32[4096]{0:T(1024)}, u32[]{:S(2)}) copy-start(f32[4096]{0:T(1024)} %param.32) | copy-start | bytes 49156
  16.0 7.6 %copy-start.9 = (s32[8,32,32]{2,1,0:T(8,128)S(1)}, s32[8,32,32]{2,1,0:T(8,128)}, u32[]{:S(2)}) copy-start(s32[8,32,32]{2,1,0:T(8,128)} %param.28) | copy-start | bytes 98308
  16.0 12.6 %copy-start.28 = (bf16[4,1024]{1,0:T(4,128)(2,1)S(1)}, bf16[4,1024]{1,0:T(4,128)(2,1)}, u32[]{:S(2)}) copy-start(bf16[4,1024]{1,0:T(4,128)(2,1)} %param.29) | copy-start | bytes 24580
  17.4 20.0 %copy-start.30 = (pred[8,32]{1,0:T(8,128)(4,1)}, pred[8,32]{1,0:T(8,128)(4,1)S(1)}, u32[]{:S(2)}) copy-start(pred[8,32]{1,0:T(8,128)(4,1)S(1)} %broadcast_compare_fusion) | copy-start | bytes 772
  18.8 11.3 %copy-start.12 = (bf16[8,32,1024]{2,1,0:T(8,128)(2,1)S(1)}, bf16[8,32,1024]{2,1,0:T(8,128)(2,1)}, u32[]{:S(2)}) copy-start(bf16[8,32,1024]{2,1,0:T(8,128)(2,1)} %param.41) | copy-start | bytes 1572868
  22.4 18.4 %copy-start.41 = (s32[8]{0:T(128)S(1)}, s32[8]{0:T(128)}, u32[]{:S(2)}) copy-start(s32[8]{0:T(128)} %fusion.121) | copy-start | bytes 100
  26.2 15.1 %copy-start.37 = (s32[8]{0:T(128)}, s32[8]{0:T(128)S(1)}, u32[]{:S(2)}) copy-start(s32[8]{0:T(128)S(1)} %dynamic-slice_reduce_fusion) | copy-start | bytes 100
  43.5 40.7 %all-to-all-start.1 = ((bf16[32,32,432]{2,1,0:T(8,128)(2,1)}), bf16[32,32,432]{2,1,0:T(8,128)(2,1)}, u32[]{:S(2)}, u32[]{:S(2)}) async-start(bf16[32,32,432]{2,1,0:T(8,128)(2,1)} %copy.635), calls=%async_computation.1 | async-start | bytes 2097152 | tf_op jit(solution)/shard_map/all_to_all | solution.py:225
  56.1 9.1 %copy-start.17 = (s32[8,32,32]{2,1,0:T(8,128)S(1)}, s32[8,32,32]{2,1,0:T(8,128)}, u32[]{:S(2)}) copy-start(s32[8,32,32]{2,1,0:T(8,128)} %param.43) | copy-start | bytes 98308
  67.3 6.3 %copy-start.10 = (s32[8,32,32]{2,1,0:T(8,128)S(1)}, s32[8,32,32]{2,1,0:T(8,128)}, u32[]{:S(2)}) copy-start(s32[8,32,32]{2,1,0:T(8,128)} %param.28) | copy-start | bytes 98308
  75.2 10.4 %copy-start.38 = (s32[8]{0:T(128)S(1)}, s32[8]{0:T(128)}, u32[]{:S(2)}) copy-start(s32[8]{0:T(128)} %copy-done.37) | copy-start | bytes 100
  76.8 10.0 %copy-start.19 = (bf16[8,3,512]{2,1,0:T(4,128)(2,1)S(1)}, bf16[8,3,512]{2,1,0:T(4,128)(2,1)}, u32[]{:S(2)}) copy-start(bf16[8,3,512]{2,1,0:T(4,128)(2,1)} %copy-done.18) | copy-start | bytes 73732
  96.4 6.8 %copy-start.2 = (bf16[16,16,3088]{2,0,1:T(8,128)(2,1)S(1)}, bf16[16,16,3088]{2,0,1:T(8,128)(2,1)}, u32[]{:S(2)}) copy-start(bf16[16,16,3088]{2,0,1:T(8,128)(2,1)} %copy-done.1) | copy-start | bytes 4743172
  96.4 52.7 %all-to-all-start.2 = ((bf16[32,32,1024]{2,1,0:T(8,128)(2,1)}), bf16[32,32,1024]{2,1,0:T(8,128)(2,1)}, u32[]{:S(2)}, u32[]{:S(2)}) async-start(bf16[32,32,1024]{2,1,0:T(8,128)(2,1)} %copy.683), calls=%async_computation.2 | async-start | bytes 4194304 | tf_op jit(solution)/shard_map/all_to_all | solution.py:246
  120.7 32.3 %copy-start.3 = (f32[8,32,1024]{2,1,0:T(8,128)S(1)}, f32[8,32,1024]{2,1,0:T(8,128)}, u32[]{:S(2)}) copy-start(f32[8,32,1024]{2,1,0:T(8,128)} %reshape.552) | copy-start | bytes 3145732
  120.8 32.3 %copy-start.4 = (f32[8,32,1024]{2,1,0:T(8,128)S(1)}, f32[8,32,1024]{2,1,0:T(8,128)}, u32[]{:S(2)}) copy-start(f32[8,32,1024]{2,1,0:T(8,128)} %reshape.551) | copy-start | bytes 3145732
  120.8 32.3 %copy-start.29 = (f32[1024]{0:T(1024)S(1)}, f32[1024]{0:T(1024)}, u32[]{:S(2)}) copy-start(f32[1024]{0:T(1024)} %mul.324) | copy-start | bytes 12292
  154.1 2.5 %collective-permute-start = (f32[8,32]{1,0:T(8,128)S(1)}, f32[8,32]{1,0:T(8,128)S(1)}, u32[]{:S(2)}, u32[]{:S(2)}) collective-permute-start(f32[8,32]{1,0:T(8,128)S(1)} %get-tuple-element.8), channel_id=1, source_target_pairs={{0,1},{1,0},{2,3},{3,2},{4,5},{5,4},{6,7},{7,6},{8,9},{9,8},{10,11... | collective-permute-start | bytes 3080 | tf_op jit(solution)/shard_map/ppermute | solution.py:291
  (38 other events, 110.3 us)

commit v11 on v10

--- a/solution.py
+++ b/solution.py
@@ -218,15 +218,16 @@
         [group_rows[..., own_width:], new_tree.astype(jnp.bfloat16)], axis=-1
     )
     new_len = new_part.shape[-1]
+    old_len = old_part.shape[-1]
     exchange = jnp.concatenate(
-        [spread(send_hot, new_part), spread(recv_hot, old_part)],
+        [spread(recv_hot, old_part), spread(send_hot, new_part)],
         axis=-1,
     )
     exchange = lax.all_to_all(exchange, "req", split_axis=0, concat_axis=0, tiled=True)
     tails_new = (
-        gather_back(recv_hot, exchange[..., :new_len]).astype(jnp.bfloat16).reshape(reqs_dev, 3, -1)
-    )
-    rows_old = gather_back(send_hot, exchange[..., new_len:]).astype(jnp.bfloat16)
+        gather_back(recv_hot, exchange[..., old_len:]).astype(jnp.bfloat16).reshape(reqs_dev, 3, -1)
+    )
+    rows_old = gather_back(send_hot, exchange[..., :old_len]).astype(jnp.bfloat16)
     tree_old = rows_old[..., own_width:].astype(jnp.int32)
     kernel_own = own_columns(kernel_groups, span_groups, head_count, per_dest)[head_index]
     shift_own = own_columns(shift_groups, span_groups, head_count, per_dest)[head_index]
@@ -246,7 +247,9 @@
     carried_moved = lax.all_to_all(
         spread(send_hot, carried_old.astype(jnp.bfloat16)), "req", split_axis=0, concat_axis=0, tiled=True
     )
-    carried = gather_back(recv_hot, carried_moved)
+    carried = jnp.einsum(
+        "pa,p...->a...", recv_hot, carried_moved, preferred_element_type=jnp.bfloat16
+    ).astype(jnp.float32)
     conv_heads = tree_conv(
         head_rows, tails_new[..., :head_width], new_tree, kernel_heads, shift_heads
     )

time: 159 us -> 159 us (level)
    dot_general x3 -> x2, matrix products: 4.71 us -> 0.72 us  [gather_back(): jnp.einsum('pa,p...->a...', hot, moved, preferred_element_type=jnp.float32)]
    dot_general x0 -> x1, matrix products: none -> 3.96 us  [shards(): jnp.einsum('pa,p...->a...', recv_hot, carried_moved, preferred_element_ty...]
    unnamed x124 -> x122, local copies, waits for them, and re-layouts: 7.68 us -> 7.72 us
where the time goes in v11:
time: 159 us; the launch traced here: 158 us
  waiting for transfers between devices  43.2 us (27%)
  local copies, waits for them, and re-layouts  38.2 us (24%)
  matrix products  33.1 us (21%)
  starting transfers between devices  25.3 us (16%)
  other arithmetic  17.1 us (11%)
    all_to_all x1, waiting for transfers between devices, shards(): lax.all_to_all(spread(send_hot, carried_old.astype(jnp.bfloat16)), 'req',...  28.1 us
    all_to_all x1, starting transfers between devices, shards(): lax.all_to_all(exchange, 'req', split_axis=0, concat_axis=0, tiled=True)  12.6 us
    unnamed x122, local copies, waits for them, and re-layouts  7.72 us
    all_to_all x1, starting transfers between devices, shards(): lax.all_to_all(bundle, 'head', split_axis=1, concat_axis=0, tiled=True)  7.7 us
    dot_general x9, matrix products, tree_conv(): jnp.einsum('btj,bjc->btc', picked, tree_rows, preferred_element_type=jnp....  6.46 us
    all_to_all x1, waiting for transfers between devices, shards(): lax.all_to_all(bundle, 'head', split_axis=1, concat_axis=0, tiled=True)  6.45 us
    all_to_all x1, waiting for transfers between devices, shards(): lax.all_to_all(exchange, 'req', split_axis=0, concat_axis=0, tiled=True)  6.42 us
    dot_general x1, matrix products, shards(): jnp.einsum('bjgqp,bjgn->bgqpn', weighted, key_slice, preferred_element_ty...  5.68 us
  transfers between devices with their start and end apart: 4, of which 4 were waited for; matrix products, arithmetic and copies ran while one was open for 35% of the time, Pallas kernels for 0%

profile of v11, /device:TPU:1, one launch (start us, length us, event | category | flops | bytes accessed | tf_op | source)
XLA Modules:
  0.0 158.0 jit_solution(9941275024985759520)
XLA Ops:
  8.3 7.7 %all-to-all-start = ((bf16[16,16,3088]{2,0,1:T(8,128)(2,1)}), bf16[16,16,3088]{2,0,1:T(8,128)(2,1)S(1)}, u32[]{:S(2)}, u32[]{:S(2)}) async-start(bf16[16,16,3088]{2,0,1:T(8,128)(2,1)} %copy_dynamic-update-slice_fusion), calls=%async_computation | async-start | bytes 3276800 | tf_op jit(solution)/shard_map/all_to_all | solution.py:195
  31.0 6.4 %all-to-all-done = bf16[16,16,3088]{2,0,1:T(8,128)(2,1)S(1)} async-done(((bf16[16,16,3088]{2,0,1:T(8,128)(2,1)}), bf16[16,16,3088]{2,0,1:T(8,128)(2,1)S(1)}, u32[]{:S(2)}, u32[]{:S(2)}) %all-to-all-start) | async-done | bytes 1581088 | tf_op jit(solution)/shard_map/all_to_all | solution.py:195
  41.7 1.6 %copy.635 = bf16[32,32,432]{2,1,0:T(8,128)(2,1)} copy(bf16[32,32,432]{2,0,1:T(8,128)(2,1)S(1)} %pad_maximum_fusion) | data formatting | bytes 1769472 | tf_op jit(solution)/shard_map/concatenate | solution.py:222
  43.3 12.6 %all-to-all-start.1 = ((bf16[32,32,432]{2,1,0:T(8,128)(2,1)}), bf16[32,32,432]{2,1,0:T(8,128)(2,1)}, u32[]{:S(2)}, u32[]{:S(2)}) async-start(bf16[32,32,432]{2,1,0:T(8,128)(2,1)} %copy.635), calls=%async_computation.1 | async-start | bytes 2097152 | tf_op jit(solution)/shard_map/all_to_all | solution.py:226
  56.0 1.3 broadcast_select_fusion.1
  57.9 1.6 %reshape.567 = f32[8,32,16,64]{3,2,1,0:T(8,128)S(1)} reshape(bf16[8,32,1024]{2,1,0:T(8,128)(2,1)} %param.38) | data formatting | bytes 1572864 | tf_op jit(solution)/shard_map/convert_element_type | solution.py:163
  60.9 1.5 slice.132
  67.1 5.7 %fusion = bf16[8,1,16,64,256]{4,3,2,0,1:T(8,128)(2,1)} fusion(bf16[8,16,64,256]{3,2,1,0:T(8,128)(2,1)} %param.37, f32[8,16]{1,0:T(8,128)S(1)} %exp.52, f32[8,32,16,64]{3,2,1,0:T(8,128)S(1)} %reshape.567, f32[8,32,16]{1,2,0:T(8,128)S(1)} %bitcast_multiply_fusion, bf16[8,32,2048]{2,1,0:T(8,128)(2,1)S(1)} %copy-done, s32[]{:T(128)S(6)} %select_n.199), kind=kOutput, calls=%fused_computation.6 | convolution fusion | flops 143130624 | bytes 10686468 | tf_op jit(solution)/shard_map/bjgqp,bjgn->bgqpn/dot_general | solution.py:171
  75.1 1.5 reshape.552
  77.6 6.4 %all-to-all-done.1 = bf16[32,32,432]{2,1,0:T(8,128)(2,1)} async-done(((bf16[32,32,432]{2,1,0:T(8,128)(2,1)}), bf16[32,32,432]{2,1,0:T(8,128)(2,1)}, u32[]{:S(2)}, u32[]{:S(2)}) %all-to-all-start.1) | async-done | bytes 884768 | tf_op jit(solution)/shard_map/all_to_all | solution.py:226
  89.2 3.5 %convolution_convert_fusion.2 = bf16[8,32,1024]{2,1,0:T(8,128)(2,1)S(1)} fusion(bf16[8,1024,256]{2,1,0:T(8,128)(2,1)} %bitcast.129, bf16[8,32,256]{2,0,1:T(8,128)(2,1)S(1)} %multiply_convert_fusion.5), kind=kOutput, calls=%fused_computation.26 | convolution fusion | flops 134479872 | bytes 4849664 | tf_op jit(solution)/shard_map/btn,bmn->btm/dot_general | solution.py:241
  93.5 2.5 %copy.683 = bf16[32,32,1024]{2,1,0:T(8,128)(2,1)} copy(bf16[32,32,1024]{2,0,1:T(8,128)(2,1)S(1)} %convolution_convert_fusion) | data formatting | bytes 4194304 | tf_op jit(solution)/shard_map/convert_element_type | solution.py:128
  96.0 4.7 %all-to-all-start.2 = ((bf16[32,32,1024]{2,1,0:T(8,128)(2,1)}), bf16[32,32,1024]{2,1,0:T(8,128)(2,1)}, u32[]{:S(2)}, u32[]{:S(2)}) async-start(bf16[32,32,1024]{2,1,0:T(8,128)(2,1)} %copy.683), calls=%async_computation.2 | async-start | bytes 4194304 | tf_op jit(solution)/shard_map/all_to_all | solution.py:247
  103.7 1.3 fusion.62
  105.4 1.3 fusion.70
  106.7 1.3 slice.138
  110.5 1.3 fusion.14
  112.7 1.7 %fusion.4 = f32[8,32,1024]{2,1,0:T(8,128)S(1)} fusion(f32[8,32,1024]{2,1,0:T(8,128)} %fusion.62, f32[1024]{0:T(1024)S(1)} %bitcast.156, bf16[8,3,1536]{2,1,0:T(4,128)(2,1)S(1)} %reshape.547, s32[8,32]{1,0:T(8,128)S(1)} %get-tuple-element.42), kind=kOutput, calls=%fused_computation.16 | convolution fusion | flops 2097920 | bytes 2170880 | tf_op jit(solution)/shard_map/bti,bic->btc/dot_general | solution.py:29
  116.4 1.4 convolution_bitcast_fusion
  119.0 1.6 reshape.551
  120.6 28.1 %all-to-all-done.2 = bf16[32,32,1024]{2,1,0:T(8,128)(2,1)} async-done(((bf16[32,32,1024]{2,1,0:T(8,128)(2,1)}), bf16[32,32,1024]{2,1,0:T(8,128)(2,1)}, u32[]{:S(2)}, u32[]{:S(2)}) %all-to-all-start.2) | async-done | bytes 2097184 | tf_op jit(solution)/shard_map/all_to_all | solution.py:247
  148.7 4.0 %fusion.1 = bf16[8,32,1024]{2,0,1:T(8,128)(2,1)S(1)} fusion(bf16[32,32,1024]{2,1,0:T(8,128)(2,1)} %all-to-all-done.2, s32[8]{0:T(128)S(1)} %copy-done.41), kind=kOutput, calls=%fused_computation.7 | convolution fusion | flops 16777472 | bytes 2621472 | tf_op jit(solution)/shard_map/pa,p...->a.../dot_general | solution.py:250
  152.7 1.9 %multiply_reduce_fusion = (f32[8,32]{1,0:T(8,128)S(1)}, f32[8,32,1024]{2,1,0:T(8,128)S(1)}) fusion(bf16[8,32,1024]{2,1,0:T(8,128)(2,1)} %bitcast.143, bf16[8,32,1024]{2,1,0:T(8,128)(2,1)S(1)} %copy-done.6, f32[1024]{0:T(1024)S(1)} %copy-done.28, f32[8,32,1024]{2,1,0:T(8,128)S(1)} %copy-done.4, f32[8,32,1024]{2,1,0:T(8,128)S(1)} %copy-done.3, ...), kind=kLoop, calls=%fused_computation.50 | loop fusion | flops 3669760 | bytes 4723712 | tf_op jit(solution)/shard_map/reduce_sum | solution.py:292
  154.8 2.2 %collective-permute-done = f32[8,32]{1,0:T(8,128)S(1)} collective-permute-done((f32[8,32]{1,0:T(8,128)S(1)}, f32[8,32]{1,0:T(8,128)S(1)}, u32[]{:S(2)}, u32[]{:S(2)}) %collective-permute-start) | collective-permute-done | bytes 1056 | tf_op jit(solution)/shard_map/ppermute | solution.py:294
  (248 shorter events, 53.7 us)
Async XLA Ops:
  0.0 67.1 %copy-start = (bf16[8,32,2048]{2,1,0:T(8,128)(2,1)S(1)}, bf16[8,32,2048]{2,1,0:T(8,128)(2,1)}, u32[]{:S(2)}) copy-start(bf16[8,32,2048]{2,1,0:T(8,128)(2,1)} %param.39) | copy-start | bytes 3145732
  6.8 9.3 %copy-start.54 = (s32[128]{0:T(128)S(1)}, s32[128]{0:T(128)}, u32[]{:S(2)}) copy-start(s32[128]{0:T(128)} %param.45) | copy-start | bytes 1540
  6.8 9.7 %copy-start.53 = (s32[8]{0:T(128)S(1)}, s32[8]{0:T(128)}, u32[]{:S(2)}) copy-start(s32[8]{0:T(128)} %param.44) | copy-start | bytes 100
  6.8 9.8 %copy-start.15 = (s32[8,32,32]{2,1,0:T(8,128)S(1)}, s32[8,32,32]{2,1,0:T(8,128)}, u32[]{:S(2)}) copy-start(s32[8,32,32]{2,1,0:T(8,128)} %param.43) | copy-start | bytes 98308
  8.3 12.6 %copy-start.25 = (bf16[4,4096]{1,0:T(4,128)(2,1)S(1)}, bf16[4,4096]{1,0:T(4,128)(2,1)}, u32[]{:S(2)}) copy-start(bf16[4,4096]{1,0:T(4,128)(2,1)} %param.31) | copy-start | bytes 98308
  8.3 29.1 %all-to-all-start = ((bf16[16,16,3088]{2,0,1:T(8,128)(2,1)}), bf16[16,16,3088]{2,0,1:T(8,128)(2,1)S(1)}, u32[]{:S(2)}, u32[]{:S(2)}) async-start(bf16[16,16,3088]{2,0,1:T(8,128)(2,1)} %copy_dynamic-update-slice_fusion), calls=%async_computation | async-start | bytes 3276800 | tf_op jit(solution)/shard_map/all_to_all | solution.py:195
  16.0 6.3 %copy-start.32 = (f32[4096]{0:T(1024)S(1)}, f32[4096]{0:T(1024)}, u32[]{:S(2)}) copy-start(f32[4096]{0:T(1024)} %param.32) | copy-start | bytes 49156
  16.0 7.5 %copy-start.8 = (s32[8,32,32]{2,1,0:T(8,128)S(1)}, s32[8,32,32]{2,1,0:T(8,128)}, u32[]{:S(2)}) copy-start(s32[8,32,32]{2,1,0:T(8,128)} %param.28) | copy-start | bytes 98308
  16.0 12.6 %copy-start.27 = (bf16[4,1024]{1,0:T(4,128)(2,1)S(1)}, bf16[4,1024]{1,0:T(4,128)(2,1)}, u32[]{:S(2)}) copy-start(bf16[4,1024]{1,0:T(4,128)(2,1)} %param.29) | copy-start | bytes 24580
  17.4 20.0 %copy-start.29 = (pred[8,32]{1,0:T(8,128)(4,1)}, pred[8,32]{1,0:T(8,128)(4,1)S(1)}, u32[]{:S(2)}) copy-start(pred[8,32]{1,0:T(8,128)(4,1)S(1)} %broadcast_compare_fusion) | copy-start | bytes 772
  18.8 11.3 %copy-start.11 = (bf16[8,32,1024]{2,1,0:T(8,128)(2,1)S(1)}, bf16[8,32,1024]{2,1,0:T(8,128)(2,1)}, u32[]{:S(2)}) copy-start(bf16[8,32,1024]{2,1,0:T(8,128)(2,1)} %param.41) | copy-start | bytes 1572868
  22.3 18.5 %copy-start.40 = (s32[8]{0:T(128)S(1)}, s32[8]{0:T(128)}, u32[]{:S(2)}) copy-start(s32[8]{0:T(128)} %fusion.119) | copy-start | bytes 100
  26.1 15.2 %copy-start.36 = (s32[8]{0:T(128)}, s32[8]{0:T(128)S(1)}, u32[]{:S(2)}) copy-start(s32[8]{0:T(128)S(1)} %dynamic-slice_reduce_fusion) | copy-start | bytes 100
  43.3 40.7 %all-to-all-start.1 = ((bf16[32,32,432]{2,1,0:T(8,128)(2,1)}), bf16[32,32,432]{2,1,0:T(8,128)(2,1)}, u32[]{:S(2)}, u32[]{:S(2)}) async-start(bf16[32,32,432]{2,1,0:T(8,128)(2,1)} %copy.635), calls=%async_computation.1 | async-start | bytes 2097152 | tf_op jit(solution)/shard_map/all_to_all | solution.py:226
  56.0 9.1 %copy-start.16 = (s32[8,32,32]{2,1,0:T(8,128)S(1)}, s32[8,32,32]{2,1,0:T(8,128)}, u32[]{:S(2)}) copy-start(s32[8,32,32]{2,1,0:T(8,128)} %param.43) | copy-start | bytes 98308
  67.1 6.3 %copy-start.9 = (s32[8,32,32]{2,1,0:T(8,128)S(1)}, s32[8,32,32]{2,1,0:T(8,128)}, u32[]{:S(2)}) copy-start(s32[8,32,32]{2,1,0:T(8,128)} %param.28) | copy-start | bytes 98308
  75.1 10.2 %copy-start.37 = (s32[8]{0:T(128)S(1)}, s32[8]{0:T(128)}, u32[]{:S(2)}) copy-start(s32[8]{0:T(128)} %copy-done.36) | copy-start | bytes 100
  76.6 9.8 %copy-start.18 = (bf16[8,3,512]{2,1,0:T(4,128)(2,1)S(1)}, bf16[8,3,512]{2,1,0:T(4,128)(2,1)}, u32[]{:S(2)}) copy-start(bf16[8,3,512]{2,1,0:T(4,128)(2,1)} %copy-done.17) | copy-start | bytes 73732
  96.0 6.8 %copy-start.2 = (bf16[16,16,3088]{2,0,1:T(8,128)(2,1)S(1)}, bf16[16,16,3088]{2,0,1:T(8,128)(2,1)}, u32[]{:S(2)}) copy-start(bf16[16,16,3088]{2,0,1:T(8,128)(2,1)} %copy-done.1) | copy-start | bytes 4743172
  96.0 52.7 %all-to-all-start.2 = ((bf16[32,32,1024]{2,1,0:T(8,128)(2,1)}), bf16[32,32,1024]{2,1,0:T(8,128)(2,1)}, u32[]{:S(2)}, u32[]{:S(2)}) async-start(bf16[32,32,1024]{2,1,0:T(8,128)(2,1)} %copy.683), calls=%async_computation.2 | async-start | bytes 4194304 | tf_op jit(solution)/shard_map/all_to_all | solution.py:247
  120.6 32.1 %copy-start.3 = (f32[8,32,1024]{2,1,0:T(8,128)S(1)}, f32[8,32,1024]{2,1,0:T(8,128)}, u32[]{:S(2)}) copy-start(f32[8,32,1024]{2,1,0:T(8,128)} %reshape.552) | copy-start | bytes 3145732
  120.6 32.1 %copy-start.4 = (f32[8,32,1024]{2,1,0:T(8,128)S(1)}, f32[8,32,1024]{2,1,0:T(8,128)}, u32[]{:S(2)}) copy-start(f32[8,32,1024]{2,1,0:T(8,128)} %reshape.551) | copy-start | bytes 3145732
  120.6 32.1 %copy-start.28 = (f32[1024]{0:T(1024)S(1)}, f32[1024]{0:T(1024)}, u32[]{:S(2)}) copy-start(f32[1024]{0:T(1024)} %mul.324) | copy-start | bytes 12292
  154.5 2.5 %collective-permute-start = (f32[8,32]{1,0:T(8,128)S(1)}, f32[8,32]{1,0:T(8,128)S(1)}, u32[]{:S(2)}, u32[]{:S(2)}) collective-permute-start(f32[8,32]{1,0:T(8,128)S(1)} %get-tuple-element.8), channel_id=1, source_target_pairs={{0,1},{1,0},{2,3},{3,2},{4,5},{5,4},{6,7},{7,6},{8,9},{9,8},{10,11... | collective-permute-start | bytes 3080 | tf_op jit(solution)/shard_map/ppermute | solution.py:294
  (37 other events, 108.9 us)

commit v12 on v10

--- a/solution.py
+++ b/solution.py
@@ -243,9 +243,10 @@
         carry_state.reshape(reqs_dev, head_width, STATE),
         preferred_element_type=jnp.float32,
     )
-    carried_moved = lax.all_to_all(
-        spread(send_hot, carried_old.astype(jnp.bfloat16)), "req", split_axis=0, concat_axis=0, tiled=True
-    )
+    carried_placed = jnp.sum(
+        send_hot[:, :, None, None] * carried_old.astype(jnp.bfloat16)[None], axis=1
+    )
+    carried_moved = lax.all_to_all(carried_placed, "req", split_axis=0, concat_axis=0, tiled=True)
     carried = gather_back(recv_hot, carried_moved)
     conv_heads = tree_conv(
         head_rows, tails_new[..., :head_width], new_tree, kernel_heads, shift_heads

time: 159 us -> 159 us (level)
  other arithmetic: 16.4 us -> 20.1 us
  waiting for transfers between devices: 43.3 us -> 40 us
    all_to_all x1, waiting for transfers between devices: 6.38 us -> 3.07 us  [shards(): lax.all_to_all(exchange, 'req', split_axis=0, concat_axis=0, tiled=True)]
    reduce_sum x0 -> x1, other arithmetic: none -> 3 us  [shards(): jnp.sum(send_hot[:, :, None, None] * carried_old.astype(jnp.bfloat16)[Non...]
    convert_element_type x1, local copies, waits for them, and re-layouts: 2.5 us -> 0.76 us  [shards(): send_hot = (send_pos[None, :] == slot_ids[:, None]).astype(jnp.bfloat16)]
  transfers between devices with their start and end apart: 4 -> 4, of which waited for: 4 -> 4; matrix products, arithmetic and copies ran while one was open for 35% -> 37% of each run, Pallas kernels for 0% -> 0%
where the time goes in v12:
time: 159 us; the launch traced here: 158 us
  waiting for transfers between devices  40 us (25%)
  local copies, waits for them, and re-layouts  39.2 us (25%)
  matrix products  32.2 us (20%)
  starting transfers between devices  25.4 us (16%)
  other arithmetic  20.1 us (13%)
    all_to_all x1, waiting for transfers between devices, shards(): lax.all_to_all(carried_placed, 'req', split_axis=0, concat_axis=0, tiled=...  29 us
    all_to_all x1, starting transfers between devices, shards(): lax.all_to_all(exchange, 'req', split_axis=0, concat_axis=0, tiled=True)  12.6 us
    unnamed x124, local copies, waits for them, and re-layouts  8.34 us
    all_to_all x1, starting transfers between devices, shards(): lax.all_to_all(bundle, 'head', split_axis=1, concat_axis=0, tiled=True)  7.7 us
    dot_general x9, matrix products, tree_conv(): jnp.einsum('btj,bjc->btc', picked, tree_rows, preferred_element_type=jnp....  6.49 us
    all_to_all x1, waiting for transfers between devices, shards(): lax.all_to_all(bundle, 'head', split_axis=1, concat_axis=0, tiled=True)  5.73 us
    dot_general x1, matrix products, shards(): jnp.einsum('bjgqp,bjgn->bgqpn', weighted, key_slice, preferred_element_ty...  5.67 us
    dot_general x9, matrix products, tree_conv(): jnp.einsum('bti,bic->btc', older_rows, tail_rows, preferred_element_type=...  5.52 us
  transfers between devices with their start and end apart: 4, of which 4 were waited for; matrix products, arithmetic and copies ran while one was open for 37% of the time, Pallas kernels for 0%

profile of v12, /device:TPU:1, one launch (start us, length us, event | category | flops | bytes accessed | tf_op | source)
XLA Modules:
  0.0 158.1 jit_solution(13877413526964146661)
XLA Ops:
  8.4 7.7 %all-to-all-start = ((bf16[16,16,3088]{2,0,1:T(8,128)(2,1)}), bf16[16,16,3088]{2,0,1:T(8,128)(2,1)S(1)}, u32[]{:S(2)}, u32[]{:S(2)}) async-start(bf16[16,16,3088]{2,0,1:T(8,128)(2,1)} %copy_dynamic-update-slice_fusion), calls=%async_computation | async-start | bytes 3276800 | tf_op jit(solution)/shard_map/all_to_all | solution.py:195
  31.8 5.7 %all-to-all-done = bf16[16,16,3088]{2,0,1:T(8,128)(2,1)S(1)} async-done(((bf16[16,16,3088]{2,0,1:T(8,128)(2,1)}), bf16[16,16,3088]{2,0,1:T(8,128)(2,1)S(1)}, u32[]{:S(2)}, u32[]{:S(2)}) %all-to-all-start) | async-done | bytes 1581088 | tf_op jit(solution)/shard_map/all_to_all | solution.py:195
  41.9 1.6 %copy.631 = bf16[32,32,432]{2,1,0:T(8,128)(2,1)} copy(bf16[32,32,432]{2,0,1:T(8,128)(2,1)S(1)} %pad_maximum_fusion) | data formatting | bytes 1769472 | tf_op jit(solution)/shard_map/concatenate | solution.py:221
  43.5 12.6 %all-to-all-start.1 = ((bf16[32,32,432]{2,1,0:T(8,128)(2,1)}), bf16[32,32,432]{2,1,0:T(8,128)(2,1)}, u32[]{:S(2)}, u32[]{:S(2)}) async-start(bf16[32,32,432]{2,1,0:T(8,128)(2,1)} %copy.631), calls=%async_computation.1 | async-start | bytes 2097152 | tf_op jit(solution)/shard_map/all_to_all | solution.py:225
  56.2 1.4 broadcast_select_fusion.1
  58.1 1.6 %reshape.589 = f32[8,32,16,64]{3,2,1,0:T(8,128)S(1)} reshape(bf16[8,32,1024]{2,1,0:T(8,128)(2,1)} %param.38) | data formatting | bytes 1572864 | tf_op jit(solution)/shard_map/convert_element_type | solution.py:163
  61.9 1.4 mul.340
  63.2 1.5 slice.132
  64.7 1.5 copy.687
  66.2 1.4 reshape.580
  70.6 5.7 %fusion = bf16[8,1,16,64,256]{4,3,2,0,1:T(8,128)(2,1)} fusion(bf16[8,16,64,256]{3,2,1,0:T(8,128)(2,1)} %param.37, f32[8,16]{1,0:T(8,128)S(1)} %exp.52, f32[8,32,16,64]{3,2,1,0:T(8,128)S(1)} %reshape.589, f32[8,32,16]{1,2,0:T(8,128)S(1)} %bitcast_multiply_fusion, bf16[8,32,2048]{2,1,0:T(8,128)(2,1)S(1)} %copy-done, s32[]{:T(128)S(6)} %select_n.199), kind=kOutput, calls=%fused_computation.7 | convolution fusion | flops 143130624 | bytes 10686468 | tf_op jit(solution)/shard_map/bjgqp,bjgn->bgqpn/dot_general | solution.py:171
  78.6 1.5 reshape.574
  81.2 3.1 %all-to-all-done.1 = bf16[32,32,432]{2,1,0:T(8,128)(2,1)} async-done(((bf16[32,32,432]{2,1,0:T(8,128)(2,1)}), bf16[32,32,432]{2,1,0:T(8,128)(2,1)}, u32[]{:S(2)}, u32[]{:S(2)}) %all-to-all-start.1) | async-done | bytes 884768 | tf_op jit(solution)/shard_map/all_to_all | solution.py:225
  84.3 1.5 slice.147
  89.6 3.5 %convolution_convert_fusion.1 = bf16[8,32,1024]{2,1,0:T(8,128)(2,1)S(1)} fusion(bf16[8,1024,256]{2,1,0:T(8,128)(2,1)} %bitcast.128, bf16[8,32,256]{2,0,1:T(8,128)(2,1)S(1)} %multiply_convert_fusion.5), kind=kOutput, calls=%fused_computation.26 | convolution fusion | flops 134479872 | bytes 4849664 | tf_op jit(solution)/shard_map/btn,bmn->btm/dot_general | solution.py:240
  93.1 3.0 %multiply_reduce_fusion = bf16[32,32,1024]{2,1,0:T(8,128)(2,1)} fusion(bf16[8,32,1024]{2,1,0:T(8,128)(2,1)S(1)} %convolution_convert_fusion.1, bf16[32,8]{1,0:T(8,128)(2,1)S(1)} %copy.652), kind=kLoop, calls=%fused_computation.5 | loop fusion | flops 15728640 | bytes 2621952 | tf_op jit(solution)/shard_map/reduce_sum | solution.py:246
  96.1 4.7 %all-to-all-start.2 = ((bf16[32,32,1024]{2,1,0:T(8,128)(2,1)}), bf16[32,32,1024]{2,1,0:T(8,128)(2,1)}, u32[]{:S(2)}, u32[]{:S(2)}) async-start(bf16[32,32,1024]{2,1,0:T(8,128)(2,1)} %multiply_reduce_fusion), calls=%async_computation.2 | async-start | bytes 4194304 | tf_op jit(solution)/shard_map/all_to_all | solution.py:249
  103.9 1.3 fusion.63
  112.7 1.7 %fusion.4 = f32[8,32,1024]{2,1,0:T(8,128)S(1)} fusion(f32[8,32,1024]{2,1,0:T(8,128)} %fusion.63, f32[1024]{0:T(1024)S(1)} %bitcast.155, bf16[8,3,1536]{2,1,0:T(4,128)(2,1)S(1)} %reshape.569, s32[8,32]{1,0:T(8,128)S(1)} %get-tuple-element.42), kind=kOutput, calls=%fused_computation.16 | convolution fusion | flops 2097920 | bytes 2170880 | tf_op jit(solution)/shard_map/bti,bic->btc/dot_general | solution.py:29
  116.4 1.4 convolution_bitcast_fusion
  119.0 1.6 reshape.573
  120.5 29.0 %all-to-all-done.2 = bf16[32,32,1024]{2,1,0:T(8,128)(2,1)} async-done(((bf16[32,32,1024]{2,1,0:T(8,128)(2,1)}), bf16[32,32,1024]{2,1,0:T(8,128)(2,1)}, u32[]{:S(2)}, u32[]{:S(2)}) %all-to-all-start.2) | async-done | bytes 2097184 | tf_op jit(solution)/shard_map/all_to_all | solution.py:249
  149.5 4.0 %fusion.1 = f32[8,32,1024]{2,0,1:T(8,128)S(1)} fusion(bf16[32,32,1024]{2,1,0:T(8,128)(2,1)} %all-to-all-done.2, s32[8]{0:T(128)S(1)} %copy-done.42), kind=kOutput, calls=%fused_computation.8 | convolution fusion | flops 16777472 | bytes 3145760 | tf_op jit(solution)/shard_map/pa,p...->a.../dot_general | solution.py:131
  154.9 2.2 %collective-permute-done = f32[8,32]{1,0:T(8,128)S(1)} collective-permute-done((f32[8,32]{1,0:T(8,128)S(1)}, f32[8,32]{1,0:T(8,128)S(1)}, u32[]{:S(2)}, u32[]{:S(2)}) %collective-permute-start) | collective-permute-done | bytes 1056 | tf_op jit(solution)/shard_map/ppermute | solution.py:292
  (251 shorter events, 56.4 us)
Async XLA Ops:
  0.0 70.6 %copy-start = (bf16[8,32,2048]{2,1,0:T(8,128)(2,1)S(1)}, bf16[8,32,2048]{2,1,0:T(8,128)(2,1)}, u32[]{:S(2)}) copy-start(bf16[8,32,2048]{2,1,0:T(8,128)(2,1)} %param.39) | copy-start | bytes 3145732
  6.8 9.4 %copy-start.55 = (s32[128]{0:T(128)S(1)}, s32[128]{0:T(128)}, u32[]{:S(2)}) copy-start(s32[128]{0:T(128)} %param.45) | copy-start | bytes 1540
  6.8 9.7 %copy-start.54 = (s32[8]{0:T(128)S(1)}, s32[8]{0:T(128)}, u32[]{:S(2)}) copy-start(s32[8]{0:T(128)} %param.44) | copy-start | bytes 100
  6.8 9.8 %copy-start.16 = (s32[8,32,32]{2,1,0:T(8,128)S(1)}, s32[8,32,32]{2,1,0:T(8,128)}, u32[]{:S(2)}) copy-start(s32[8,32,32]{2,1,0:T(8,128)} %param.43) | copy-start | bytes 98308
  8.4 12.6 %copy-start.26 = (bf16[4,4096]{1,0:T(4,128)(2,1)S(1)}, bf16[4,4096]{1,0:T(4,128)(2,1)}, u32[]{:S(2)}) copy-start(bf16[4,4096]{1,0:T(4,128)(2,1)} %param.31) | copy-start | bytes 98308
  8.4 29.1 %all-to-all-start = ((bf16[16,16,3088]{2,0,1:T(8,128)(2,1)}), bf16[16,16,3088]{2,0,1:T(8,128)(2,1)S(1)}, u32[]{:S(2)}, u32[]{:S(2)}) async-start(bf16[16,16,3088]{2,0,1:T(8,128)(2,1)} %copy_dynamic-update-slice_fusion), calls=%async_computation | async-start | bytes 3276800 | tf_op jit(solution)/shard_map/all_to_all | solution.py:195
  16.1 6.3 %copy-start.33 = (f32[4096]{0:T(1024)S(1)}, f32[4096]{0:T(1024)}, u32[]{:S(2)}) copy-start(f32[4096]{0:T(1024)} %param.32) | copy-start | bytes 49156
  16.1 8.4 %copy-start.9 = (s32[8,32,32]{2,1,0:T(8,128)S(1)}, s32[8,32,32]{2,1,0:T(8,128)}, u32[]{:S(2)}) copy-start(s32[8,32,32]{2,1,0:T(8,128)} %param.28) | copy-start | bytes 98308
  16.1 13.3 %copy-start.28 = (bf16[4,1024]{1,0:T(4,128)(2,1)S(1)}, bf16[4,1024]{1,0:T(4,128)(2,1)}, u32[]{:S(2)}) copy-start(bf16[4,1024]{1,0:T(4,128)(2,1)} %param.29) | copy-start | bytes 24580
  17.4 20.1 %copy-start.30 = (pred[8,32]{1,0:T(8,128)(4,1)}, pred[8,32]{1,0:T(8,128)(4,1)S(1)}, u32[]{:S(2)}) copy-start(pred[8,32]{1,0:T(8,128)(4,1)S(1)} %broadcast_compare_fusion) | copy-start | bytes 772
  18.8 12.0 %copy-start.12 = (bf16[8,32,1024]{2,1,0:T(8,128)(2,1)S(1)}, bf16[8,32,1024]{2,1,0:T(8,128)(2,1)}, u32[]{:S(2)}) copy-start(bf16[8,32,1024]{2,1,0:T(8,128)(2,1)} %param.41) | copy-start | bytes 1572868
  22.5 18.4 %copy-start.41 = (s32[8]{0:T(128)S(1)}, s32[8]{0:T(128)}, u32[]{:S(2)}) copy-start(s32[8]{0:T(128)} %fusion.119) | copy-start | bytes 100
  23.9 17.5 %copy-start.34 = (s32[8]{0:T(128)}, s32[8]{0:T(128)S(1)}, u32[]{:S(2)}) copy-start(s32[8]{0:T(128)S(1)} %dynamic-slice_reduce_fusion) | copy-start | bytes 100
  43.5 40.7 %all-to-all-start.1 = ((bf16[32,32,432]{2,1,0:T(8,128)(2,1)}), bf16[32,32,432]{2,1,0:T(8,128)(2,1)}, u32[]{:S(2)}, u32[]{:S(2)}) async-start(bf16[32,32,432]{2,1,0:T(8,128)(2,1)} %copy.631), calls=%async_computation.1 | async-start | bytes 2097152 | tf_op jit(solution)/shard_map/all_to_all | solution.py:225
  56.2 12.5 %copy-start.17 = (s32[8,32,32]{2,1,0:T(8,128)S(1)}, s32[8,32,32]{2,1,0:T(8,128)}, u32[]{:S(2)}) copy-start(s32[8,32,32]{2,1,0:T(8,128)} %param.43) | copy-start | bytes 98308
  70.6 6.3 %copy-start.10 = (s32[8,32,32]{2,1,0:T(8,128)S(1)}, s32[8,32,32]{2,1,0:T(8,128)}, u32[]{:S(2)}) copy-start(s32[8,32,32]{2,1,0:T(8,128)} %param.28) | copy-start | bytes 98308
  78.6 7.2 %copy-start.35 = (s32[8]{0:T(128)S(1)}, s32[8]{0:T(128)}, u32[]{:S(2)}) copy-start(s32[8]{0:T(128)} %copy-done.34) | copy-start | bytes 100
  80.2 6.7 %copy-start.19 = (bf16[8,3,512]{2,1,0:T(4,128)(2,1)S(1)}, bf16[8,3,512]{2,1,0:T(4,128)(2,1)}, u32[]{:S(2)}) copy-start(bf16[8,3,512]{2,1,0:T(4,128)(2,1)} %copy-done.18) | copy-start | bytes 73732
  96.1 6.8 %copy-start.2 = (bf16[16,16,3088]{2,0,1:T(8,128)(2,1)S(1)}, bf16[16,16,3088]{2,0,1:T(8,128)(2,1)}, u32[]{:S(2)}) copy-start(bf16[16,16,3088]{2,0,1:T(8,128)(2,1)} %copy-done.1) | copy-start | bytes 4743172
  96.1 53.4 %all-to-all-start.2 = ((bf16[32,32,1024]{2,1,0:T(8,128)(2,1)}), bf16[32,32,1024]{2,1,0:T(8,128)(2,1)}, u32[]{:S(2)}, u32[]{:S(2)}) async-start(bf16[32,32,1024]{2,1,0:T(8,128)(2,1)} %multiply_reduce_fusion), calls=%async_computation.2 | async-start | bytes 4194304 | tf_op jit(solution)/shard_map/all_to_all | solution.py:249
  120.5 33.0 %copy-start.3 = (f32[8,32,1024]{2,1,0:T(8,128)S(1)}, f32[8,32,1024]{2,1,0:T(8,128)}, u32[]{:S(2)}) copy-start(f32[8,32,1024]{2,1,0:T(8,128)} %reshape.574) | copy-start | bytes 3145732
  120.5 33.0 %copy-start.4 = (f32[8,32,1024]{2,1,0:T(8,128)S(1)}, f32[8,32,1024]{2,1,0:T(8,128)}, u32[]{:S(2)}) copy-start(f32[8,32,1024]{2,1,0:T(8,128)} %reshape.573) | copy-start | bytes 3145732
  120.5 33.0 %copy-start.29 = (f32[1024]{0:T(1024)S(1)}, f32[1024]{0:T(1024)}, u32[]{:S(2)}) copy-start(f32[1024]{0:T(1024)} %mul.340) | copy-start | bytes 12292
  154.6 2.5 %collective-permute-start = (f32[8,32]{1,0:T(8,128)S(1)}, f32[8,32]{1,0:T(8,128)S(1)}, u32[]{:S(2)}, u32[]{:S(2)}) collective-permute-start(f32[8,32]{1,0:T(8,128)S(1)} %get-tuple-element.8), channel_id=1, source_target_pairs={{0,1},{1,0},{2,3},{3,2},{4,5},{5,4},{6,7},{7,6},{8,9},{9,8},{10,11... | collective-permute-start | bytes 3080 | tf_op jit(solution)/shard_map/ppermute | solution.py:292
  (38 other events, 110.6 us)

commit v13 on v10

--- a/solution.py
+++ b/solution.py
@@ -218,15 +218,24 @@
         [group_rows[..., own_width:], new_tree.astype(jnp.bfloat16)], axis=-1
     )
     new_len = new_part.shape[-1]
+    half = NODES // 2
+    old_len = old_part.shape[-1]
     exchange = jnp.concatenate(
-        [spread(send_hot, new_part), spread(recv_hot, old_part)],
+        [
+            spread(recv_hot, old_part.reshape(reqs_dev, half, 2 * old_len)),
+            spread(send_hot, new_part.reshape(reqs_dev, half, 2 * new_len)),
+        ],
         axis=-1,
     )
     exchange = lax.all_to_all(exchange, "req", split_axis=0, concat_axis=0, tiled=True)
     tails_new = (
-        gather_back(recv_hot, exchange[..., :new_len]).astype(jnp.bfloat16).reshape(reqs_dev, 3, -1)
-    )
-    rows_old = gather_back(send_hot, exchange[..., new_len:]).astype(jnp.bfloat16)
+        gather_back(recv_hot, exchange[..., 2 * old_len :]).astype(jnp.bfloat16).reshape(reqs_dev, 3, -1)
+    )
+    rows_old = (
+        gather_back(send_hot, exchange[..., : 2 * old_len])
+        .astype(jnp.bfloat16)
+        .reshape(reqs_dev, NODES, old_len)
+    )
     tree_old = rows_old[..., own_width:].astype(jnp.int32)
     kernel_own = own_columns(kernel_groups, span_groups, head_count, per_dest)[head_index]
     shift_own = own_columns(shift_groups, span_groups, head_count, per_dest)[head_index]

time: 159 us -> 154 us (0.969)
  other arithmetic: 16.4 us -> 10.8 us
  matrix products: 33.1 us -> 36.4 us
    all_to_all x1, waiting for transfers between devices: 6.43 us -> 9.99 us  [shards(): lax.all_to_all(bundle, 'head', split_axis=1, concat_axis=0, tiled=True)]
    all_to_all x1, waiting for transfers between devices: 6.38 us -> 3.7 us  [shards(): lax.all_to_all(exchange, 'req', split_axis=0, concat_axis=0, tiled=True)]
    unnamed x124 -> x97, local copies, waits for them, and re-layouts: 7.68 us -> 5.49 us
    all_to_all x1, waiting for transfers between devices: 28.3 us -> 26.2 us  [shards(): lax.all_to_all(spread(send_hot, carried_old.astype(jnp.bfloat16)), 'req',...]
    dot_general x3, matrix products: 1.72 us -> 3.45 us  [spread(): jnp.einsum('pa,a...->p...', hot, payload, preferred_element_type=jnp.floa...]
    and x3 -> x0, other arithmetic: 1.64 us -> none  [tree_conv(): (ancestry == 1) & (node_depth[:, None, :] == node_depth[:, :, None] - upw...]
    dot_general x9, matrix products: 5.52 us -> 7.12 us  [tree_conv(): jnp.einsum('bti,bic->btc', older_rows, tail_rows, preferred_element_type=...]
    dot_general x9 -> x8, matrix products: 6.48 us -> 6.78 us  [tree_conv(): jnp.einsum('btj,bjc->btc', picked, tree_rows, preferred_element_type=jnp....]
where the time goes in v13:
time: 154 us; the launch traced here: 153 us
  waiting for transfers between devices  42 us (27%)
  local copies, waits for them, and re-layouts  37.6 us (24%)
  matrix products  36.4 us (24%)
  starting transfers between devices  25.4 us (16%)
  other arithmetic  10.8 us (7%)
    all_to_all x1, waiting for transfers between devices, shards(): lax.all_to_all(spread(send_hot, carried_old.astype(jnp.bfloat16)), 'req',...  26.2 us
    all_to_all x1, starting transfers between devices, shards(): lax.all_to_all(exchange, 'req', split_axis=0, concat_axis=0, tiled=True)  12.6 us
    all_to_all x1, waiting for transfers between devices, shards(): lax.all_to_all(bundle, 'head', split_axis=1, concat_axis=0, tiled=True)  9.99 us
    all_to_all x1, starting transfers between devices, shards(): lax.all_to_all(bundle, 'head', split_axis=1, concat_axis=0, tiled=True)  7.7 us
    dot_general x9, matrix products, tree_conv(): jnp.einsum('bti,bic->btc', older_rows, tail_rows, preferred_element_type=...  7.12 us
    dot_general x8, matrix products, tree_conv(): jnp.einsum('btj,bjc->btc', picked, tree_rows, preferred_element_type=jnp....  6.78 us
    dot_general x1, matrix products, shards(): jnp.einsum('bjgqp,bjgn->bgqpn', weighted, key_slice, preferred_element_ty...  5.68 us
    unnamed x97, local copies, waits for them, and re-layouts  5.49 us
  transfers between devices with their start and end apart: 4, of which 4 were waited for; matrix products, arithmetic and copies ran while one was open for 35% of the time, Pallas kernels for 0%

profile of v13, /device:TPU:1, one launch (start us, length us, event | category | flops | bytes accessed | tf_op | source)
XLA Modules:
  0.0 153.2 jit_solution(5778093513891598094)
XLA Ops:
  8.4 7.7 %all-to-all-start = ((bf16[16,16,3088]{2,0,1:T(8,128)(2,1)}), bf16[16,16,3088]{2,0,1:T(8,128)(2,1)S(1)}, u32[]{:S(2)}, u32[]{:S(2)}) async-start(bf16[16,16,3088]{2,0,1:T(8,128)(2,1)} %copy_dynamic-update-slice_fusion), calls=%async_computation | async-start | bytes 3276800 | tf_op jit(solution)/shard_map/all_to_all | solution.py:195
  27.5 10.0 %all-to-all-done = bf16[16,16,3088]{2,0,1:T(8,128)(2,1)S(1)} async-done(((bf16[16,16,3088]{2,0,1:T(8,128)(2,1)}), bf16[16,16,3088]{2,0,1:T(8,128)(2,1)S(1)}, u32[]{:S(2)}, u32[]{:S(2)}) %all-to-all-start) | async-done | bytes 1581088 | tf_op jit(solution)/shard_map/all_to_all | solution.py:195
  40.9 1.4 convolution_convert_fusion.1
  43.7 12.6 %all-to-all-start.1 = ((bf16[32,16,864]{2,1,0:T(8,128)(2,1)}), bf16[32,16,864]{2,1,0:T(8,128)(2,1)}, u32[]{:S(2)}, u32[]{:S(2)}) async-start(bf16[32,16,864]{2,1,0:T(8,128)(2,1)} %copy.251), calls=%async_computation.1 | async-start | bytes 1835008 | tf_op jit(solution)/shard_map/all_to_all | solution.py:230
  57.1 1.6 %reshape.571 = f32[8,32,16,64]{3,2,1,0:T(8,128)S(1)} reshape(bf16[8,32,1024]{2,1,0:T(8,128)(2,1)} %param.38) | data formatting | bytes 1572864 | tf_op jit(solution)/shard_map/convert_element_type | solution.py:163
  59.6 1.5 slice.132
  63.7 1.3 select_reduce_fusion.1
  66.0 5.7 %fusion = bf16[8,1,16,64,256]{4,3,2,0,1:T(8,128)(2,1)} fusion(bf16[8,16,64,256]{3,2,1,0:T(8,128)(2,1)} %param.37, f32[8,16]{1,0:T(8,128)S(1)} %exp.52, f32[8,32,16,64]{3,2,1,0:T(8,128)S(1)} %reshape.571, f32[8,32,16]{1,2,0:T(8,128)S(1)} %bitcast_multiply_fusion, bf16[8,32,2048]{2,1,0:T(8,128)(2,1)S(1)} %copy-done, s32[]{:T(128)S(6)} %select_n.199), kind=kOutput, calls=%fused_computation.6 | convolution fusion | flops 143130624 | bytes 10686468 | tf_op jit(solution)/shard_map/bjgqp,bjgn->bgqpn/dot_general | solution.py:171
  74.0 1.5 broadcast_in_dim.106
  75.5 1.6 %reshape.555 = f32[8,32,1024]{2,1,0:T(8,128)} reshape(f32[8,32,16,64]{3,2,1,0:T(8,128)S(1)} %broadcast_in_dim.106) | data formatting | bytes 2097152 | tf_op jit(solution)/shard_map/reshape | solution.py:290
  78.1 3.7 %all-to-all-done.1 = bf16[32,16,864]{2,1,0:T(8,128)(2,1)} async-done(((bf16[32,16,864]{2,1,0:T(8,128)(2,1)}), bf16[32,16,864]{2,1,0:T(8,128)(2,1)}, u32[]{:S(2)}, u32[]{:S(2)}) %all-to-all-start.1) | async-done | bytes 884768 | tf_op jit(solution)/shard_map/all_to_all | solution.py:230
  84.9 3.7 %convolution_convert_fusion.2 = bf16[8,32,1024]{2,1,0:T(8,128)(2,1)S(1)} fusion(bf16[8,1024,256]{2,1,0:T(8,128)(2,1)} %bitcast.129, f32[8,32,256]{2,1,0:T(8,128)S(1)} %fusion.19, f32[8,32,256]{2,1,0:T(8,128)S(1)} %fusion.100, f32[256]{0:T(256)S(1)} %bitcast.162, bf16[8,32,288]{2,1,0:T(8,128)(2,1)S(1)} %reshape.556, s32[8,32]{1,0:T(8,128)S(1)} %get-tuple-element.24, ...), kind=kOutput, calls=%fused_computation.26 | convolution fusion | flops 139231232 | bytes 5393408 | tf_op jit(solution)/shard_map/btn,bmn->btm/dot_general | solution.py:249
  89.4 2.5 %copy.270 = bf16[32,32,1024]{2,1,0:T(8,128)(2,1)} copy(bf16[32,32,1024]{2,0,1:T(8,128)(2,1)S(1)} %convolution_convert_fusion) | data formatting | bytes 4194304 | tf_op jit(solution)/shard_map/convert_element_type | solution.py:128
  91.9 4.7 %all-to-all-start.2 = ((bf16[32,32,1024]{2,1,0:T(8,128)(2,1)}), bf16[32,32,1024]{2,1,0:T(8,128)(2,1)}, u32[]{:S(2)}, u32[]{:S(2)}) async-start(bf16[32,32,1024]{2,1,0:T(8,128)(2,1)} %copy.270), calls=%async_computation.2 | async-start | bytes 4194304 | tf_op jit(solution)/shard_map/all_to_all | solution.py:255
  99.7 1.4 fusion.69
  101.4 1.4 fusion.65
  104.9 1.7 %reshape.550 = bf16[8,3,1536]{2,1,0:T(4,128)(2,1)} reshape(bf16[8,16,288]{2,1,0:T(8,128)(2,1)} %copy.253) | data formatting | bytes 147456 | tf_op jit(solution)/shard_map/reshape | solution.py:232
  107.7 1.4 fusion.14
  110.7 1.7 %fusion.4 = f32[8,32,1024]{2,1,0:T(8,128)S(1)} fusion(f32[8,32,1024]{2,1,0:T(8,128)} %fusion.69, f32[1024]{0:T(1024)S(1)} %bitcast.156, bf16[8,3,1536]{2,1,0:T(4,128)(2,1)S(1)} %copy-done.12, s32[8,32]{1,0:T(8,128)S(1)} %get-tuple-element.37), kind=kOutput, calls=%fused_computation.15 | convolution fusion | flops 2097920 | bytes 2170880 | tf_op jit(solution)/shard_map/bti,bic->btc/dot_general | solution.py:29
  114.3 1.4 convolution_bitcast_fusion
  116.9 1.6 %reshape.554 = f32[8,32,1024]{2,1,0:T(8,128)} reshape(f32[8,32,1,16,64]{4,3,1,0,2:T(8,128)S(1)} %copy.262) | data formatting | bytes 2097152 | tf_op jit(solution)/shard_map/reshape | solution.py:289
  118.5 26.2 %all-to-all-done.2 = bf16[32,32,1024]{2,1,0:T(8,128)(2,1)} async-done(((bf16[32,32,1024]{2,1,0:T(8,128)(2,1)}), bf16[32,32,1024]{2,1,0:T(8,128)(2,1)}, u32[]{:S(2)}, u32[]{:S(2)}) %all-to-all-start.2) | async-done | bytes 2097184 | tf_op jit(solution)/shard_map/all_to_all | solution.py:255
  144.7 4.0 %fusion.1 = f32[8,32,1024]{2,0,1:T(8,128)S(1)} fusion(bf16[32,32,1024]{2,1,0:T(8,128)(2,1)} %all-to-all-done.2, s32[8]{0:T(128)S(1)} %copy-done.28), kind=kOutput, calls=%fused_computation.7 | convolution fusion | flops 16777472 | bytes 3145760 | tf_op jit(solution)/shard_map/pa,p...->a.../dot_general | solution.py:131
  150.1 2.2 %collective-permute-done = f32[8,32]{1,0:T(8,128)S(1)} collective-permute-done((f32[8,32]{1,0:T(8,128)S(1)}, f32[8,32]{1,0:T(8,128)S(1)}, u32[]{:S(2)}, u32[]{:S(2)}) %collective-permute-start) | collective-permute-done | bytes 1056 | tf_op jit(solution)/shard_map/ppermute | solution.py:300
  (212 shorter events, 50.1 us)
Async XLA Ops:
  0.0 65.9 %copy-start = (bf16[8,32,2048]{2,1,0:T(8,128)(2,1)S(1)}, bf16[8,32,2048]{2,1,0:T(8,128)(2,1)}, u32[]{:S(2)}) copy-start(bf16[8,32,2048]{2,1,0:T(8,128)(2,1)} %param.39) | copy-start | bytes 3145732
  6.8 9.4 %copy-start.41 = (s32[128]{0:T(128)S(1)}, s32[128]{0:T(128)}, u32[]{:S(2)}) copy-start(s32[128]{0:T(128)} %param.45) | copy-start | bytes 1540
  6.8 9.7 %copy-start.40 = (s32[8]{0:T(128)S(1)}, s32[8]{0:T(128)}, u32[]{:S(2)}) copy-start(s32[8]{0:T(128)} %param.44) | copy-start | bytes 100
  6.8 9.8 %copy-start.9 = (s32[8,32,32]{2,1,0:T(8,128)S(1)}, s32[8,32,32]{2,1,0:T(8,128)}, u32[]{:S(2)}) copy-start(s32[8,32,32]{2,1,0:T(8,128)} %param.28) | copy-start | bytes 98308
  6.8 9.8 %copy-start.16 = (s32[8,32,32]{2,1,0:T(8,128)S(1)}, s32[8,32,32]{2,1,0:T(8,128)}, u32[]{:S(2)}) copy-start(s32[8,32,32]{2,1,0:T(8,128)} %param.43) | copy-start | bytes 98308
  8.4 12.5 %copy-start.21 = (bf16[4,4096]{1,0:T(4,128)(2,1)S(1)}, bf16[4,4096]{1,0:T(4,128)(2,1)}, u32[]{:S(2)}) copy-start(bf16[4,4096]{1,0:T(4,128)(2,1)} %param.31) | copy-start | bytes 98308
  8.4 29.1 %all-to-all-start = ((bf16[16,16,3088]{2,0,1:T(8,128)(2,1)}), bf16[16,16,3088]{2,0,1:T(8,128)(2,1)S(1)}, u32[]{:S(2)}, u32[]{:S(2)}) async-start(bf16[16,16,3088]{2,0,1:T(8,128)(2,1)} %copy_dynamic-update-slice_fusion), calls=%async_computation | async-start | bytes 3276800 | tf_op jit(solution)/shard_map/all_to_all | solution.py:195
  16.1 7.1 %copy-start.43 = (f32[16]{0:T(128)S(1)}, f32[16]{0:T(128)}, u32[]{:S(2)}) copy-start(f32[16]{0:T(128)} %param.33) | copy-start | bytes 196
  16.1 9.5 %copy-start.22 = (bf16[4,1024]{1,0:T(4,128)(2,1)S(1)}, bf16[4,1024]{1,0:T(4,128)(2,1)}, u32[]{:S(2)}) copy-start(bf16[4,1024]{1,0:T(4,128)(2,1)} %param.29) | copy-start | bytes 24580
  19.3 18.2 %copy-start.17 = (bf16[24,256]{0,1:T(8,128)(2,1)S(1)}, bf16[24,256]{0,1:T(8,128)(2,1)}, u32[]{:S(2)}) copy-start(bf16[24,256]{0,1:T(8,128)(2,1)} %mul.275) | copy-start | bytes 36868
  19.3 19.4 %copy-start.18 = (bf16[8,32,32]{2,1,0:T(8,128)(2,1)S(1)}, bf16[8,32,32]{2,1,0:T(8,128)(2,1)}, u32[]{:S(2)}) copy-start(bf16[8,32,32]{2,1,0:T(8,128)(2,1)} %get-tuple-element.48) | copy-start | bytes 49156
  20.3 20.6 %copy-start.27 = (s32[8]{0:T(128)}, s32[8]{0:T(128)S(1)}, u32[]{:S(2)}) copy-start(s32[8]{0:T(128)S(1)} %fusion.137) | copy-start | bytes 100
  43.7 38.1 %all-to-all-start.1 = ((bf16[32,16,864]{2,1,0:T(8,128)(2,1)}), bf16[32,16,864]{2,1,0:T(8,128)(2,1)}, u32[]{:S(2)}, u32[]{:S(2)}) async-start(bf16[32,16,864]{2,1,0:T(8,128)(2,1)} %copy.251), calls=%async_computation.1 | async-start | bytes 1835008 | tf_op jit(solution)/shard_map/all_to_all | solution.py:230
  77.1 7.4 %slice-start = ((f32[1,512]{1,0:T(1,128)}), f32[1,256]{1,0:T(1,128)S(1)}, s32[]{:S(2)}) async-start(f32[1,512]{1,0:T(1,128)} %copy-done.25), calls=%async_computation.3 | async-start | bytes 2048 | tf_op jit(solution)/shard_map/slice | solution.py:247
  77.1 7.4 %copy-start.33 = (f32[1,256]{1,0:T(1,128)S(1)}, f32[1,256]{1,0:T(1,128)}, u32[]{:S(2)}) copy-start(f32[1,256]{1,0:T(1,128)} %get-tuple-element.31) | copy-start | bytes 3076
  77.1 7.4 %copy-start.34 = (f32[1,256]{1,0:T(1,128)S(1)}, f32[1,256]{1,0:T(1,128)}, u32[]{:S(2)}) copy-start(f32[1,256]{1,0:T(1,128)} %get-tuple-element.32) | copy-start | bytes 3076
  78.1 6.5 %copy-start.32 = (f32[1,256]{1,0:T(1,128)S(1)}, f32[1,256]{1,0:T(1,128)}, u32[]{:S(2)}) copy-start(f32[1,256]{1,0:T(1,128)} %get-tuple-element.30) | copy-start | bytes 3076
  91.9 6.8 %copy-start.2 = (bf16[16,16,3088]{2,0,1:T(8,128)(2,1)S(1)}, bf16[16,16,3088]{2,0,1:T(8,128)(2,1)}, u32[]{:S(2)}) copy-start(bf16[16,16,3088]{2,0,1:T(8,128)(2,1)} %copy-done.1) | copy-start | bytes 4743172
  91.9 52.8 %all-to-all-start.2 = ((bf16[32,32,1024]{2,1,0:T(8,128)(2,1)}), bf16[32,32,1024]{2,1,0:T(8,128)(2,1)}, u32[]{:S(2)}, u32[]{:S(2)}) async-start(bf16[32,32,1024]{2,1,0:T(8,128)(2,1)} %copy.270), calls=%async_computation.2 | async-start | bytes 4194304 | tf_op jit(solution)/shard_map/all_to_all | solution.py:255
  102.8 6.3 %copy-start.38 = (f32[1,1,512]{2,0,1:T(1,128)S(1)}, f32[1,1,512]{2,0,1:T(1,128)}, u32[]{:S(2)}) copy-start(f32[1,1,512]{2,0,1:T(1,128)} %get-tuple-element.16) | copy-start | bytes 6148
  102.8 6.3 %copy-start.39 = (f32[1,1,512]{2,0,1:T(1,128)S(1)}, f32[1,1,512]{2,0,1:T(1,128)}, u32[]{:S(2)}) copy-start(f32[1,1,512]{2,0,1:T(1,128)} %get-tuple-element.19) | copy-start | bytes 6148
  118.5 30.2 %copy-start.3 = (f32[8,32,1024]{2,1,0:T(8,128)S(1)}, f32[8,32,1024]{2,1,0:T(8,128)}, u32[]{:S(2)}) copy-start(f32[8,32,1024]{2,1,0:T(8,128)} %reshape.555) | copy-start | bytes 3145732
  118.5 30.2 %copy-start.4 = (f32[8,32,1024]{2,1,0:T(8,128)S(1)}, f32[8,32,1024]{2,1,0:T(8,128)}, u32[]{:S(2)}) copy-start(f32[8,32,1024]{2,1,0:T(8,128)} %reshape.554) | copy-start | bytes 3145732
  149.7 2.5 %collective-permute-start = (f32[8,32]{1,0:T(8,128)S(1)}, f32[8,32]{1,0:T(8,128)S(1)}, u32[]{:S(2)}, u32[]{:S(2)}) collective-permute-start(f32[8,32]{1,0:T(8,128)S(1)} %get-tuple-element.8), channel_id=1, source_target_pairs={{0,1},{1,0},{2,3},{3,2},{4,5},{5,4},{6,7},{7,6},{8,9},{9,8},{10,11... | collective-permute-start | bytes 3080 | tf_op jit(solution)/shard_map/ppermute | solution.py:300
  (25 other events, 79.7 us)
